TPU v7x, 32 devices: a whole 2x2x4 slice. The times are simulated.
32 devices in a mesh: section: 4 (over x, core), sp: 2 (over y), rep: 4 (over z).
Axes of the slice: x: 2, y: 2, z: 4, core: 2. Of those that a mesh axis runs over, the one named last changes fastest.
Arguments:
- tokens: float32 [2, 2, 24, 3072], P('sp', None, 'section', 'rep'), may hold values from -120 to 120
- mod_scale: float32 [3072], replicated, may hold values from -3 to 3
- mod_shift: float32 [3072], replicated, may hold values from -3 to 3
- proj_weight: float32 [64, 3072], replicated, may hold values from -0.109375 to 0.109375
- proj_bias: float32 [64], replicated, may hold values from -3 to 3
- noisy_latent: float32 [2, 4, 48, 16], P(None, 'sp', 'section'), may hold values from -120 to 120
- in_weight: float32 [3, 3, 3, 16, 512], replicated, may hold values from -0.3125 to 0.3125
- in_bias: float32 [512], replicated, may hold values from -3 to 3
- conv_weight: bfloat16 [3, 3, 3, 256, 512], P(None, None, None, 'rep'), may hold values from -0.0546875 to 0.0546875
- conv_bias: float32 [256], P('rep'), may hold values from -3 to 3
- norm_gain: float32 [256], P('rep'), may hold values from 0.25 to 1.75
- norm_bias: float32 [256], P('rep'), may hold values from -3 to 3
Outputs:
- decoded: float32 [8, 96, 512], P('sp', 'section', 'rep')
All inputs are finite; a program needn't handle non-finite values.
Results may differ from a plain program's by a relative error of at most 0.0026.
Values sent between devices are 32-bit elements; how exact they have to be, the bound alone decides.
No kernel may reach another device: no remote copies, remote signals or barrier semaphores. Data moves between devices by JAX's collectives and lax.ppermute only.
A program may use at most 64 MiB of HBM per device.

v0:
```python
import jax
import jax.numpy as jnp
from jax import lax
from jax.sharding import PartitionSpec as P

D = 3072
LC = 16
CO = 256
GROUPS = 32


def with_halo(block, sides, width):
    for axis, dim in sides:
        count = lax.axis_size(axis)
        forward = [(i, i + 1) for i in range(count - 1)]
        backward = [(target, source) for source, target in forward]
        low = lax.ppermute(
            lax.slice_in_dim(block, block.shape[dim] - width, None, axis=dim), axis, forward
        )
        high = lax.ppermute(lax.slice_in_dim(block, 0, width, axis=dim), axis, backward)
        block = jnp.concatenate([low, block, high], axis=dim)
    return block


def valid_conv(volume, kernel, kernel_spec, precision_mode):
    front = jnp.concatenate([volume[:1], volume[:1], volume], axis=0)
    result = lax.conv_general_dilated(
        front[None],
        kernel,
        (1, 1, 1),
        "VALID",
        dimension_numbers=("NDHWC", kernel_spec, "NDHWC"),
        precision=precision_mode,
        preferred_element_type=jnp.float32,
    )
    return result[0]


def per_device(
    tokens,
    mod_scale,
    mod_shift,
    proj_weight,
    proj_bias,
    noisy_latent,
    in_weight,
    in_bias,
    conv_weight,
    conv_bias,
    norm_gain,
    norm_bias,
):
    local_width = tokens.shape[-1]
    scaled_weight = proj_weight * (1.0 + mod_scale)[None, :]
    center_column = jnp.sum(scaled_weight, axis=1)
    shift_column = (
        jnp.dot(
            proj_weight,
            mod_shift,
            precision=lax.Precision.HIGHEST,
            preferred_element_type=jnp.float32,
        )
        + proj_bias
    )
    local_weight = lax.dynamic_slice_in_dim(
        scaled_weight, lax.axis_index("rep") * local_width, local_width, 1
    )
    moved_tokens = lax.all_to_all(tokens, "sp", split_axis=1, concat_axis=0, tiled=True)
    projected = lax.dot_general(
        moved_tokens,
        local_weight,
        (((3,), (1,)), ((), ())),
        precision=lax.Precision.HIGHEST,
        preferred_element_type=jnp.float32,
    )
    projected, first_sums, square_sums = (
        projected,
        jnp.sum(moved_tokens, axis=-1),
        jnp.sum(moved_tokens * moved_tokens, axis=-1),
    )
    projected, first_sums, square_sums = lax.psum((projected, first_sums, square_sums), "rep")
    token_mean = first_sums / D
    token_var = square_sums / D - token_mean * token_mean
    velocity = (
        lax.rsqrt(token_var + 1e-06)[..., None]
        * (projected - token_mean[..., None] * center_column)
        + shift_column
    )
    frames, slab_rows, band_cols = (velocity.shape[0], velocity.shape[1], velocity.shape[2])
    patches = (
        velocity.reshape(frames, slab_rows, band_cols, LC, 2, 2)
        .transpose(0, 1, 4, 2, 5, 3)
        .reshape(frames, 2 * slab_rows, 2 * band_cols, LC)
    )
    clean = noisy_latent - 0.5 * patches
    extended = with_halo(clean, (("section", 2), ("sp", 1)), 2)
    inner_features = valid_conv(extended, in_weight, "DHWIO", lax.Precision.HIGHEST) + in_bias
    latent_rows = 2 * slab_rows
    latent_cols = 2 * band_cols
    row_global = lax.axis_index("sp") * latent_rows - 1 + jnp.arange(latent_rows + 2)
    col_global = lax.axis_index("section") * latent_cols - 1 + jnp.arange(latent_cols + 2)
    row_inside = (row_global >= 0) & (row_global < latent_rows * lax.axis_size("sp"))
    col_inside = (col_global >= 0) & (col_global < latent_cols * lax.axis_size("section"))
    inside = row_inside[None, :, None, None] & col_inside[None, None, :, None]
    features = jnp.where(inside, inner_features, 0.0).astype(jnp.bfloat16)
    upsampled = jnp.repeat(jnp.repeat(features, 2, axis=1), 2, axis=2)[:, 1:-1, 1:-1, :]
    mixed = valid_conv(upsampled, conv_weight, "DHWOI", None) + conv_bias
    group_size = CO // GROUPS
    local_groups = mixed.shape[-1] // group_size
    grouped = mixed.reshape(-1, local_groups, group_size)
    cell_count = grouped.shape[0] * group_size * lax.axis_size("section") * lax.axis_size("sp")
    group_mean = lax.psum(jnp.sum(grouped, axis=(0, 2)), ("section", "sp")) / cell_count
    deviation = grouped - group_mean[None, :, None]
    group_var = (
        lax.psum(jnp.sum(deviation * deviation, axis=(0, 2)), ("section", "sp")) / cell_count
    )
    normed = (
        (grouped - group_mean[None, :, None]) * lax.rsqrt(group_var + 1e-06)[None, :, None]
    ).reshape(mixed.shape)
    activated = jax.nn.silu(normed * norm_gain + norm_bias)
    out_rows, out_cols, out_chan = (activated.shape[1], activated.shape[2], activated.shape[3])
    return activated.transpose(1, 2, 3, 0).reshape(out_rows, out_cols, out_chan * frames)


def solution(mesh):
    return jax.shard_map(
        per_device,
        mesh=mesh,
        in_specs=(
            P("sp", None, "section", "rep"),
            P(),
            P(),
            P(),
            P(),
            P(None, "sp", "section", None),
            P(),
            P(),
            P(None, None, None, "rep", None),
            P("rep"),
            P("rep"),
            P("rep"),
        ),
        out_specs=P("sp", "section", "rep"),
        check_vma=False,
    )
```

profile of v0, /device:TPU:0, one launch (start us, length us, event | category | flops | bytes accessed | tf_op | source)
XLA Modules:
  0.0 79.5 jit_solution(5452324065720546734)
XLA Ops:
  0.0 1.6 %copy.53 = f32[1,2,6,768]{3,0,2,1:T(1,128)} copy(f32[1,2,6,768]{3,1,2,0:T(2,128)} %param.12) | data formatting | bytes 73728 | tf_op args[0]
  1.6 4.2 %all-to-all-start = ((f32[1,2,6,768]{3,0,2,1:T(1,128)}), f32[1,2,6,768]{3,0,2,1:T(1,128)S(1)}, u32[]{:S(2)}, u32[]{:S(2)}) async-start(f32[1,2,6,768]{3,0,2,1:T(1,128)} %copy.53), calls=%async_computation | async-start | bytes 73728 | tf_op jit(solution)/shard_map/all_to_all | solution.py:68
  5.8 0.7 broadcast_add_fusion
  6.5 1.3 %fusion.37 = (f32[64]{0:T(128)S(1)}, f32[64,3072]{1,0:T(8,128)S(1)}) fusion(f32[64,3072]{1,0:T(8,128)} %param.15, f32[3072]{0:T(1024)S(1)} %broadcast_add_fusion), kind=kLoop, calls=%fused_computation.63 | loop fusion | flops 393152 | bytes 1585408 | tf_op jit(solution)/shard_map/reduce_sum | solution.py:55
  7.9 0.7 fusion.11
  8.7 1.1 %all-to-all-done = f32[1,2,6,768]{3,0,2,1:T(1,128)S(1)} async-done(((f32[1,2,6,768]{3,0,2,1:T(1,128)}), f32[1,2,6,768]{3,0,2,1:T(1,128)S(1)}, u32[]{:S(2)}, u32[]{:S(2)}) %all-to-all-start) | async-done | bytes 36896 | tf_op jit(solution)/shard_map/all_to_all | solution.py:68
  9.8 0.2 convolution_bitcast_fusion
  10.1 0.2 multiply_reduce_fusion
  10.3 19.4 %all-reduce = (f32[2,1,6,64]{3,2,0,1:T(8,128)S(1)}, f32[2,1,6]{2,0,1:T(2,128)S(1)}, f32[2,1,6]{2,0,1:T(2,128)S(1)}) all-reduce(f32[2,1,6,64]{3,2,0,1:T(8,128)S(1)} %convolution_bitcast_fusion, f32[2,1,6]{2,0,1:T(2,128)S(1)} %bitcast.85, f32[2,1,6]{2,0,1:T(2,128)S(1)} %bitcast.84), channel_id=1, replica_groups=mesh['section'=4,'sp'=2,'rep'=4] {'rep'}, use_global_device_ids=true, to_apply=%region_4.0 | all-reduce | flops 792 | bytes 6336 | tf_op jit(solution)/shard_map/psum | solution.py:81
  29.9 0.1 copy.57
  30.1 1.3 %collective-permute-start = (f32[2,2,2,16]{3,1,2,0:T(2,128)S(1)}, f32[2,2,2,16]{3,1,2,0:T(2,128)S(1)}, u32[]{:S(2)}, u32[]{:S(2)}) collective-permute-start(f32[2,2,2,16]{3,1,2,0:T(2,128)S(1)} %get-tuple-element.12), channel_id=1, source_target_pairs={{0,8},{8,16},{16,24},{1,9},{9,17},{17,25},{2,10},{10,18},{18,26},{... | collective-permute-start | bytes 1544 | tf_op jit(solution)/shard_map/ppermute | solution.py:17
  31.4 1.3 %collective-permute-start.1 = (f32[2,2,2,16]{3,1,2,0:T(2,128)S(1)}, f32[2,2,2,16]{3,1,2,0:T(2,128)S(1)}, u32[]{:S(2)}, u32[]{:S(2)}) collective-permute-start(f32[2,2,2,16]{3,1,2,0:T(2,128)S(1)} %get-tuple-element.13), channel_id=1, source_target_pairs={{8,0},{16,8},{24,16},{9,1},{17,9},{25,17},{10,2},{18,10},{26,18},{... | collective-permute-start | bytes 1544 | tf_op jit(solution)/shard_map/ppermute | solution.py:20
  32.7 3.5 %collective-permute-done.1 = f32[2,2,2,16]{3,1,2,0:T(2,128)S(1)} collective-permute-done((f32[2,2,2,16]{3,1,2,0:T(2,128)S(1)}, f32[2,2,2,16]{3,1,2,0:T(2,128)S(1)}, u32[]{:S(2)}, u32[]{:S(2)}) %collective-permute-start.1) | collective-permute-done | bytes 544 | tf_op jit(solution)/shard_map/ppermute | solution.py:20
  36.2 1.3 %collective-permute-start.3 = (f32[2,2,16,16]{3,1,2,0:T(2,128)S(1)}, f32[2,2,16,16]{3,1,2,0:T(2,128)S(1)}, u32[]{:S(2)}, u32[]{:S(2)}) collective-permute-start(f32[2,2,16,16]{3,1,2,0:T(2,128)S(1)} %pad_maximum_fusion.4), channel_id=1, source_target_pairs={{4,0},{5,1},{6,2},{7,3},{12,8},{13,9},{14,10},{15,11},{20,16},{21,... | collective-permute-start | bytes 12296 | tf_op jit(solution)/shard_map/ppermute | solution.py:20
  37.5 4.5 %collective-permute-start.2 = (f32[2,2,16,16]{3,1,2,0:T(2,128)S(1)}, f32[2,2,16,16]{3,1,2,0:T(2,128)S(1)}, u32[]{:S(2)}, u32[]{:S(2)}) collective-permute-start(f32[2,2,16,16]{3,1,2,0:T(2,128)S(1)} %pad_maximum_fusion.4), channel_id=1, source_target_pairs={{0,4},{1,5},{2,6},{3,7},{8,12},{9,13},{10,14},{11,15},{16,20},{17,... | collective-permute-start | bytes 12296 | tf_op jit(solution)/shard_map/ppermute | solution.py:17
  42.1 1.5 %collective-permute-done.2 = f32[2,2,16,16]{3,1,2,0:T(2,128)S(1)} collective-permute-done((f32[2,2,16,16]{3,1,2,0:T(2,128)S(1)}, f32[2,2,16,16]{3,1,2,0:T(2,128)S(1)}, u32[]{:S(2)}, u32[]{:S(2)}) %collective-permute-start.2) | collective-permute-done | bytes 4128 | tf_op jit(solution)/shard_map/ppermute | solution.py:17
  43.9 2.8 %convolution_select_fusion = f32[2,4,8,2,512]{4,2,3,1,0:T(8,128)S(1)} fusion(f32[3,3,3,16,512]{4,3,2,1,0:T(8,128)} %param.18, f32[4,6,1,7,2,16]{5,3,4,1,0,2:T(8,128)S(1)} %slice.29, f32[4,6,1,8,2,16]{5,3,4,1,0,2:T(8,128)S(1)} %copy.60, pred[8,2]{0,1:T(4,128)(4,1)S(1)} %copy-done.10), kind=kOutput, calls=%fused_computation.8 | convolution fusion | flops 339841024 | bytes 1192976 | tf_op jit(solution)/shard_map/conv_general_dilated | solution.py:27
  46.7 0.2 copy.61
  46.9 0.1 fusion.19
  47.0 0.1 broadcast_in_dim.23
  47.4 0.2 maximum_bitcast_fusion
  47.6 0.5 copy.68
  48.2 0.3 pad.1.clone
  48.4 0.4 copy.64
  49.0 2.0 %select_reduce_fusion.1 = (f32[64]{0:T(128)S(1)}, f32[2,4,8,4,64]{4,2,3,1,0:T(8,128)S(1)}) fusion(f32[64]{0:T(128)S(1)} %copy-done.5, pred[8,4]{0,1:T(4,128)(4,1)S(1)} %copy-done.9, bf16[3,3,3,64,512]{4,3,2,1,0:T(8,128)(2,1)S(1)} %copy-done, bf16[4,6,1,7,2,512]{5,3,4,1,0,2:T(8,128)(2,1)S(1)} %slice.33, bf16[4,6,1,8,4,512]{5,3,4,1,0,2:T(8,128)(2,1)S(1)} %copy.64), kind=kOutput, calls=%fused_computation.31 | convolution fusion | flops 456589248 | bytes 2966048 | tf_op jit(solution)/shard_map/conv_general_dilated | solution.py:27
  51.1 0.1 reduce_sum.70
  51.2 14.4 %psum.38 = f32[8]{0:T(128)S(1)} all-reduce(f32[8]{0:T(128)S(1)} %reduce_sum.70), channel_id=1, replica_groups=mesh['section'=4,'sp'=2,'rep'=4] {'section','sp'}, use_global_device_ids=true, to_apply=%region_8.9 | all-reduce | flops 8 | bytes 64 | tf_op jit(solution)/shard_map/psum | solution.py:112
  65.8 0.1 select_reduce_fusion
  66.0 0.1 reduce_sum.73
  66.2 12.2 %psum.39 = f32[8]{0:T(128)S(1)} all-reduce(f32[8]{0:T(128)S(1)} %reduce_sum.73), channel_id=1, replica_groups=mesh['section'=4,'sp'=2,'rep'=4] {'section','sp'}, use_global_device_ids=true, to_apply=%region_11.12 | all-reduce | flops 8 | bytes 64 | tf_op jit(solution)/shard_map/psum | solution.py:115
  78.7 0.2 copy.66
  78.8 0.7 copy.67
  (54 shorter events, 1.5 us)
Async XLA Ops:
  0.0 49.0 %copy-start = (bf16[3,3,3,64,512]{4,3,2,1,0:T(8,128)(2,1)S(1)}, bf16[3,3,3,64,512]{4,3,2,1,0:T(8,128)(2,1)}, u32[]{:S(2)}) copy-start(bf16[3,3,3,64,512]{4,3,2,1,0:T(8,128)(2,1)} %param.20) | copy-start | bytes 5308420
  0.0 7.9 %copy-start.1 = (f32[64,3072]{1,0:T(8,128)S(1)}, f32[64,3072]{1,0:T(8,128)}, u32[]{:S(2)}) copy-start(f32[64,3072]{1,0:T(8,128)} %param.15) | copy-start | bytes 2359300
  0.0 7.9 %copy-start.6 = (f32[64]{0:T(128)S(1)}, f32[64]{0:T(128)}, u32[]{:S(2)}) copy-start(f32[64]{0:T(128)} %param.16) | copy-start | bytes 772
  0.0 7.9 %copy-start.3 = (f32[3072]{0:T(1024)S(1)}, f32[3072]{0:T(1024)}, u32[]{:S(2)}) copy-start(f32[3072]{0:T(1024)} %param.14) | copy-start | bytes 36868
  0.0 30.0 %copy-start.2 = (f32[2,2,12,16]{3,1,2,0:T(2,128)S(1)}, f32[2,2,12,16]{3,1,2,0:T(2,128)}, u32[]{:S(2)}) copy-start(f32[2,2,12,16]{3,1,2,0:T(2,128)} %param.17) | copy-start | bytes 9220
  1.6 8.2 %all-to-all-start = ((f32[1,2,6,768]{3,0,2,1:T(1,128)}), f32[1,2,6,768]{3,0,2,1:T(1,128)S(1)}, u32[]{:S(2)}, u32[]{:S(2)}) async-start(f32[1,2,6,768]{3,0,2,1:T(1,128)} %copy.53), calls=%async_computation | async-start | bytes 73728 | tf_op jit(solution)/shard_map/all_to_all | solution.py:68
  7.9 36.0 %copy-start.10 = (pred[8,2]{0,1:T(4,128)(4,1)S(1)}, pred[8,2]{0,1:T(4,128)(4,1)}, u32[]{:S(2)}) copy-start(pred[8,2]{0,1:T(4,128)(4,1)} %constant.62) | copy-start | bytes 52
  30.1 2.6 %collective-permute-start = (f32[2,2,2,16]{3,1,2,0:T(2,128)S(1)}, f32[2,2,2,16]{3,1,2,0:T(2,128)S(1)}, u32[]{:S(2)}, u32[]{:S(2)}) collective-permute-start(f32[2,2,2,16]{3,1,2,0:T(2,128)S(1)} %get-tuple-element.12), channel_id=1, source_target_pairs={{0,8},{8,16},{16,24},{1,9},{9,17},{17,25},{2,10},{10,18},{18,26},{... | collective-permute-start | bytes 1544 | tf_op jit(solution)/shard_map/ppermute | solution.py:17
  31.4 4.8 %collective-permute-start.1 = (f32[2,2,2,16]{3,1,2,0:T(2,128)S(1)}, f32[2,2,2,16]{3,1,2,0:T(2,128)S(1)}, u32[]{:S(2)}, u32[]{:S(2)}) collective-permute-start(f32[2,2,2,16]{3,1,2,0:T(2,128)S(1)} %get-tuple-element.13), channel_id=1, source_target_pairs={{8,0},{16,8},{24,16},{9,1},{17,9},{25,17},{10,2},{18,10},{26,18},{... | collective-permute-start | bytes 1544 | tf_op jit(solution)/shard_map/ppermute | solution.py:20
  36.2 5.9 %collective-permute-start.3 = (f32[2,2,16,16]{3,1,2,0:T(2,128)S(1)}, f32[2,2,16,16]{3,1,2,0:T(2,128)S(1)}, u32[]{:S(2)}, u32[]{:S(2)}) collective-permute-start(f32[2,2,16,16]{3,1,2,0:T(2,128)S(1)} %pad_maximum_fusion.4), channel_id=1, source_target_pairs={{4,0},{5,1},{6,2},{7,3},{12,8},{13,9},{14,10},{15,11},{20,16},{21,... | collective-permute-start | bytes 12296 | tf_op jit(solution)/shard_map/ppermute | solution.py:20
  37.5 6.1 %collective-permute-start.2 = (f32[2,2,16,16]{3,1,2,0:T(2,128)S(1)}, f32[2,2,16,16]{3,1,2,0:T(2,128)S(1)}, u32[]{:S(2)}, u32[]{:S(2)}) collective-permute-start(f32[2,2,16,16]{3,1,2,0:T(2,128)S(1)} %pad_maximum_fusion.4), channel_id=1, source_target_pairs={{0,4},{1,5},{2,6},{3,7},{8,12},{9,13},{10,14},{11,15},{16,20},{17,... | collective-permute-start | bytes 12296 | tf_op jit(solution)/shard_map/ppermute | solution.py:17
  43.8 3.0 %copy-start.4 = (f32[512]{0:T(512)S(1)}, f32[512]{0:T(512)}, u32[]{:S(2)}) copy-start(f32[512]{0:T(512)} %param.19) | copy-start | bytes 6148
  48.1 0.9 %copy-start.5 = (f32[64]{0:T(128)S(1)}, f32[64]{0:T(128)}, u32[]{:S(2)}) copy-start(f32[64]{0:T(128)} %param.21) | copy-start | bytes 772
  48.1 0.9 %copy-start.9 = (pred[8,4]{0,1:T(4,128)(4,1)S(1)}, pred[8,4]{0,1:T(4,128)(4,1)}, u32[]{:S(2)}) copy-start(pred[8,4]{0,1:T(4,128)(4,1)} %constant.61) | copy-start | bytes 100
  49.0 29.6 %copy-start.7 = (f32[64]{0:T(128)S(1)}, f32[64]{0:T(128)}, u32[]{:S(2)}) copy-start(f32[64]{0:T(128)} %param.23) | copy-start | bytes 772
  49.0 29.6 %copy-start.8 = (f32[64]{0:T(128)S(1)}, f32[64]{0:T(128)}, u32[]{:S(2)}) copy-start(f32[64]{0:T(128)} %param.22) | copy-start | bytes 772
where the time goes:
time: 80 us; the launch traced here: 79.5 us
  blocking collectives  46.1 us (58%)
  starting transfers between devices  12.7 us (16%)
  waiting for transfers between devices  6.12 us (8%)
  matrix products  5.79 us (7%)
  local copies, waits for them, and re-layouts  5.24 us (7%)
  other arithmetic  3.28 us (4%)
    psum x1, blocking collectives, per_device(): lax.psum((projected, first_sums, square_sums), 'rep')  19.4 us
    psum x1, blocking collectives, per_device(): lax.psum(jnp.sum(grouped, axis=(0, 2)), ('section', 'sp')) / cell_count  14.4 us
    psum x1, blocking collectives, per_device(): lax.psum(jnp.sum(deviation * deviation, axis=(0, 2)), ('section', 'sp'))  12.2 us
    ppermute x2, starting transfers between devices, with_halo(): lax.ppermute(lax.slice_in_dim(block, block.shape[dim] - width, None, axis...  5.84 us
    conv_general_dilated x2, matrix products, valid_conv(): lax.conv_general_dilated(front[None], kernel, (1, 1, 1), 'VALID', dimensi...  4.83 us
    all_to_all x1, starting transfers between devices, per_device(): lax.all_to_all(tokens, 'sp', split_axis=1, concat_axis=0, tiled=True)  4.24 us
    ppermute x2, waiting for transfers between devices, with_halo(): lax.ppermute(lax.slice_in_dim(block, 0, width, axis=dim), axis, backward)  3.47 us
    ppermute x2, starting transfers between devices, with_halo(): lax.ppermute(lax.slice_in_dim(block, 0, width, axis=dim), axis, backward)  2.58 us
  transfers between devices with their start and end apart: 5, of which 3 were waited for; matrix products, arithmetic and copies ran while one was open for 4% of the time, Pallas kernels for 0%

commit v1 on v0

v1 whole, which is shorter than its diff:
```python
import jax
import jax.numpy as jnp
from jax import lax
from jax.sharding import PartitionSpec as P

D = 3072
LC = 16
CO = 256
GROUPS = 32
ALL = ("section", "sp", "rep")
BLOCKS = ("section", "sp")


def valid_conv(volume, kernel, kernel_spec, precision_mode):
    front = jnp.concatenate([volume[:1], volume[:1], volume], axis=0)
    result = lax.conv_general_dilated(
        front[None],
        kernel,
        (1, 1, 1),
        "VALID",
        dimension_numbers=("NDHWC", kernel_spec, "NDHWC"),
        precision=precision_mode,
        preferred_element_type=jnp.float32,
    )
    return result[0]


def neighbours(stack, index, axis):
    pad = [(0, 0)] * stack.ndim
    pad[axis] = (1, 1)
    return lax.dynamic_slice_in_dim(jnp.pad(stack, pad), index, 3, axis)


def per_device(
    tokens,
    mod_scale,
    mod_shift,
    proj_weight,
    proj_bias,
    noisy_latent,
    in_weight,
    in_bias,
    conv_weight,
    conv_bias,
    norm_gain,
    norm_bias,
):
    n_sec, n_sp, n_rep = (lax.axis_size(a) for a in ALL)
    n_dev = n_sec * n_sp * n_rep
    sec, spi, rep = (lax.axis_index(a) for a in ALL)
    tok_frames, patch_rows, band_cols, local_width = tokens.shape
    frames, lat_rows, lat_cols, _ = noisy_latent.shape
    full_width = local_width * n_rep
    out_width = proj_weight.shape[0]

    scaled_weight = proj_weight * (1.0 + mod_scale)[None, :]
    shard_columns = jnp.sum(scaled_weight.reshape(out_width, n_rep, local_width), axis=2).T
    shift_column = (
        jnp.dot(
            proj_weight,
            mod_shift,
            precision=lax.Precision.HIGHEST,
            preferred_element_type=jnp.float32,
        )
        + proj_bias
    )
    local_weight = lax.dynamic_slice_in_dim(scaled_weight, rep * local_width, local_width, 1)

    shard_mean = jnp.mean(tokens, axis=-1, keepdims=True)
    centred = tokens - shard_mean
    shard_m2 = jnp.sum(centred * centred, axis=-1, keepdims=True)
    projected = lax.dot_general(
        centred,
        local_weight,
        (((3,), (1,)), ((), ())),
        precision=lax.Precision.HIGHEST,
        preferred_element_type=jnp.float32,
    )
    partial = jnp.concatenate([projected, shard_mean, shard_m2], axis=-1)

    slab = lat_rows // 2
    if patch_rows <= slab + 2:
        window = patch_rows
        per_slab = jnp.broadcast_to(partial[None], (n_sp,) + partial.shape)
    else:
        window = slab + 2
        padded = jnp.pad(partial, ((0, 0), (1, 1), (0, 0), (0, 0)))
        per_slab = jnp.stack([padded[:, p * slab : p * slab + window] for p in range(n_sp)])
    per_slab = per_slab.reshape(n_sp, -1)
    part_size = per_slab.shape[1]

    frame_rows = frames * lat_rows
    if frame_rows % n_rep == 0:
        share = frame_rows // n_rep
        latent_part = lax.dynamic_slice_in_dim(
            noisy_latent.reshape(frame_rows, -1), rep * share, share, 0
        ).reshape(-1)
    else:
        share = frame_rows
        latent_part = noisy_latent.reshape(-1)

    send = jnp.concatenate(
        [
            jnp.broadcast_to(per_slab[None, :, None], (n_sec, n_sp, n_rep, part_size)),
            jnp.broadcast_to(latent_part, (n_sec, n_sp, n_rep, latent_part.shape[0])),
        ],
        axis=-1,
    ).reshape(n_dev, -1)
    received = lax.all_to_all(send, ALL, 0, 0, tiled=False).reshape(n_sec, n_sp, n_rep, -1)

    parts = neighbours(received[..., :part_size], sec, 0).reshape(
        3, n_sp, n_rep, tok_frames, window, band_cols, out_width + 2
    )
    means = parts[..., out_width]
    mean = jnp.mean(means, axis=2)
    offsets = means - mean[:, :, None]
    m2 = jnp.sum(parts[..., out_width + 1], axis=2) + local_width * jnp.sum(
        offsets * offsets, axis=2
    )
    token_var = m2 / full_width
    centred_proj = jnp.sum(parts[..., :out_width], axis=2) + jnp.sum(
        offsets[..., None] * shard_columns.reshape(1, 1, n_rep, 1, 1, 1, out_width), axis=2
    )
    velocity = lax.rsqrt(token_var + 1e-06)[..., None] * centred_proj + shift_column
    patches = (
        velocity.reshape(3, frames, window, band_cols, LC, 2, 2)
        .transpose(1, 2, 5, 0, 3, 6, 4)
        .reshape(frames, 2 * window, 3 * 2 * band_cols, LC)
    )

    shares = neighbours(received[..., part_size:], sec, 0)
    if share == frame_rows:
        shares = shares[:, :, 0]
    latent = shares.reshape(3, n_sp, frames, lat_rows, lat_cols, LC)
    if window == patch_rows:
        latent = latent.transpose(2, 1, 3, 0, 4, 5).reshape(
            frames, n_sp * lat_rows, 3 * lat_cols, LC
        )
        clean = latent - 0.5 * patches
        clean = jnp.pad(clean, ((0, 0), (2, 2), (0, 0), (0, 0)))
        clean = lax.dynamic_slice_in_dim(clean, spi * lat_rows, lat_rows + 4, 1)
    else:
        latent = neighbours(latent.transpose(1, 2, 3, 0, 4, 5), spi, 0)
        latent = latent.transpose(1, 0, 2, 3, 4, 5).reshape(
            frames, 3 * lat_rows, 3 * lat_cols, LC
        )[:, lat_rows - 2 : 2 * lat_rows + 2]
        clean = latent - 0.5 * patches
    clean = clean[:, :, lat_cols - 2 : 2 * lat_cols + 2]

    row_global = spi * lat_rows - 2 + jnp.arange(lat_rows + 4)
    col_global = sec * lat_cols - 2 + jnp.arange(lat_cols + 4)
    row_inside = (row_global >= 0) & (row_global < lat_rows * n_sp)
    col_inside = (col_global >= 0) & (col_global < lat_cols * n_sec)
    clean = jnp.where(row_inside[None, :, None, None] & col_inside[None, None, :, None], clean, 0.0)

    inner_features = valid_conv(clean, in_weight, "DHWIO", lax.Precision.HIGHEST) + in_bias
    inside = row_inside[None, 1:-1, None, None] & col_inside[None, None, 1:-1, None]
    features = jnp.where(inside, inner_features, 0.0).astype(jnp.bfloat16)
    upsampled = jnp.repeat(jnp.repeat(features, 2, axis=1), 2, axis=2)[:, 1:-1, 1:-1, :]
    mixed = valid_conv(upsampled, conv_weight, "DHWOI", None) + conv_bias

    group_size = CO // GROUPS
    local_groups = mixed.shape[-1] // group_size
    grouped = mixed.reshape(-1, local_groups, group_size)
    block_count = grouped.shape[0] * group_size
    block_mean = jnp.sum(grouped, axis=(0, 2)) / block_count
    deviation = grouped - block_mean[None, :, None]
    block_m2 = jnp.sum(deviation * deviation, axis=(0, 2))
    n_blocks = n_sec * n_sp
    stats = jnp.broadcast_to(
        jnp.concatenate([block_mean, block_m2])[None], (n_blocks, 2 * local_groups)
    )
    stats = lax.all_to_all(stats, BLOCKS, 0, 0, tiled=False)
    group_mean = jnp.mean(stats[:, :local_groups], axis=0)
    mean_offsets = stats[:, :local_groups] - group_mean[None]
    group_var = (
        jnp.sum(stats[:, local_groups:], axis=0)
        + block_count * jnp.sum(mean_offsets * mean_offsets, axis=0)
    ) / (block_count * n_blocks)

    normed = (
        (grouped - group_mean[None, :, None]) * lax.rsqrt(group_var + 1e-06)[None, :, None]
    ).reshape(mixed.shape)
    activated = jax.nn.silu(normed * norm_gain + norm_bias)
    out_rows, out_cols, out_chan = (activated.shape[1], activated.shape[2], activated.shape[3])
    return activated.transpose(1, 2, 3, 0).reshape(out_rows, out_cols, out_chan * frames)


def solution(mesh):
    return jax.shard_map(
        per_device,
        mesh=mesh,
        in_specs=(
            P("sp", None, "section", "rep"),
            P(),
            P(),
            P(),
            P(),
            P(None, "sp", "section", None),
            P(),
            P(),
            P(None, None, None, "rep", None),
            P("rep"),
            P("rep"),
            P("rep"),
        ),
        out_specs=P("sp", "section", "rep"),
        check_vma=False,
    )
```

time: 80 us -> 43 us (0.54)
  blocking collectives: 46.1 us -> 0 us
  waiting for transfers between devices: 6.12 us -> 10.3 us
  other arithmetic: 3.28 us -> 6.71 us
  local copies, waits for them, and re-layouts: 5.24 us -> 8.59 us
  starting transfers between devices: 12.7 us -> 10.6 us
    psum x3 -> x0, blocking collectives: 46.1 us -> none  [the longest x1 19.4 us: per_device(): lax.psum((projected, first_sums, square_sums), 'rep')]
    all_to_all x1 -> x2, waiting for transfers between devices: 1.15 us -> 10.3 us  [the longest x1 5.86 us: per_device(): lax.all_to_all(send, ALL, 0, 0, tiled=False).reshape(n_sec, n_sp, n_rep, -1)]
    ppermute x4 -> x0, starting transfers between devices: 8.42 us -> none  [the longest x2 5.84 us: with_halo(): lax.ppermute(lax.slice_in_dim(block, block.shape[dim] - width, None, axis...]
    all_to_all x1 -> x2, starting transfers between devices: 4.24 us -> 10.6 us  [the longest x1 7.31 us: per_device(): lax.all_to_all(send, ALL, 0, 0, tiled=False).reshape(n_sec, n_sp, n_rep, -1)]
    ppermute x4 -> x0, waiting for transfers between devices: 4.97 us -> none  [the longest x2 3.47 us: with_halo(): lax.ppermute(lax.slice_in_dim(block, 0, width, axis=dim), axis, backward)]
    mul x2, other arithmetic: 0.09 us -> 1.45 us  [the longest x1 1.19 us: per_device(): scaled_weight = proj_weight * (1.0 + mod_scale)[None, :]]
    another operation x0 -> x1, other arithmetic: none -> 0.93 us
    mul x2, local copies, waits for them, and re-layouts: 0.23 us -> 1.09 us  [the longest x1 0.68 us: per_device(): offsets[..., None] * shard_columns.reshape(1, 1, n_rep, 1, 1, 1, out_width)]
  transfers between devices with their start and end apart: 5 -> 2, of which waited for: 3 -> 2; matrix products, arithmetic and copies ran while one was open for 4% -> 4% of each run, Pallas kernels for 0% -> 0%
where the time goes in v1:
time: 43 us; the launch traced here: 42.6 us
  starting transfers between devices  10.6 us (25%)
  waiting for transfers between devices  10.3 us (24%)
  local copies, waits for them, and re-layouts  8.59 us (20%)
  other arithmetic  6.71 us (16%)
  matrix products  5.85 us (14%)
  between operations  0.53 us (1%)
    all_to_all x1, starting transfers between devices, per_device(): lax.all_to_all(send, ALL, 0, 0, tiled=False).reshape(n_sec, n_sp, n_rep, -1)  7.31 us
    all_to_all x1, waiting for transfers between devices, per_device(): lax.all_to_all(send, ALL, 0, 0, tiled=False).reshape(n_sec, n_sp, n_rep, -1)  5.86 us
    conv_general_dilated x2, matrix products, valid_conv(): lax.conv_general_dilated(front[None], kernel, (1, 1, 1), 'VALID', dimensi...  4.84 us
    all_to_all x1, waiting for transfers between devices, per_device(): stats = lax.all_to_all(stats, BLOCKS, 0, 0, tiled=False)  4.45 us
    all_to_all x1, starting transfers between devices, per_device(): stats = lax.all_to_all(stats, BLOCKS, 0, 0, tiled=False)  3.31 us
    unnamed x22, local copies, waits for them, and re-layouts  1.29 us
    mul x1, other arithmetic, per_device(): scaled_weight = proj_weight * (1.0 + mod_scale)[None, :]  1.19 us
    reduce_sum x1, other arithmetic, per_device(): shard_mean = jnp.mean(tokens, axis=-1, keepdims=True)  1.01 us
  transfers between devices with their start and end apart: 2, of which 2 were waited for; matrix products, arithmetic and copies ran while one was open for 4% of the time, Pallas kernels for 0%

profile of v1, /device:TPU:0, one launch (start us, length us, event | category | flops | bytes accessed | tf_op | source)
XLA Modules:
  0.0 42.6 jit_solution(17001831079033753043)
XLA Ops:
  0.0 1.0 %reduce_sum.131 = f32[2,6]{0,1:T(8,128)S(1)} reduce(f32[1,2,6,768]{3,1,2,0:T(2,128)} %param.12, f32[]{:T(128)} %constant.20.clone.1), dimensions={0,3}, to_apply=%region_0.0 | reduce | flops 9204 | bytes 36916 | tf_op jit(solution)/shard_map/reduce_sum | solution.py:69
  1.2 0.7 %broadcast_add_fusion = f32[3072]{0:T(1024)S(1)} fusion(f32[3072]{0:T(1024)} %param.13), kind=kLoop, calls=%fused_computation.58 | loop fusion | flops 3072 | bytes 24576 | tf_op jit(solution)/shard_map/add | solution.py:56
  1.9 0.7 %copy.60 = f32[2,2,12,16]{3,2,1,0:T(8,128)S(1)} copy(f32[2,2,12,16]{3,1,2,0:T(2,128)} %param.17) | data formatting | bytes 6144 | tf_op args[5]
  2.7 0.9 %subtract_bitcast_fusion = (f32[2,6,768]{2,0,1:T(2,128)S(1)}, f32[2,6]{0,1:T(8,128)S(1)}) fusion(f32[1,2,6,768]{3,1,2,0:T(2,128)} %param.12, f32[2,6]{0,1:T(8,128)S(1)} %get-tuple-element.13), kind=kLoop, calls=%fused_computation.52 | loop fusion | flops 27636 | bytes 73824 | tf_op jit(solution)/shard_map/reshape.5
  3.8 1.2 %broadcast_multiply_fusion = f32[64,3072]{1,0:T(8,128)S(1)} fusion(f32[64,3072]{1,0:T(8,128)} %param.15, f32[3072]{0:T(1024)S(1)} %broadcast_add_fusion), kind=kLoop, calls=%fused_computation.21 | loop fusion | flops 196608 | bytes 1585152 | tf_op jit(solution)/shard_map/mul | solution.py:56
  5.0 0.3 convolution_bitcast_fusion
  5.5 0.7 %broadcast.270 = f32[32,1,984]{2,1,0:T(1,128)} broadcast(f32[984]{0:T(1024)S(1)} %pad_maximum_fusion.2), dimensions={2} | broadcast | bytes 129888 | tf_op jit(solution)/shard_map/all_to_all | solution.py:109
  6.2 7.3 %all-to-all-start = ((f32[32,1,984]{2,1,0:T(1,128)}), f32[32,1,984]{2,1,0:T(1,128)S(1)}, u32[]{:S(2)}, u32[]{:S(2)}) async-start(f32[32,1,984]{2,1,0:T(1,128)} %broadcast.270), calls=%async_computation | async-start | bytes 262144 | tf_op jit(solution)/shard_map/all_to_all | solution.py:109
  13.6 0.7 %fusion.11 = f32[64]{0:T(128)S(1)} fusion(f32[64]{0:T(128)S(1)} %copy-done.5, f32[64,3072]{1,0:T(8,128)S(1)} %copy-done.1, f32[3072,1]{0,1:T(1,128)S(1)} %bitcast.95), kind=kOutput, calls=%fused_computation.12 | convolution fusion | flops 2359360 | bytes 799232 | tf_op jit(solution)/shard_map/dot_general | solution.py:59
  14.6 0.4 reshape.280
  15.1 0.2 reduce_sum.137
  15.4 5.9 %all-to-all-done = f32[32,1,984]{2,1,0:T(1,128)S(1)} async-done(((f32[32,1,984]{2,1,0:T(1,128)}), f32[32,1,984]{2,1,0:T(1,128)S(1)}, u32[]{:S(2)}, u32[]{:S(2)}) %all-to-all-start) | async-done | bytes 125984 | tf_op jit(solution)/shard_map/all_to_all | solution.py:109
  21.3 0.3 reduce.13
  21.8 0.2 reshape.279
  22.0 0.3 slice_reduce_fusion.3
  22.5 0.7 %copy.80 = f32[3,2,4,1,2,6,1]{2,5,4,1,0,6,3:T(8,128)S(1)} copy(f32[3,2,4,1,2,6,1]{6,5,4,2,1,0,3:T(8,128)S(1)} %slice_subtract_fusion) | data formatting | bytes 2304 | tf_op jit(solution)/shard_map/mul | solution.py:122
  23.4 0.2 multiply_reduce_fusion
  23.6 0.2 copy.64
  23.8 0.3 multiply_bitcast_fusion
  24.1 0.4 copy.65
  24.8 2.8 %convolution_select_fusion = f32[2,4,8,2,512]{4,2,3,1,0:T(8,128)S(1)} fusion(f32[3,3,3,16,512]{4,3,2,1,0:T(8,128)} %param.18, f32[4,6,1,7,2,16]{5,3,4,1,0,2:T(8,128)S(1)} %slice.66, f32[4,6,1,8,2,16]{5,3,4,1,0,2:T(8,128)S(1)} %copy.68, pred[8,2]{0,1:T(4,128)(4,1)S(1)} %copy-done.9), kind=kOutput, calls=%fused_computation.8 | convolution fusion | flops 339841024 | bytes 1192976 | tf_op jit(solution)/shard_map/conv_general_dilated | solution.py:16
  27.7 0.2 copy.69
  28.4 0.2 maximum_bitcast_fusion
  28.6 0.5 %copy.82 = bf16[4,6,1,26,512]{4,0,3,1,2:T(4,128)(2,1)S(1)} copy(bf16[4,6,1,26,512]{4,1,3,0,2:T(8,128)(2,1)S(1)} %maximum_bitcast_fusion) | data formatting | bytes 1277952
  29.1 0.3 pad.16.clone
  29.4 0.4 %copy.72 = bf16[4,6,1,8,4,512]{5,3,4,1,0,2:T(8,128)(2,1)S(1)} copy(bf16[4,6,1,8,4,512]{5,0,4,3,1,2:T(4,128)(2,1)S(1)} %bitcast.79) | data formatting | bytes 1572864 | tf_op jit(solution)/shard_map/conv_general_dilated | solution.py:16
  30.0 2.0 %select_reduce_fusion.1 = (f32[64]{0:T(128)S(1)}, f32[2,4,8,4,64]{4,2,3,1,0:T(8,128)S(1)}) fusion(f32[64]{0:T(128)S(1)} %copy-done.4, pred[8,4]{0,1:T(4,128)(4,1)S(1)} %copy-done.8, bf16[3,3,3,64,512]{4,3,2,1,0:T(8,128)(2,1)S(1)} %copy-done, bf16[4,6,1,7,2,512]{5,3,4,1,0,2:T(8,128)(2,1)S(1)} %slice.70, bf16[4,6,1,8,4,512]{5,3,4,1,0,2:T(8,128)(2,1)S(1)} %copy.72), kind=kOutput, calls=%fused_computation.41 | convolution fusion | flops 456589248 | bytes 2966048 | tf_op jit(solution)/shard_map/conv_general_dilated | solution.py:16
  32.8 0.6 %broadcast_in_dim.89 = f32[8,1,16]{2,1,0:T(1,128)} broadcast(f32[16]{0:T(128)S(1)} %pad_maximum_fusion.3), dimensions={2} | broadcast | bytes 576 | tf_op jit(solution)/shard_map/broadcast_in_dim | solution.py:170
  33.4 3.3 %all-to-all-start.1 = ((f32[8,1,16]{2,1,0:T(1,128)}), f32[8,1,16]{2,1,0:T(1,128)S(1)}, u32[]{:S(2)}, u32[]{:S(2)}) async-start(f32[8,1,16]{2,1,0:T(1,128)} %broadcast_in_dim.89), calls=%async_computation.1 | async-start | bytes 8192 | tf_op jit(solution)/shard_map/all_to_all | solution.py:173
  36.8 4.4 %all-to-all-done.1 = f32[8,1,16]{2,1,0:T(1,128)S(1)} async-done(((f32[8,1,16]{2,1,0:T(1,128)}), f32[8,1,16]{2,1,0:T(1,128)S(1)}, u32[]{:S(2)}, u32[]{:S(2)}) %all-to-all-start.1) | async-done | bytes 544 | tf_op jit(solution)/shard_map/all_to_all | solution.py:173
  41.7 0.2 copy.74
  41.9 0.7 %copy.75 = f32[4,24,128]{2,1,0:T(8,128)} copy(f32[4,24,128]{1,2,0:T(8,128)S(1)} %bitcast.83) | data formatting | bytes 98304 | tf_op jit(solution)/shard_map/reshape | solution.py:186
  (82 shorter events, 3.9 us)
Async XLA Ops:
  0.0 30.0 %copy-start = (bf16[3,3,3,64,512]{4,3,2,1,0:T(8,128)(2,1)S(1)}, bf16[3,3,3,64,512]{4,3,2,1,0:T(8,128)(2,1)}, u32[]{:S(2)}) copy-start(bf16[3,3,3,64,512]{4,3,2,1,0:T(8,128)(2,1)} %param.20) | copy-start | bytes 5308420
  0.0 13.6 %copy-start.1 = (f32[64,3072]{1,0:T(8,128)S(1)}, f32[64,3072]{1,0:T(8,128)}, u32[]{:S(2)}) copy-start(f32[64,3072]{1,0:T(8,128)} %param.15) | copy-start | bytes 2359300
  0.0 13.6 %copy-start.5 = (f32[64]{0:T(128)S(1)}, f32[64]{0:T(128)}, u32[]{:S(2)}) copy-start(f32[64]{0:T(128)} %param.16) | copy-start | bytes 772
  0.0 13.6 %copy-start.2 = (f32[3072]{0:T(1024)S(1)}, f32[3072]{0:T(1024)}, u32[]{:S(2)}) copy-start(f32[3072]{0:T(1024)} %param.14) | copy-start | bytes 36868
  6.2 15.1 %all-to-all-start = ((f32[32,1,984]{2,1,0:T(1,128)}), f32[32,1,984]{2,1,0:T(1,128)S(1)}, u32[]{:S(2)}, u32[]{:S(2)}) async-start(f32[32,1,984]{2,1,0:T(1,128)} %broadcast.270), calls=%async_computation | async-start | bytes 262144 | tf_op jit(solution)/shard_map/all_to_all | solution.py:109
  23.8 1.0 %copy-start.9 = (pred[8,2]{0,1:T(4,128)(4,1)S(1)}, pred[8,2]{0,1:T(4,128)(4,1)}, u32[]{:S(2)}) copy-start(pred[8,2]{0,1:T(4,128)(4,1)} %constant.86) | copy-start | bytes 52
  24.8 3.0 %copy-start.3 = (f32[512]{0:T(512)S(1)}, f32[512]{0:T(512)}, u32[]{:S(2)}) copy-start(f32[512]{0:T(512)} %param.19) | copy-start | bytes 6148
  29.1 0.9 %copy-start.4 = (f32[64]{0:T(128)S(1)}, f32[64]{0:T(128)}, u32[]{:S(2)}) copy-start(f32[64]{0:T(128)} %param.21) | copy-start | bytes 772
  29.1 0.9 %copy-start.8 = (pred[8,4]{0,1:T(4,128)(4,1)S(1)}, pred[8,4]{0,1:T(4,128)(4,1)}, u32[]{:S(2)}) copy-start(pred[8,4]{0,1:T(4,128)(4,1)} %constant.85) | copy-start | bytes 100
  30.0 11.7 %copy-start.6 = (f32[64]{0:T(128)S(1)}, f32[64]{0:T(128)}, u32[]{:S(2)}) copy-start(f32[64]{0:T(128)} %param.23) | copy-start | bytes 772
  30.0 11.6 %copy-start.7 = (f32[64]{0:T(128)S(1)}, f32[64]{0:T(128)}, u32[]{:S(2)}) copy-start(f32[64]{0:T(128)} %param.22) | copy-start | bytes 772
  33.4 7.8 %all-to-all-start.1 = ((f32[8,1,16]{2,1,0:T(1,128)}), f32[8,1,16]{2,1,0:T(1,128)S(1)}, u32[]{:S(2)}, u32[]{:S(2)}) async-start(f32[8,1,16]{2,1,0:T(1,128)} %broadcast_in_dim.89), calls=%async_computation.1 | async-start | bytes 8192 | tf_op jit(solution)/shard_map/all_to_all | solution.py:173

commit v2 on v1

--- a/solution.py
+++ b/solution.py
@@ -53,6 +53,56 @@
     full_width = local_width * n_rep
     out_width = proj_weight.shape[0]
 
+    low = rep * local_width
+    local_weight = lax.dynamic_slice_in_dim(proj_weight, low, local_width, 1) * (
+        1.0 + lax.dynamic_slice_in_dim(mod_scale, low, local_width, 0)
+    )[None, :]
+
+    rows = tokens.reshape(-1, local_width)
+    shard_mean = jnp.mean(rows, axis=-1, keepdims=True)
+    centred = rows - shard_mean
+    shard_m2 = jnp.sum(centred * centred, axis=-1, keepdims=True)
+    projected = lax.dot_general(
+        centred,
+        local_weight,
+        (((1,), (1,)), ((), ())),
+        precision=lax.Precision.HIGHEST,
+        preferred_element_type=jnp.float32,
+    )
+    partial = jnp.concatenate([projected, shard_mean, shard_m2], axis=-1).reshape(
+        tok_frames, patch_rows, band_cols, out_width + 2
+    )
+
+    slab = lat_rows // 2
+    if patch_rows <= slab + 2:
+        window = patch_rows
+        per_slab = jnp.broadcast_to(partial[None], (n_sp,) + partial.shape)
+    else:
+        window = slab + 2
+        padded = jnp.pad(partial, ((0, 0), (1, 1), (0, 0), (0, 0)))
+        per_slab = jnp.stack([padded[:, p * slab : p * slab + window] for p in range(n_sp)])
+    per_slab = per_slab.reshape(n_sp, -1)
+    part_size = per_slab.shape[1]
+
+    frame_rows = frames * lat_rows
+    if frame_rows % n_rep == 0:
+        share = frame_rows // n_rep
+        latent_part = lax.dynamic_slice_in_dim(
+            noisy_latent.reshape(frame_rows, -1), rep * share, share, 0
+        ).reshape(-1)
+    else:
+        share = frame_rows
+        latent_part = noisy_latent.reshape(-1)
+
+    send = jnp.concatenate(
+        [
+            jnp.broadcast_to(per_slab[None, :, None], (n_sec, n_sp, n_rep, part_size)),
+            jnp.broadcast_to(latent_part, (n_sec, n_sp, n_rep, latent_part.shape[0])),
+        ],
+        axis=-1,
+    ).reshape(n_dev, -1)
+    received = lax.all_to_all(send, ALL, 0, 0, tiled=False).reshape(n_sec, n_sp, n_rep, -1)
+
     scaled_weight = proj_weight * (1.0 + mod_scale)[None, :]
     shard_columns = jnp.sum(scaled_weight.reshape(out_width, n_rep, local_width), axis=2).T
     shift_column = (
@@ -64,50 +114,6 @@
         )
         + proj_bias
     )
-    local_weight = lax.dynamic_slice_in_dim(scaled_weight, rep * local_width, local_width, 1)
-
-    shard_mean = jnp.mean(tokens, axis=-1, keepdims=True)
-    centred = tokens - shard_mean
-    shard_m2 = jnp.sum(centred * centred, axis=-1, keepdims=True)
-    projected = lax.dot_general(
-        centred,
-        local_weight,
-        (((3,), (1,)), ((), ())),
-        precision=lax.Precision.HIGHEST,
-        preferred_element_type=jnp.float32,
-    )
-    partial = jnp.concatenate([projected, shard_mean, shard_m2], axis=-1)
-
-    slab = lat_rows // 2
-    if patch_rows <= slab + 2:
-        window = patch_rows
-        per_slab = jnp.broadcast_to(partial[None], (n_sp,) + partial.shape)
-    else:
-        window = slab + 2
-        padded = jnp.pad(partial, ((0, 0), (1, 1), (0, 0), (0, 0)))
-        per_slab = jnp.stack([padded[:, p * slab : p * slab + window] for p in range(n_sp)])
-    per_slab = per_slab.reshape(n_sp, -1)
-    part_size = per_slab.shape[1]
-
-    frame_rows = frames * lat_rows
-    if frame_rows % n_rep == 0:
-        share = frame_rows // n_rep
-        latent_part = lax.dynamic_slice_in_dim(
-            noisy_latent.reshape(frame_rows, -1), rep * share, share, 0
-        ).reshape(-1)
-    else:
-        share = frame_rows
-        latent_part = noisy_latent.reshape(-1)
-
-    send = jnp.concatenate(
-        [
-            jnp.broadcast_to(per_slab[None, :, None], (n_sec, n_sp, n_rep, part_size)),
-            jnp.broadcast_to(latent_part, (n_sec, n_sp, n_rep, latent_part.shape[0])),
-        ],
-        axis=-1,
-    ).reshape(n_dev, -1)
-    received = lax.all_to_all(send, ALL, 0, 0, tiled=False).reshape(n_sec, n_sp, n_rep, -1)
-
     parts = neighbours(received[..., :part_size], sec, 0).reshape(
         3, n_sp, n_rep, tok_frames, window, band_cols, out_width + 2
     )
@@ -153,7 +159,7 @@
     col_inside = (col_global >= 0) & (col_global < lat_cols * n_sec)
     clean = jnp.where(row_inside[None, :, None, None] & col_inside[None, None, :, None], clean, 0.0)
 
-    inner_features = valid_conv(clean, in_weight, "DHWIO", lax.Precision.HIGHEST) + in_bias
+    inner_features = valid_conv(clean, in_weight, "DHWIO", lax.Precision.HIGH) + in_bias
     inside = row_inside[None, 1:-1, None, None] & col_inside[None, None, 1:-1, None]
     features = jnp.where(inside, inner_features, 0.0).astype(jnp.bfloat16)
     upsampled = jnp.repeat(jnp.repeat(features, 2, axis=1), 2, axis=2)[:, 1:-1, 1:-1, :]

time: 43 us -> 43 us (level)
  waiting for transfers between devices: 10.3 us -> 8.42 us
  other arithmetic: 6.71 us -> 8.33 us
    all_to_all x1, waiting for transfers between devices: 5.86 us -> 3.97 us  [per_device(): lax.all_to_all(send, ALL, 0, 0, tiled=False).reshape(n_sec, n_sp, n_rep, -1)]
    reduce_sum x1 -> x2, other arithmetic: 1.01 us -> 1.95 us  [the longest x1 1.01 us: per_device(): shard_mean = jnp.mean(rows, axis=-1, keepdims=True)]
    another operation x1 -> x0, other arithmetic: 0.93 us -> none
    dot_general x1, matrix products: 0.29 us -> 1.21 us  [per_device(): lax.dot_general(centred, local_weight, (((1,), (1,)), ((), ())), precisio...]
    sub x0 -> x1, other arithmetic: none -> 0.85 us  [per_device(): centred = rows - shard_mean]
    add x0 -> x1, other arithmetic: none -> 0.77 us  [per_device(): 1.0 + lax.dynamic_slice_in_dim(mod_scale, low, local_width, 0)]
    conv_general_dilated x2, matrix products: 4.84 us -> 4.11 us  [valid_conv(): lax.conv_general_dilated(front[None], kernel, (1, 1, 1), 'VALID', dimensi...]
  transfers between devices with their start and end apart: 2 -> 2, of which waited for: 2 -> 2; matrix products, arithmetic and copies ran while one was open for 4% -> 9% of each run, Pallas kernels for 0% -> 0%
where the time goes in v2:
time: 43 us; the launch traced here: 42.5 us
  starting transfers between devices  10.6 us (25%)
  local copies, waits for them, and re-layouts  8.59 us (20%)
  waiting for transfers between devices  8.42 us (20%)
  other arithmetic  8.33 us (19%)
  matrix products  6.05 us (14%)
  between operations  0.5 us (1%)
    all_to_all x1, starting transfers between devices, per_device(): lax.all_to_all(send, ALL, 0, 0, tiled=False).reshape(n_sec, n_sp, n_rep, -1)  7.3 us
    all_to_all x1, waiting for transfers between devices, per_device(): stats = lax.all_to_all(stats, BLOCKS, 0, 0, tiled=False)  4.45 us
    conv_general_dilated x2, matrix products, valid_conv(): lax.conv_general_dilated(front[None], kernel, (1, 1, 1), 'VALID', dimensi...  4.11 us
    all_to_all x1, waiting for transfers between devices, per_device(): lax.all_to_all(send, ALL, 0, 0, tiled=False).reshape(n_sec, n_sp, n_rep, -1)  3.97 us
    all_to_all x1, starting transfers between devices, per_device(): stats = lax.all_to_all(stats, BLOCKS, 0, 0, tiled=False)  3.31 us
    unnamed x22, local copies, waits for them, and re-layouts  1.3 us
    dot_general x1, matrix products, per_device(): lax.dot_general(centred, local_weight, (((1,), (1,)), ((), ())), precisio...  1.21 us
    mul x1, other arithmetic, per_device(): scaled_weight = proj_weight * (1.0 + mod_scale)[None, :]  1.19 us
  transfers between devices with their start and end apart: 2, of which 2 were waited for; matrix products, arithmetic and copies ran while one was open for 9% of the time, Pallas kernels for 0%

profile of v2, /device:TPU:0, one launch (start us, length us, event | category | flops | bytes accessed | tf_op | source)
XLA Modules:
  0.0 42.5 jit_solution(7305127757635210021)
XLA Ops:
  0.0 1.0 %reduce_sum.131 = f32[2,6]{0,1:T(8,128)S(1)} reduce(f32[1,2,6,768]{3,1,2,0:T(2,128)} %param.12, f32[]{:T(128)} %constant.19.clone.1), dimensions={0,3}, to_apply=%region_0.0 | reduce | flops 9204 | bytes 36916 | tf_op jit(solution)/shard_map/reduce_sum | solution.py:62
  1.0 0.9 %multiply_reduce_fusion.1 = f32[2,6]{0,1:T(8,128)S(1)} fusion(f32[1,2,6,768]{3,1,2,0:T(2,128)} %param.12, f32[2,6]{0,1:T(8,128)S(1)} %get-tuple-element.11), kind=kLoop, calls=%fused_computation.54 | loop fusion | flops 27636 | bytes 36960 | tf_op jit(solution)/shard_map/reduce_sum | solution.py:64
  2.0 0.8 %bitcast_subtract_fusion = f32[2,6,768]{2,0,1:T(2,128)S(1)} fusion(f32[1,2,6,768]{3,1,2,0:T(2,128)} %param.12, f32[2,6]{0,1:T(8,128)S(1)} %get-tuple-element.11), kind=kLoop, calls=%fused_computation.53 | loop fusion | flops 9216 | bytes 73776 | tf_op jit(solution)/shard_map/sub | solution.py:63
  3.1 0.8 %dynamic-slice_add_fusion = f32[768]{0:T(1024)S(1)} fusion(f32[3072]{0:T(1024)} %param.13, s32[]{:T(128)S(6)} %select_n.22), kind=kLoop, calls=%fused_computation.64 | loop fusion | flops 768 | bytes 6148 | tf_op jit(solution)/shard_map/add | solution.py:58
  3.9 1.2 %convolution_bitcast_fusion = f32[1,1,2,6,64]{4,3,2,1,0:T(8,128)S(1)} fusion(f32[64,3072]{1,0:T(8,128)} %param.15, s32[]{:T(128)S(6)} %select_n.22, f32[768]{0:T(1024)S(1)} %dynamic-slice_add_fusion, f32[2,6,768]{2,0,1:T(2,128)S(1)} %bitcast_subtract_fusion), kind=kOutput, calls=%fused_computation.10 | convolution fusion | flops 7127040 | bytes 239620 | tf_op jit(solution)/shard_map/dot_general | solution.py:65
  5.2 0.7 %copy.62 = f32[2,2,12,16]{3,2,1,0:T(8,128)S(1)} copy(f32[2,2,12,16]{3,1,2,0:T(2,128)} %param.17) | data formatting | bytes 6144 | tf_op args[5]
  6.2 0.7 %broadcast.284 = f32[32,1,984]{2,1,0:T(1,128)} broadcast(f32[984]{0:T(1024)S(1)} %pad_maximum_fusion.2), dimensions={2} | broadcast | bytes 129888 | tf_op jit(solution)/shard_map/all_to_all | solution.py:104
  6.9 7.3 %all-to-all-start = ((f32[32,1,984]{2,1,0:T(1,128)}), f32[32,1,984]{2,1,0:T(1,128)S(1)}, u32[]{:S(2)}, u32[]{:S(2)}) async-start(f32[32,1,984]{2,1,0:T(1,128)} %broadcast.284), calls=%async_computation | async-start | bytes 262144 | tf_op jit(solution)/shard_map/all_to_all | solution.py:104
  14.2 0.7 %broadcast_add_fusion = f32[3072]{0:T(1024)S(1)} fusion(f32[3072]{0:T(1024)} %param.13), kind=kLoop, calls=%fused_computation.59 | loop fusion | flops 3072 | bytes 24576 | tf_op jit(solution)/shard_map/add | solution.py:106
  14.9 1.2 %broadcast_multiply_fusion = f32[64,3072]{1,0:T(8,128)S(1)} fusion(f32[64,3072]{1,0:T(8,128)} %param.15, f32[3072]{0:T(1024)S(1)} %broadcast_add_fusion), kind=kLoop, calls=%fused_computation.21 | loop fusion | flops 196608 | bytes 1585152 | tf_op jit(solution)/shard_map/mul | solution.py:106
  16.1 0.7 %fusion.11 = f32[64]{0:T(128)S(1)} fusion(f32[64]{0:T(128)S(1)} %copy-done.5, f32[64,3072]{1,0:T(8,128)S(1)} %copy-done.1, f32[3072,1]{0,1:T(1,128)S(1)} %bitcast.95), kind=kOutput, calls=%fused_computation.12 | convolution fusion | flops 2359360 | bytes 799232 | tf_op jit(solution)/shard_map/dot_general | solution.py:109
  17.2 0.4 reshape.307
  17.6 0.2 reduce_sum.137
  17.9 4.0 %all-to-all-done = f32[32,1,984]{2,1,0:T(1,128)S(1)} async-done(((f32[32,1,984]{2,1,0:T(1,128)}), f32[32,1,984]{2,1,0:T(1,128)S(1)}, u32[]{:S(2)}, u32[]{:S(2)}) %all-to-all-start) | async-done | bytes 125984 | tf_op jit(solution)/shard_map/all_to_all | solution.py:104
  21.9 0.3 reduce.13
  22.6 0.3 slice_reduce_fusion.3
  23.1 0.7 %copy.82 = f32[3,2,4,1,2,6,1]{2,5,4,1,0,6,3:T(8,128)S(1)} copy(f32[3,2,4,1,2,6,1]{6,5,4,2,1,0,3:T(8,128)S(1)} %slice_subtract_fusion) | data formatting | bytes 2304 | tf_op jit(solution)/shard_map/mul | solution.py:128
  24.0 0.2 multiply_reduce_fusion
  24.2 0.2 copy.66
  24.5 0.3 multiply_bitcast_fusion
  24.7 0.4 copy.67
  25.4 2.1 %convolution_select_fusion = f32[2,4,8,2,512]{4,2,3,1,0:T(8,128)S(1)} fusion(f32[3,3,3,16,512]{4,3,2,1,0:T(8,128)} %param.18, f32[4,6,1,7,2,16]{5,3,4,1,0,2:T(8,128)S(1)} %slice.66, f32[4,6,1,8,2,16]{5,3,4,1,0,2:T(8,128)S(1)} %copy.70, pred[8,2]{0,1:T(4,128)(4,1)S(1)} %copy-done.9), kind=kOutput, calls=%fused_computation.8 | convolution fusion | flops 169971712 | bytes 1192976 | tf_op jit(solution)/shard_map/conv_general_dilated | solution.py:16
  27.6 0.2 copy.71
  28.3 0.2 maximum_bitcast_fusion
  28.5 0.5 %copy.84 = bf16[4,6,1,26,512]{4,0,3,1,2:T(4,128)(2,1)S(1)} copy(bf16[4,6,1,26,512]{4,1,3,0,2:T(8,128)(2,1)S(1)} %maximum_bitcast_fusion) | data formatting | bytes 1277952
  29.0 0.3 pad.16.clone
  29.3 0.4 %copy.74 = bf16[4,6,1,8,4,512]{5,3,4,1,0,2:T(8,128)(2,1)S(1)} copy(bf16[4,6,1,8,4,512]{5,0,4,3,1,2:T(4,128)(2,1)S(1)} %bitcast.79) | data formatting | bytes 1572864 | tf_op jit(solution)/shard_map/conv_general_dilated | solution.py:16
  29.9 2.0 %select_reduce_fusion.1 = (f32[64]{0:T(128)S(1)}, f32[2,4,8,4,64]{4,2,3,1,0:T(8,128)S(1)}) fusion(f32[64]{0:T(128)S(1)} %copy-done.4, pred[8,4]{0,1:T(4,128)(4,1)S(1)} %copy-done.8, bf16[3,3,3,64,512]{4,3,2,1,0:T(8,128)(2,1)S(1)} %copy-done, bf16[4,6,1,7,2,512]{5,3,4,1,0,2:T(8,128)(2,1)S(1)} %slice.70, bf16[4,6,1,8,4,512]{5,3,4,1,0,2:T(8,128)(2,1)S(1)} %copy.74), kind=kOutput, calls=%fused_computation.42 | convolution fusion | flops 456589248 | bytes 2966048 | tf_op jit(solution)/shard_map/conv_general_dilated | solution.py:16
  32.7 0.6 %broadcast_in_dim.86 = f32[8,1,16]{2,1,0:T(1,128)} broadcast(f32[16]{0:T(128)S(1)} %pad_maximum_fusion.3), dimensions={2} | broadcast | bytes 576 | tf_op jit(solution)/shard_map/broadcast_in_dim | solution.py:176
  33.3 3.3 %all-to-all-start.1 = ((f32[8,1,16]{2,1,0:T(1,128)}), f32[8,1,16]{2,1,0:T(1,128)S(1)}, u32[]{:S(2)}, u32[]{:S(2)}) async-start(f32[8,1,16]{2,1,0:T(1,128)} %broadcast_in_dim.86), calls=%async_computation.1 | async-start | bytes 8192 | tf_op jit(solution)/shard_map/all_to_all | solution.py:179
  36.7 4.4 %all-to-all-done.1 = f32[8,1,16]{2,1,0:T(1,128)S(1)} async-done(((f32[8,1,16]{2,1,0:T(1,128)}), f32[8,1,16]{2,1,0:T(1,128)S(1)}, u32[]{:S(2)}, u32[]{:S(2)}) %all-to-all-start.1) | async-done | bytes 544 | tf_op jit(solution)/shard_map/all_to_all | solution.py:179
  41.8 0.7 %copy.77 = f32[4,24,128]{2,1,0:T(8,128)} copy(f32[4,24,128]{1,2,0:T(8,128)S(1)} %bitcast.83) | data formatting | bytes 98304 | tf_op jit(solution)/shard_map/reshape | solution.py:192
  (84 shorter events, 4.2 us)
Async XLA Ops:
  0.0 29.9 %copy-start = (bf16[3,3,3,64,512]{4,3,2,1,0:T(8,128)(2,1)S(1)}, bf16[3,3,3,64,512]{4,3,2,1,0:T(8,128)(2,1)}, u32[]{:S(2)}) copy-start(bf16[3,3,3,64,512]{4,3,2,1,0:T(8,128)(2,1)} %param.20) | copy-start | bytes 5308420
  0.0 16.1 %copy-start.1 = (f32[64,3072]{1,0:T(8,128)S(1)}, f32[64,3072]{1,0:T(8,128)}, u32[]{:S(2)}) copy-start(f32[64,3072]{1,0:T(8,128)} %param.15) | copy-start | bytes 2359300
  0.0 16.1 %copy-start.5 = (f32[64]{0:T(128)S(1)}, f32[64]{0:T(128)}, u32[]{:S(2)}) copy-start(f32[64]{0:T(128)} %param.16) | copy-start | bytes 772
  0.0 16.1 %copy-start.2 = (f32[3072]{0:T(1024)S(1)}, f32[3072]{0:T(1024)}, u32[]{:S(2)}) copy-start(f32[3072]{0:T(1024)} %param.14) | copy-start | bytes 36868
  6.9 15.0 %all-to-all-start = ((f32[32,1,984]{2,1,0:T(1,128)}), f32[32,1,984]{2,1,0:T(1,128)S(1)}, u32[]{:S(2)}, u32[]{:S(2)}) async-start(f32[32,1,984]{2,1,0:T(1,128)} %broadcast.284), calls=%async_computation | async-start | bytes 262144 | tf_op jit(solution)/shard_map/all_to_all | solution.py:104
  24.4 1.0 %copy-start.9 = (pred[8,2]{0,1:T(4,128)(4,1)S(1)}, pred[8,2]{0,1:T(4,128)(4,1)}, u32[]{:S(2)}) copy-start(pred[8,2]{0,1:T(4,128)(4,1)} %constant.87) | copy-start | bytes 52
  25.4 2.3 %copy-start.3 = (f32[512]{0:T(512)S(1)}, f32[512]{0:T(512)}, u32[]{:S(2)}) copy-start(f32[512]{0:T(512)} %param.19) | copy-start | bytes 6148
  29.0 0.9 %copy-start.4 = (f32[64]{0:T(128)S(1)}, f32[64]{0:T(128)}, u32[]{:S(2)}) copy-start(f32[64]{0:T(128)} %param.21) | copy-start | bytes 772
  29.0 0.9 %copy-start.8 = (pred[8,4]{0,1:T(4,128)(4,1)S(1)}, pred[8,4]{0,1:T(4,128)(4,1)}, u32[]{:S(2)}) copy-start(pred[8,4]{0,1:T(4,128)(4,1)} %constant.86) | copy-start | bytes 100
  29.9 11.7 %copy-start.6 = (f32[64]{0:T(128)S(1)}, f32[64]{0:T(128)}, u32[]{:S(2)}) copy-start(f32[64]{0:T(128)} %param.23) | copy-start | bytes 772
  29.9 11.6 %copy-start.7 = (f32[64]{0:T(128)S(1)}, f32[64]{0:T(128)}, u32[]{:S(2)}) copy-start(f32[64]{0:T(128)} %param.22) | copy-start | bytes 772
  33.3 7.8 %all-to-all-start.1 = ((f32[8,1,16]{2,1,0:T(1,128)}), f32[8,1,16]{2,1,0:T(1,128)S(1)}, u32[]{:S(2)}, u32[]{:S(2)}) async-start(f32[8,1,16]{2,1,0:T(1,128)} %broadcast_in_dim.86), calls=%async_computation.1 | async-start | bytes 8192 | tf_op jit(solution)/shard_map/all_to_all | solution.py:179

commit v3 on v2

--- a/solution.py
+++ b/solution.py
@@ -1,6 +1,8 @@
 import jax
 import jax.numpy as jnp
 from jax import lax
+from jax.experimental import pallas as pl
+from jax.experimental.pallas import tpu as pltpu
 from jax.sharding import PartitionSpec as P
 
 D = 3072
@@ -23,6 +25,53 @@
         preferred_element_type=jnp.float32,
     )
     return result[0]
+
+
+def shard_kernel(rep_ref, tok_ref, weight_ref, scale_ref, proj_ref, mean_ref, m2_ref):
+    weight = weight_ref[...] * (1.0 + scale_ref[...])
+    for frame in range(tok_ref.shape[0]):
+        for row in range(tok_ref.shape[1]):
+            x = tok_ref[frame, row]
+            mean = jnp.mean(x, axis=1, keepdims=True)
+            centred = x - mean
+            proj_ref[frame, row] = lax.dot_general(
+                centred,
+                weight,
+                (((1,), (1,)), ((), ())),
+                precision=lax.Precision.HIGHEST,
+                preferred_element_type=jnp.float32,
+            )
+            mean_ref[frame, row] = mean
+            m2_ref[frame, row] = jnp.sum(centred * centred, axis=1, keepdims=True)
+
+
+def shard_moments(tokens, proj_weight, mod_scale, rep):
+    tok_frames, patch_rows, band_cols, local_width = tokens.shape
+    out_width = proj_weight.shape[0]
+    whole = lambda i, r: (0, 0, 0, 0)
+    lead = (tok_frames, patch_rows, band_cols)
+    return pl.pallas_call(
+        shard_kernel,
+        grid_spec=pltpu.PrefetchScalarGridSpec(
+            num_scalar_prefetch=1,
+            grid=(1,),
+            in_specs=[
+                pl.BlockSpec(tokens.shape, whole),
+                pl.BlockSpec((out_width, local_width), lambda i, r: (0, r[0])),
+                pl.BlockSpec((1, local_width), lambda i, r: (0, r[0])),
+            ],
+            out_specs=[
+                pl.BlockSpec(lead + (out_width,), whole),
+                pl.BlockSpec(lead + (1,), whole),
+                pl.BlockSpec(lead + (1,), whole),
+            ],
+        ),
+        out_shape=[
+            jax.ShapeDtypeStruct(lead + (out_width,), jnp.float32),
+            jax.ShapeDtypeStruct(lead + (1,), jnp.float32),
+            jax.ShapeDtypeStruct(lead + (1,), jnp.float32),
+        ],
+    )(rep.reshape(1).astype(jnp.int32), tokens, proj_weight, mod_scale.reshape(1, -1))
 
 
 def neighbours(stack, index, axis):
@@ -53,25 +102,8 @@
     full_width = local_width * n_rep
     out_width = proj_weight.shape[0]
 
-    low = rep * local_width
-    local_weight = lax.dynamic_slice_in_dim(proj_weight, low, local_width, 1) * (
-        1.0 + lax.dynamic_slice_in_dim(mod_scale, low, local_width, 0)
-    )[None, :]
-
-    rows = tokens.reshape(-1, local_width)
-    shard_mean = jnp.mean(rows, axis=-1, keepdims=True)
-    centred = rows - shard_mean
-    shard_m2 = jnp.sum(centred * centred, axis=-1, keepdims=True)
-    projected = lax.dot_general(
-        centred,
-        local_weight,
-        (((1,), (1,)), ((), ())),
-        precision=lax.Precision.HIGHEST,
-        preferred_element_type=jnp.float32,
-    )
-    partial = jnp.concatenate([projected, shard_mean, shard_m2], axis=-1).reshape(
-        tok_frames, patch_rows, band_cols, out_width + 2
-    )
+    projected, shard_mean, shard_m2 = shard_moments(tokens, proj_weight, mod_scale, rep)
+    partial = jnp.concatenate([projected, shard_mean, shard_m2], axis=-1)
 
     slab = lat_rows // 2
     if patch_rows <= slab + 2:

time: 43 us -> 42.2 us (0.981)
  other arithmetic: 8.33 us -> 4.35 us
  Pallas kernels: 0 us -> 2.01 us
  local copies, waits for them, and re-layouts: 8.59 us -> 9.86 us
  matrix products: 6.05 us -> 4.84 us
  waiting for transfers between devices: 8.42 us -> 9.55 us
    pallas_call x0 -> x1, Pallas kernels: none -> 2.01 us  [shard_moments(): pl.pallas_call(shard_kernel, grid_spec=pltpu.PrefetchScalarGridSpec(num_s...]
    reduce_sum x2 -> x0, other arithmetic: 1.95 us -> none  [the longest x1 1.01 us: per_device(): shard_mean = jnp.mean(rows, axis=-1, keepdims=True)]
    unnamed x22 -> x23, local copies, waits for them, and re-layouts: 1.3 us -> 2.84 us
    dot_general x1 -> x0, matrix products: 1.21 us -> none  [per_device(): lax.dot_general(centred, local_weight, (((1,), (1,)), ((), ())), precisio...]
    all_to_all x1, waiting for transfers between devices: 3.97 us -> 5.1 us  [per_device(): lax.all_to_all(send, ALL, 0, 0, tiled=False).reshape(n_sec, n_sp, n_rep, -1)]
    mul x1, other arithmetic: 1.19 us -> 0.06 us  [per_device(): scaled_weight = proj_weight * (1.0 + mod_scale)[None, :]]
    sub x1 -> x0, other arithmetic: 0.85 us -> none  [per_device(): centred = rows - shard_mean]
    add x1 -> x0, other arithmetic: 0.77 us -> none  [per_device(): 1.0 + lax.dynamic_slice_in_dim(mod_scale, low, local_width, 0)]
  transfers between devices with their start and end apart: 2 -> 2, of which waited for: 2 -> 2; matrix products, arithmetic and copies ran while one was open for 9% -> 6% of each run, Pallas kernels for 0% -> 0%
where the time goes in v3:
time: 42.2 us; the launch traced here: 41.7 us
  starting transfers between devices  10.6 us (25%)
  local copies, waits for them, and re-layouts  9.86 us (23%)
  waiting for transfers between devices  9.55 us (23%)
  matrix products  4.84 us (11%)
  other arithmetic  4.35 us (10%)
  Pallas kernels  2.01 us (5%)
  between operations  0.5 us (1%)
    all_to_all x1, starting transfers between devices, per_device(): lax.all_to_all(send, ALL, 0, 0, tiled=False).reshape(n_sec, n_sp, n_rep, -1)  7.31 us
    all_to_all x1, waiting for transfers between devices, per_device(): lax.all_to_all(send, ALL, 0, 0, tiled=False).reshape(n_sec, n_sp, n_rep, -1)  5.1 us
    all_to_all x1, waiting for transfers between devices, per_device(): stats = lax.all_to_all(stats, BLOCKS, 0, 0, tiled=False)  4.45 us
    conv_general_dilated x2, matrix products, valid_conv(): lax.conv_general_dilated(front[None], kernel, (1, 1, 1), 'VALID', dimensi...  4.11 us
    all_to_all x1, starting transfers between devices, per_device(): stats = lax.all_to_all(stats, BLOCKS, 0, 0, tiled=False)  3.31 us
    unnamed x23, local copies, waits for them, and re-layouts  2.84 us
    pallas_call x1, Pallas kernels, shard_moments(): pl.pallas_call(shard_kernel, grid_spec=pltpu.PrefetchScalarGridSpec(num_s...  2.01 us
  transfers between devices with their start and end apart: 2, of which 2 were waited for; matrix products, arithmetic and copies ran while one was open for 6% of the time, Pallas kernels for 0%

profile of v3, /device:TPU:0, one launch (start us, length us, event | category | flops | bytes accessed | tf_op | source)
XLA Modules:
  0.0 41.7 jit_solution(7084743580664422724)
XLA Ops:
  0.0 0.9 %copy.46 = f32[2,2,12,16]{3,2,1,0:T(8,128)S(1)} copy(f32[2,2,12,16]{3,1,2,0:T(2,128)} %param.17) | data formatting | bytes 6144 | tf_op args[5]
  1.0 1.4 %copy.45.tok_ref = f32[1,2,6,768]{3,2,1,0:T(8,128)} copy(f32[1,2,6,768]{3,1,2,0:T(2,128)} %param.12) | data formatting | bytes 73728 | tf_op args[0]
  2.4 2.0 %shard_map.118 = (f32[1,2,6,64]{3,2,1,0:T(8,128)}, f32[1,2,6,1]{3,2,1,0:T(8,128)}, f32[1,2,6,1]{3,2,1,0:T(8,128)}) custom-call(s32[1]{0:T(128)} %bitcast.rep_ref, f32[1,2,6,768]{3,2,1,0:T(8,128)} %copy.45.tok_ref, f32[64,3072]{1,0:T(8,128)} %weight_ref.1, f32[1,3072]{1,0:T(1,128)} %bitcast.86), custom_call_target="tpu_custom_call" | custom-call | tf_op jit(solution)/shard_map/pallas_call | solution.py:53
  4.4 0.8 %pad_maximum_fusion.1 = f32[1,2,6,66]{3,2,1,0:T(8,128)S(1)} fusion(f32[1,2,6,1]{3,2,1,0:T(8,128)} %get-tuple-element.10, f32[1,2,6,1]{3,2,1,0:T(8,128)} %get-tuple-element.9, f32[1,2,6,64]{3,2,1,0:T(8,128)} %get-tuple-element.8), kind=kLoop, calls=%fused_computation.50 | loop fusion | flops 1584 | bytes 6336 | tf_op jit(solution)/shard_map/concatenate | solution.py:106
  5.4 0.7 %broadcast.253 = f32[32,1,984]{2,1,0:T(1,128)} broadcast(f32[984]{0:T(1024)S(1)} %pad_maximum_fusion.2), dimensions={2} | broadcast | bytes 129888 | tf_op jit(solution)/shard_map/all_to_all | solution.py:136
  6.1 7.3 %all-to-all-start = ((f32[32,1,984]{2,1,0:T(1,128)}), f32[32,1,984]{2,1,0:T(1,128)S(1)}, u32[]{:S(2)}, u32[]{:S(2)}) async-start(f32[32,1,984]{2,1,0:T(1,128)} %broadcast.253), calls=%async_computation | async-start | bytes 262144 | tf_op jit(solution)/shard_map/all_to_all | solution.py:136
  13.4 0.7 %broadcast_add_fusion = f32[3072]{0:T(1024)S(1)} fusion(f32[3072]{0:T(1024)} %param.13), kind=kLoop, calls=%fused_computation.51 | loop fusion | flops 3072 | bytes 24576 | tf_op jit(solution)/shard_map/add | solution.py:138
  14.2 0.7 %fusion.11 = f32[64]{0:T(128)S(1)} fusion(f32[64]{0:T(128)S(1)} %copy-done.5, f32[64,3072]{1,0:T(8,128)S(1)} %copy-done.1, f32[3072,1]{0,1:T(1,128)S(1)} %bitcast.87), kind=kOutput, calls=%fused_computation.11 | convolution fusion | flops 2359360 | bytes 799232 | tf_op jit(solution)/shard_map/dot_general | solution.py:141
  15.3 0.4 reshape.266
  15.7 0.2 reduce_sum.117
  16.0 5.1 %all-to-all-done = f32[32,1,984]{2,1,0:T(1,128)S(1)} async-done(((f32[32,1,984]{2,1,0:T(1,128)}), f32[32,1,984]{2,1,0:T(1,128)S(1)}, u32[]{:S(2)}, u32[]{:S(2)}) %all-to-all-start) | async-done | bytes 125984 | tf_op jit(solution)/shard_map/all_to_all | solution.py:136
  21.2 0.3 reduce.11
  21.6 0.2 reshape.265
  21.8 0.3 slice_reduce_fusion.3
  22.4 0.7 %copy.62 = f32[3,2,4,1,2,6,1]{2,5,4,1,0,6,3:T(8,128)S(1)} copy(f32[3,2,4,1,2,6,1]{6,5,4,2,1,0,3:T(8,128)S(1)} %slice_subtract_fusion) | data formatting | bytes 2304 | tf_op jit(solution)/shard_map/mul | solution.py:160
  23.3 0.2 multiply_reduce_fusion
  23.5 0.2 copy.50
  23.7 0.3 multiply_bitcast_fusion
  24.0 0.4 copy.51
  24.7 2.1 %convolution_select_fusion = f32[2,4,8,2,512]{4,2,3,1,0:T(8,128)S(1)} fusion(f32[3,3,3,16,512]{4,3,2,1,0:T(8,128)} %param.18, f32[4,6,1,7,2,16]{5,3,4,1,0,2:T(8,128)S(1)} %slice.66, f32[4,6,1,8,2,16]{5,3,4,1,0,2:T(8,128)S(1)} %copy.54, pred[8,2]{0,1:T(4,128)(4,1)S(1)} %copy-done.9), kind=kOutput, calls=%fused_computation.8 | convolution fusion | flops 169971712 | bytes 1192976 | tf_op jit(solution)/shard_map/conv_general_dilated | solution.py:18
  26.8 0.2 copy.55
  27.5 0.2 maximum_bitcast_fusion
  27.7 0.5 %copy.64 = bf16[4,6,1,26,512]{4,0,3,1,2:T(4,128)(2,1)S(1)} copy(bf16[4,6,1,26,512]{4,1,3,0,2:T(8,128)(2,1)S(1)} %maximum_bitcast_fusion) | data formatting | bytes 1277952
  28.3 0.3 pad.16.clone
  28.5 0.4 %copy.58 = bf16[4,6,1,8,4,512]{5,3,4,1,0,2:T(8,128)(2,1)S(1)} copy(bf16[4,6,1,8,4,512]{5,0,4,3,1,2:T(4,128)(2,1)S(1)} %bitcast.71) | data formatting | bytes 1572864 | tf_op jit(solution)/shard_map/conv_general_dilated | solution.py:18
  29.1 2.0 %select_reduce_fusion.1 = (f32[64]{0:T(128)S(1)}, f32[2,4,8,4,64]{4,2,3,1,0:T(8,128)S(1)}) fusion(f32[64]{0:T(128)S(1)} %copy-done.4, pred[8,4]{0,1:T(4,128)(4,1)S(1)} %copy-done.8, bf16[3,3,3,64,512]{4,3,2,1,0:T(8,128)(2,1)S(1)} %copy-done, bf16[4,6,1,7,2,512]{5,3,4,1,0,2:T(8,128)(2,1)S(1)} %slice.70, bf16[4,6,1,8,4,512]{5,3,4,1,0,2:T(8,128)(2,1)S(1)} %copy.58), kind=kOutput, calls=%fused_computation.38 | convolution fusion | flops 456589248 | bytes 2966048 | tf_op jit(solution)/shard_map/conv_general_dilated | solution.py:18
  31.5 0.1 select_reduce_fusion
  31.9 0.6 %broadcast_in_dim.84 = f32[8,1,16]{2,1,0:T(1,128)} broadcast(f32[16]{0:T(128)S(1)} %pad_maximum_fusion.3), dimensions={2} | broadcast | bytes 576 | tf_op jit(solution)/shard_map/broadcast_in_dim | solution.py:208
  32.5 3.3 %all-to-all-start.1 = ((f32[8,1,16]{2,1,0:T(1,128)}), f32[8,1,16]{2,1,0:T(1,128)S(1)}, u32[]{:S(2)}, u32[]{:S(2)}) async-start(f32[8,1,16]{2,1,0:T(1,128)} %broadcast_in_dim.84), calls=%async_computation.1 | async-start | bytes 8192 | tf_op jit(solution)/shard_map/all_to_all | solution.py:211
  35.9 4.4 %all-to-all-done.1 = f32[8,1,16]{2,1,0:T(1,128)S(1)} async-done(((f32[8,1,16]{2,1,0:T(1,128)}), f32[8,1,16]{2,1,0:T(1,128)S(1)}, u32[]{:S(2)}, u32[]{:S(2)}) %all-to-all-start.1) | async-done | bytes 544 | tf_op jit(solution)/shard_map/all_to_all | solution.py:211
  40.8 0.2 copy.60
  41.0 0.7 %copy.61 = f32[4,24,128]{2,1,0:T(8,128)} copy(f32[4,24,128]{1,2,0:T(8,128)S(1)} %bitcast.75) | data formatting | bytes 98304 | tf_op jit(solution)/shard_map/reshape | solution.py:224
  (78 shorter events, 3.4 us)
Async XLA Ops:
  0.0 29.1 %copy-start = (bf16[3,3,3,64,512]{4,3,2,1,0:T(8,128)(2,1)S(1)}, bf16[3,3,3,64,512]{4,3,2,1,0:T(8,128)(2,1)}, u32[]{:S(2)}) copy-start(bf16[3,3,3,64,512]{4,3,2,1,0:T(8,128)(2,1)} %param.20) | copy-start | bytes 5308420
  0.0 14.1 %copy-start.1 = (f32[64,3072]{1,0:T(8,128)S(1)}, f32[64,3072]{1,0:T(8,128)}, u32[]{:S(2)}) copy-start(f32[64,3072]{1,0:T(8,128)} %weight_ref.1) | copy-start | bytes 2359300
  0.0 14.2 %copy-start.5 = (f32[64]{0:T(128)S(1)}, f32[64]{0:T(128)}, u32[]{:S(2)}) copy-start(f32[64]{0:T(128)} %param.16) | copy-start | bytes 772
  0.0 14.2 %copy-start.2 = (f32[3072]{0:T(1024)S(1)}, f32[3072]{0:T(1024)}, u32[]{:S(2)}) copy-start(f32[3072]{0:T(1024)} %param.14) | copy-start | bytes 36868
  6.1 15.1 %all-to-all-start = ((f32[32,1,984]{2,1,0:T(1,128)}), f32[32,1,984]{2,1,0:T(1,128)S(1)}, u32[]{:S(2)}, u32[]{:S(2)}) async-start(f32[32,1,984]{2,1,0:T(1,128)} %broadcast.253), calls=%async_computation | async-start | bytes 262144 | tf_op jit(solution)/shard_map/all_to_all | solution.py:136
  23.7 1.0 %copy-start.9 = (pred[8,2]{0,1:T(4,128)(4,1)S(1)}, pred[8,2]{0,1:T(4,128)(4,1)}, u32[]{:S(2)}) copy-start(pred[8,2]{0,1:T(4,128)(4,1)} %constant.79) | copy-start | bytes 52
  24.7 2.3 %copy-start.3 = (f32[512]{0:T(512)S(1)}, f32[512]{0:T(512)}, u32[]{:S(2)}) copy-start(f32[512]{0:T(512)} %param.19) | copy-start | bytes 6148
  28.2 0.9 %copy-start.4 = (f32[64]{0:T(128)S(1)}, f32[64]{0:T(128)}, u32[]{:S(2)}) copy-start(f32[64]{0:T(128)} %param.21) | copy-start | bytes 772
  28.2 0.9 %copy-start.8 = (pred[8,4]{0,1:T(4,128)(4,1)S(1)}, pred[8,4]{0,1:T(4,128)(4,1)}, u32[]{:S(2)}) copy-start(pred[8,4]{0,1:T(4,128)(4,1)} %constant.78) | copy-start | bytes 100
  29.1 11.7 %copy-start.6 = (f32[64]{0:T(128)S(1)}, f32[64]{0:T(128)}, u32[]{:S(2)}) copy-start(f32[64]{0:T(128)} %param.23) | copy-start | bytes 772
  29.1 11.6 %copy-start.7 = (f32[64]{0:T(128)S(1)}, f32[64]{0:T(128)}, u32[]{:S(2)}) copy-start(f32[64]{0:T(128)} %param.22) | copy-start | bytes 772
  32.5 7.8 %all-to-all-start.1 = ((f32[8,1,16]{2,1,0:T(1,128)}), f32[8,1,16]{2,1,0:T(1,128)S(1)}, u32[]{:S(2)}, u32[]{:S(2)}) async-start(f32[8,1,16]{2,1,0:T(1,128)} %broadcast_in_dim.84), calls=%async_computation.1 | async-start | bytes 8192 | tf_op jit(solution)/shard_map/all_to_all | solution.py:211

commit v4 on v3

--- a/solution.py
+++ b/solution.py
@@ -30,8 +30,8 @@
 def shard_kernel(rep_ref, tok_ref, weight_ref, scale_ref, proj_ref, mean_ref, m2_ref):
     weight = weight_ref[...] * (1.0 + scale_ref[...])
     for frame in range(tok_ref.shape[0]):
-        for row in range(tok_ref.shape[1]):
-            x = tok_ref[frame, row]
+        for row in range(tok_ref.shape[2]):
+            x = tok_ref[frame, :, row, :]
             mean = jnp.mean(x, axis=1, keepdims=True)
             centred = x - mean
             proj_ref[frame, row] = lax.dot_general(
@@ -56,7 +56,7 @@
             num_scalar_prefetch=1,
             grid=(1,),
             in_specs=[
-                pl.BlockSpec(tokens.shape, whole),
+                pl.BlockSpec((tok_frames, band_cols, patch_rows, local_width), whole),
                 pl.BlockSpec((out_width, local_width), lambda i, r: (0, r[0])),
                 pl.BlockSpec((1, local_width), lambda i, r: (0, r[0])),
             ],
@@ -71,7 +71,12 @@
             jax.ShapeDtypeStruct(lead + (1,), jnp.float32),
             jax.ShapeDtypeStruct(lead + (1,), jnp.float32),
         ],
-    )(rep.reshape(1).astype(jnp.int32), tokens, proj_weight, mod_scale.reshape(1, -1))
+    )(
+        rep.reshape(1).astype(jnp.int32),
+        tokens.transpose(0, 2, 1, 3),
+        proj_weight,
+        mod_scale.reshape(1, -1),
+    )
 
 
 def neighbours(stack, index, axis):

time: 42.2 us -> 40.8 us (0.967)
  local copies, waits for them, and re-layouts: 9.86 us -> 8.32 us
    unnamed x23 -> x22, local copies, waits for them, and re-layouts: 2.84 us -> 1.3 us
where the time goes in v4:
time: 40.8 us; the launch traced here: 40.3 us
  starting transfers between devices  10.6 us (26%)
  waiting for transfers between devices  9.55 us (23%)
  local copies, waits for them, and re-layouts  8.32 us (20%)
  matrix products  4.84 us (12%)
  other arithmetic  4.36 us (11%)
  Pallas kernels  2.18 us (5%)
  between operations  0.49 us (1%)
    all_to_all x1, starting transfers between devices, per_device(): lax.all_to_all(send, ALL, 0, 0, tiled=False).reshape(n_sec, n_sp, n_rep, -1)  7.31 us
    all_to_all x1, waiting for transfers between devices, per_device(): lax.all_to_all(send, ALL, 0, 0, tiled=False).reshape(n_sec, n_sp, n_rep, -1)  5.1 us
    all_to_all x1, waiting for transfers between devices, per_device(): stats = lax.all_to_all(stats, BLOCKS, 0, 0, tiled=False)  4.45 us
    conv_general_dilated x2, matrix products, valid_conv(): lax.conv_general_dilated(front[None], kernel, (1, 1, 1), 'VALID', dimensi...  4.11 us
    all_to_all x1, starting transfers between devices, per_device(): stats = lax.all_to_all(stats, BLOCKS, 0, 0, tiled=False)  3.31 us
    pallas_call x1, Pallas kernels, shard_moments(): pl.pallas_call(shard_kernel, grid_spec=pltpu.PrefetchScalarGridSpec(num_s...  2.18 us
    unnamed x22, local copies, waits for them, and re-layouts  1.3 us
  transfers between devices with their start and end apart: 2, of which 2 were waited for; matrix products, arithmetic and copies ran while one was open for 6% of the time, Pallas kernels for 0%

profile of v4, /device:TPU:0, one launch (start us, length us, event | category | flops | bytes accessed | tf_op | source)
XLA Modules:
  0.0 40.3 jit_solution(9030770877698677065)
XLA Ops:
  0.0 2.2 %shard_map.118 = (f32[1,2,6,64]{3,2,1,0:T(8,128)}, f32[1,2,6,1]{3,2,1,0:T(8,128)}, f32[1,2,6,1]{3,2,1,0:T(8,128)}) custom-call(s32[1]{0:T(128)} %bitcast.rep_ref, f32[1,6,2,768]{3,2,1,0:T(2,128)} %bitcast.88, f32[64,3072]{1,0:T(8,128)} %weight_ref.1, f32[1,3072]{1,0:T(1,128)} %bitcast.87), custom_call_target="tpu_custom_call" | custom-call | tf_op jit(solution)/shard_map/pallas_call | solution.py:53
  2.2 0.8 %pad_maximum_fusion.1 = f32[1,2,6,66]{3,2,1,0:T(8,128)S(1)} fusion(f32[1,2,6,1]{3,2,1,0:T(8,128)} %get-tuple-element.10, f32[1,2,6,1]{3,2,1,0:T(8,128)} %get-tuple-element.9, f32[1,2,6,64]{3,2,1,0:T(8,128)} %get-tuple-element.8), kind=kLoop, calls=%fused_computation.50 | loop fusion | flops 1584 | bytes 6336 | tf_op jit(solution)/shard_map/concatenate | solution.py:111
  3.1 0.7 %copy.42 = f32[2,2,12,16]{3,2,1,0:T(8,128)S(1)} copy(f32[2,2,12,16]{3,1,2,0:T(2,128)} %param.17) | data formatting | bytes 6144 | tf_op args[5]
  4.0 0.7 %broadcast.253 = f32[32,1,984]{2,1,0:T(1,128)} broadcast(f32[984]{0:T(1024)S(1)} %pad_maximum_fusion.2), dimensions={2} | broadcast | bytes 129888 | tf_op jit(solution)/shard_map/all_to_all | solution.py:141
  4.7 7.3 %all-to-all-start = ((f32[32,1,984]{2,1,0:T(1,128)}), f32[32,1,984]{2,1,0:T(1,128)S(1)}, u32[]{:S(2)}, u32[]{:S(2)}) async-start(f32[32,1,984]{2,1,0:T(1,128)} %broadcast.253), calls=%async_computation | async-start | bytes 262144 | tf_op jit(solution)/shard_map/all_to_all | solution.py:141
  12.0 0.7 %broadcast_add_fusion = f32[3072]{0:T(1024)S(1)} fusion(f32[3072]{0:T(1024)} %param.13), kind=kLoop, calls=%fused_computation.51 | loop fusion | flops 3072 | bytes 24576 | tf_op jit(solution)/shard_map/add | solution.py:143
  12.9 0.7 %fusion.11 = f32[64]{0:T(128)S(1)} fusion(f32[64]{0:T(128)S(1)} %copy-done.5, f32[64,3072]{1,0:T(8,128)S(1)} %copy-done.1, f32[3072,1]{0,1:T(1,128)S(1)} %bitcast.89), kind=kOutput, calls=%fused_computation.11 | convolution fusion | flops 2359360 | bytes 799232 | tf_op jit(solution)/shard_map/dot_general | solution.py:146
  13.9 0.4 reshape.266
  14.3 0.2 reduce_sum.117
  14.7 5.1 %all-to-all-done = f32[32,1,984]{2,1,0:T(1,128)S(1)} async-done(((f32[32,1,984]{2,1,0:T(1,128)}), f32[32,1,984]{2,1,0:T(1,128)S(1)}, u32[]{:S(2)}, u32[]{:S(2)}) %all-to-all-start) | async-done | bytes 125984 | tf_op jit(solution)/shard_map/all_to_all | solution.py:141
  19.8 0.3 reduce.11
  20.3 0.2 reshape.265
  20.4 0.3 slice_reduce_fusion.3
  20.8 0.1 slice_subtract_fusion
  21.0 0.7 %copy.58 = f32[3,2,4,1,2,6,1]{2,5,4,1,0,6,3:T(8,128)S(1)} copy(f32[3,2,4,1,2,6,1]{6,5,4,2,1,0,3:T(8,128)S(1)} %slice_subtract_fusion) | data formatting | bytes 2304 | tf_op jit(solution)/shard_map/mul | solution.py:165
  21.9 0.2 multiply_reduce_fusion
  22.1 0.2 copy.46
  22.3 0.3 multiply_bitcast_fusion
  22.6 0.4 %copy.47 = f32[2,2,2,3,6,2,16]{6,2,1,5,4,3,0:T(2,128)S(1)} copy(f32[2,2,2,3,6,2,16]{4,5,2,6,1,0,3:T(2,128)S(1)} %multiply_bitcast_fusion) | data formatting | bytes 36864 | tf_op jit(solution)/shard_map/mul | solution.py:182
  23.3 2.1 %convolution_select_fusion = f32[2,4,8,2,512]{4,2,3,1,0:T(8,128)S(1)} fusion(f32[3,3,3,16,512]{4,3,2,1,0:T(8,128)} %param.18, f32[4,6,1,7,2,16]{5,3,4,1,0,2:T(8,128)S(1)} %slice.66, f32[4,6,1,8,2,16]{5,3,4,1,0,2:T(8,128)S(1)} %copy.50, pred[8,2]{0,1:T(4,128)(4,1)S(1)} %copy-done.9), kind=kOutput, calls=%fused_computation.8 | convolution fusion | flops 169971712 | bytes 1192976 | tf_op jit(solution)/shard_map/conv_general_dilated | solution.py:18
  25.4 0.2 copy.51
  26.1 0.2 maximum_bitcast_fusion
  26.3 0.5 %copy.60 = bf16[4,6,1,26,512]{4,0,3,1,2:T(4,128)(2,1)S(1)} copy(bf16[4,6,1,26,512]{4,1,3,0,2:T(8,128)(2,1)S(1)} %maximum_bitcast_fusion) | data formatting | bytes 1277952
  26.9 0.3 pad.16.clone
  27.2 0.4 %copy.54 = bf16[4,6,1,8,4,512]{5,3,4,1,0,2:T(8,128)(2,1)S(1)} copy(bf16[4,6,1,8,4,512]{5,0,4,3,1,2:T(4,128)(2,1)S(1)} %bitcast.72) | data formatting | bytes 1572864 | tf_op jit(solution)/shard_map/conv_general_dilated | solution.py:18
  27.8 2.0 %select_reduce_fusion.1 = (f32[64]{0:T(128)S(1)}, f32[2,4,8,4,64]{4,2,3,1,0:T(8,128)S(1)}) fusion(f32[64]{0:T(128)S(1)} %copy-done.4, pred[8,4]{0,1:T(4,128)(4,1)S(1)} %copy-done.8, bf16[3,3,3,64,512]{4,3,2,1,0:T(8,128)(2,1)S(1)} %copy-done, bf16[4,6,1,7,2,512]{5,3,4,1,0,2:T(8,128)(2,1)S(1)} %slice.70, bf16[4,6,1,8,4,512]{5,3,4,1,0,2:T(8,128)(2,1)S(1)} %copy.54), kind=kOutput, calls=%fused_computation.38 | convolution fusion | flops 456589248 | bytes 2966048 | tf_op jit(solution)/shard_map/conv_general_dilated | solution.py:18
  30.1 0.1 select_reduce_fusion
  30.5 0.6 %broadcast_in_dim.84 = f32[8,1,16]{2,1,0:T(1,128)} broadcast(f32[16]{0:T(128)S(1)} %pad_maximum_fusion.3), dimensions={2} | broadcast | bytes 576 | tf_op jit(solution)/shard_map/broadcast_in_dim | solution.py:213
  31.1 3.3 %all-to-all-start.1 = ((f32[8,1,16]{2,1,0:T(1,128)}), f32[8,1,16]{2,1,0:T(1,128)S(1)}, u32[]{:S(2)}, u32[]{:S(2)}) async-start(f32[8,1,16]{2,1,0:T(1,128)} %broadcast_in_dim.84), calls=%async_computation.1 | async-start | bytes 8192 | tf_op jit(solution)/shard_map/all_to_all | solution.py:216
  34.5 4.4 %all-to-all-done.1 = f32[8,1,16]{2,1,0:T(1,128)S(1)} async-done(((f32[8,1,16]{2,1,0:T(1,128)}), f32[8,1,16]{2,1,0:T(1,128)S(1)}, u32[]{:S(2)}, u32[]{:S(2)}) %all-to-all-start.1) | async-done | bytes 544 | tf_op jit(solution)/shard_map/all_to_all | solution.py:216
  39.5 0.2 copy.56
  39.6 0.7 %copy.57 = f32[4,24,128]{2,1,0:T(8,128)} copy(f32[4,24,128]{1,2,0:T(8,128)S(1)} %bitcast.76) | data formatting | bytes 98304 | tf_op jit(solution)/shard_map/reshape | solution.py:229
  (77 shorter events, 3.3 us)
Async XLA Ops:
  0.0 27.7 %copy-start = (bf16[3,3,3,64,512]{4,3,2,1,0:T(8,128)(2,1)S(1)}, bf16[3,3,3,64,512]{4,3,2,1,0:T(8,128)(2,1)}, u32[]{:S(2)}) copy-start(bf16[3,3,3,64,512]{4,3,2,1,0:T(8,128)(2,1)} %param.20) | copy-start | bytes 5308420
  0.0 12.8 %copy-start.1 = (f32[64,3072]{1,0:T(8,128)S(1)}, f32[64,3072]{1,0:T(8,128)}, u32[]{:S(2)}) copy-start(f32[64,3072]{1,0:T(8,128)} %weight_ref.1) | copy-start | bytes 2359300
  0.0 12.8 %copy-start.5 = (f32[64]{0:T(128)S(1)}, f32[64]{0:T(128)}, u32[]{:S(2)}) copy-start(f32[64]{0:T(128)} %param.16) | copy-start | bytes 772
  0.0 12.8 %copy-start.2 = (f32[3072]{0:T(1024)S(1)}, f32[3072]{0:T(1024)}, u32[]{:S(2)}) copy-start(f32[3072]{0:T(1024)} %param.14) | copy-start | bytes 36868
  4.7 15.1 %all-to-all-start = ((f32[32,1,984]{2,1,0:T(1,128)}), f32[32,1,984]{2,1,0:T(1,128)S(1)}, u32[]{:S(2)}, u32[]{:S(2)}) async-start(f32[32,1,984]{2,1,0:T(1,128)} %broadcast.253), calls=%async_computation | async-start | bytes 262144 | tf_op jit(solution)/shard_map/all_to_all | solution.py:141
  22.3 1.0 %copy-start.9 = (pred[8,2]{0,1:T(4,128)(4,1)S(1)}, pred[8,2]{0,1:T(4,128)(4,1)}, u32[]{:S(2)}) copy-start(pred[8,2]{0,1:T(4,128)(4,1)} %constant.79) | copy-start | bytes 52
  23.3 2.3 %copy-start.3 = (f32[512]{0:T(512)S(1)}, f32[512]{0:T(512)}, u32[]{:S(2)}) copy-start(f32[512]{0:T(512)} %param.19) | copy-start | bytes 6148
  26.8 0.9 %copy-start.4 = (f32[64]{0:T(128)S(1)}, f32[64]{0:T(128)}, u32[]{:S(2)}) copy-start(f32[64]{0:T(128)} %param.21) | copy-start | bytes 772
  26.9 0.9 %copy-start.8 = (pred[8,4]{0,1:T(4,128)(4,1)S(1)}, pred[8,4]{0,1:T(4,128)(4,1)}, u32[]{:S(2)}) copy-start(pred[8,4]{0,1:T(4,128)(4,1)} %constant.78) | copy-start | bytes 100
  27.7 11.7 %copy-start.6 = (f32[64]{0:T(128)S(1)}, f32[64]{0:T(128)}, u32[]{:S(2)}) copy-start(f32[64]{0:T(128)} %param.23) | copy-start | bytes 772
  27.7 11.6 %copy-start.7 = (f32[64]{0:T(128)S(1)}, f32[64]{0:T(128)}, u32[]{:S(2)}) copy-start(f32[64]{0:T(128)} %param.22) | copy-start | bytes 772
  31.1 7.8 %all-to-all-start.1 = ((f32[8,1,16]{2,1,0:T(1,128)}), f32[8,1,16]{2,1,0:T(1,128)S(1)}, u32[]{:S(2)}, u32[]{:S(2)}) async-start(f32[8,1,16]{2,1,0:T(1,128)} %broadcast_in_dim.84), calls=%async_computation.1 | async-start | bytes 8192 | tf_op jit(solution)/shard_map/all_to_all | solution.py:216

commit v5 on v4

--- a/solution.py
+++ b/solution.py
@@ -27,22 +27,25 @@
     return result[0]
 
 
-def shard_kernel(rep_ref, tok_ref, weight_ref, scale_ref, proj_ref, mean_ref, m2_ref):
+def shard_kernel(rep_ref, tok_ref, weight_ref, scale_ref, out_ref):
     weight = weight_ref[...] * (1.0 + scale_ref[...])
     for frame in range(tok_ref.shape[0]):
         for row in range(tok_ref.shape[2]):
             x = tok_ref[frame, :, row, :]
             mean = jnp.mean(x, axis=1, keepdims=True)
             centred = x - mean
-            proj_ref[frame, row] = lax.dot_general(
+            width = weight.shape[0]
+            out_ref[frame, row, :, :width] = lax.dot_general(
                 centred,
                 weight,
                 (((1,), (1,)), ((), ())),
                 precision=lax.Precision.HIGHEST,
                 preferred_element_type=jnp.float32,
             )
-            mean_ref[frame, row] = mean
-            m2_ref[frame, row] = jnp.sum(centred * centred, axis=1, keepdims=True)
+            out_ref[frame, row, :, width : width + 1] = mean
+            out_ref[frame, row, :, width + 1 : width + 2] = jnp.sum(
+                centred * centred, axis=1, keepdims=True
+            )
 
 
 def shard_moments(tokens, proj_weight, mod_scale, rep):
@@ -60,17 +63,9 @@
                 pl.BlockSpec((out_width, local_width), lambda i, r: (0, r[0])),
                 pl.BlockSpec((1, local_width), lambda i, r: (0, r[0])),
             ],
-            out_specs=[
-                pl.BlockSpec(lead + (out_width,), whole),
-                pl.BlockSpec(lead + (1,), whole),
-                pl.BlockSpec(lead + (1,), whole),
-            ],
+            out_specs=pl.BlockSpec(lead + (out_width + 2,), whole),
         ),
-        out_shape=[
-            jax.ShapeDtypeStruct(lead + (out_width,), jnp.float32),
-            jax.ShapeDtypeStruct(lead + (1,), jnp.float32),
-            jax.ShapeDtypeStruct(lead + (1,), jnp.float32),
-        ],
+        out_shape=jax.ShapeDtypeStruct(lead + (out_width + 2,), jnp.float32),
     )(
         rep.reshape(1).astype(jnp.int32),
         tokens.transpose(0, 2, 1, 3),
@@ -107,8 +102,7 @@
     full_width = local_width * n_rep
     out_width = proj_weight.shape[0]
 
-    projected, shard_mean, shard_m2 = shard_moments(tokens, proj_weight, mod_scale, rep)
-    partial = jnp.concatenate([projected, shard_mean, shard_m2], axis=-1)
+    partial = shard_moments(tokens, proj_weight, mod_scale, rep)
 
     slab = lat_rows // 2
     if patch_rows <= slab + 2:
@@ -121,15 +115,14 @@
     per_slab = per_slab.reshape(n_sp, -1)
     part_size = per_slab.shape[1]
 
-    frame_rows = frames * lat_rows
-    if frame_rows % n_rep == 0:
-        share = frame_rows // n_rep
-        latent_part = lax.dynamic_slice_in_dim(
-            noisy_latent.reshape(frame_rows, -1), rep * share, share, 0
-        ).reshape(-1)
+    lines = frames * lat_cols
+    stored = noisy_latent.transpose(0, 2, 1, 3).reshape(lines, lat_rows, LC)
+    if lines % n_rep == 0:
+        share = lines // n_rep
+        latent_part = lax.dynamic_slice_in_dim(stored, rep * share, share, 0).reshape(-1)
     else:
-        share = frame_rows
-        latent_part = noisy_latent.reshape(-1)
+        share = lines
+        latent_part = stored.reshape(-1)
 
     send = jnp.concatenate(
         [
@@ -172,9 +165,9 @@
     )
 
     shares = neighbours(received[..., part_size:], sec, 0)
-    if share == frame_rows:
+    if share == lines:
         shares = shares[:, :, 0]
-    latent = shares.reshape(3, n_sp, frames, lat_rows, lat_cols, LC)
+    latent = shares.reshape(3, n_sp, frames, lat_cols, lat_rows, LC).transpose(0, 1, 2, 4, 3, 5)
     if window == patch_rows:
         latent = latent.transpose(2, 1, 3, 0, 4, 5).reshape(
             frames, n_sp * lat_rows, 3 * lat_cols, LC

time: 40.8 us -> 40.6 us (level)
  local copies, waits for them, and re-layouts: 8.32 us -> 9.14 us
  other arithmetic: 4.36 us -> 3.55 us
    dynamic_slice x1, local copies, waits for them, and re-layouts: 0.01 us -> 0.85 us  [per_device(): lax.dynamic_slice_in_dim(stored, rep * share, share, 0).reshape(-1)]
    concatenate x1 -> x0, other arithmetic: 0.81 us -> none  [per_device(): partial = jnp.concatenate([projected, shard_mean, shard_m2], axis=-1)]
    unnamed x22 -> x21, local copies, waits for them, and re-layouts: 1.3 us -> 0.55 us
    broadcast_in_dim x1, local copies, waits for them, and re-layouts: 0.08 us -> 0.77 us  [per_device(): per_slab = jnp.broadcast_to(partial[None], (n_sp,) + partial.shape)]
where the time goes in v5:
time: 40.6 us; the launch traced here: 40.2 us
  starting transfers between devices  10.6 us (26%)
  waiting for transfers between devices  9.55 us (24%)
  local copies, waits for them, and re-layouts  9.14 us (23%)
  matrix products  4.84 us (12%)
  other arithmetic  3.55 us (9%)
  Pallas kernels  2.03 us (5%)
  between operations  0.49 us (1%)
    all_to_all x1, starting transfers between devices, per_device(): lax.all_to_all(send, ALL, 0, 0, tiled=False).reshape(n_sec, n_sp, n_rep, -1)  7.31 us
    all_to_all x1, waiting for transfers between devices, per_device(): lax.all_to_all(send, ALL, 0, 0, tiled=False).reshape(n_sec, n_sp, n_rep, -1)  5.1 us
    all_to_all x1, waiting for transfers between devices, per_device(): stats = lax.all_to_all(stats, BLOCKS, 0, 0, tiled=False)  4.45 us
    conv_general_dilated x2, matrix products, valid_conv(): lax.conv_general_dilated(front[None], kernel, (1, 1, 1), 'VALID', dimensi...  4.11 us
    all_to_all x1, starting transfers between devices, per_device(): stats = lax.all_to_all(stats, BLOCKS, 0, 0, tiled=False)  3.31 us
    pallas_call x1, Pallas kernels, shard_moments(): pl.pallas_call(shard_kernel, grid_spec=pltpu.PrefetchScalarGridSpec(num_s...  2.03 us
    dynamic_slice x1, local copies, waits for them, and re-layouts, per_device(): lax.dynamic_slice_in_dim(stored, rep * share, share, 0).reshape(-1)  0.85 us
  transfers between devices with their start and end apart: 2, of which 2 were waited for; matrix products, arithmetic and copies ran while one was open for 6% of the time, Pallas kernels for 0%

profile of v5, /device:TPU:0, one launch (start us, length us, event | category | flops | bytes accessed | tf_op | source)
XLA Modules:
  0.0 40.2 jit_solution(3470040772294766854)
XLA Ops:
  0.0 0.8 %constant_dynamic-slice_fusion = f32[6,2,16]{2,1,0:T(2,128)S(1)} fusion(f32[24,2,16]{2,1,0:T(2,128)} %bitcast.92, s32[]{:T(128)S(6)} %select_n.18), kind=kLoop, calls=%fused_computation.61 | loop fusion | bytes 1540 | tf_op jit(solution)/shard_map/dynamic_slice | solution.py:122
  1.0 2.0 %shard_map.118 = f32[1,2,6,66]{3,2,1,0:T(8,128)} custom-call(s32[1]{0:T(128)} %bitcast.rep_ref, f32[1,6,2,768]{3,2,1,0:T(2,128)} %bitcast.90, f32[64,3072]{1,0:T(8,128)} %weight_ref.1, f32[1,3072]{1,0:T(1,128)} %bitcast.89), custom_call_target="tpu_custom_call" | custom-call | tf_op jit(solution)/shard_map/pallas_call | solution.py:56
  3.0 0.8 %reshape.305 = f32[792]{0:T(1024)S(1)} reshape(f32[1,2,6,66]{3,2,1,0:T(8,128)} %shard_map.118) | data formatting | bytes 6336 | tf_op jit(solution)/shard_map/broadcast_in_dim | solution.py:110
  3.8 0.7 %broadcast.253 = f32[32,1,984]{2,1,0:T(1,128)} broadcast(f32[984]{0:T(1024)S(1)} %pad_maximum_fusion.1), dimensions={2} | broadcast | bytes 129888 | tf_op jit(solution)/shard_map/all_to_all | solution.py:134
  4.5 7.3 %all-to-all-start = ((f32[32,1,984]{2,1,0:T(1,128)}), f32[32,1,984]{2,1,0:T(1,128)S(1)}, u32[]{:S(2)}, u32[]{:S(2)}) async-start(f32[32,1,984]{2,1,0:T(1,128)} %broadcast.253), calls=%async_computation | async-start | bytes 262144 | tf_op jit(solution)/shard_map/all_to_all | solution.py:134
  11.9 0.7 %broadcast_add_fusion = f32[3072]{0:T(1024)S(1)} fusion(f32[3072]{0:T(1024)} %param.13), kind=kLoop, calls=%fused_computation.50 | loop fusion | flops 3072 | bytes 24576 | tf_op jit(solution)/shard_map/add | solution.py:136
  12.7 0.7 %fusion.11 = f32[64]{0:T(128)S(1)} fusion(f32[64]{0:T(128)S(1)} %copy-done.5, f32[64,3072]{1,0:T(8,128)S(1)} %copy-done.1, f32[3072,1]{0,1:T(1,128)S(1)} %bitcast.91), kind=kOutput, calls=%fused_computation.11 | convolution fusion | flops 2359360 | bytes 799232 | tf_op jit(solution)/shard_map/dot_general | solution.py:139
  13.8 0.4 reshape.266
  14.2 0.2 reduce_sum.117
  14.5 5.1 %all-to-all-done = f32[32,1,984]{2,1,0:T(1,128)S(1)} async-done(((f32[32,1,984]{2,1,0:T(1,128)}), f32[32,1,984]{2,1,0:T(1,128)S(1)}, u32[]{:S(2)}, u32[]{:S(2)}) %all-to-all-start) | async-done | bytes 125984 | tf_op jit(solution)/shard_map/all_to_all | solution.py:134
  19.6 0.3 reduce.11
  20.1 0.2 reshape.265
  20.3 0.3 slice_reduce_fusion.3
  20.8 0.7 %copy.55 = f32[3,2,4,1,2,6,1]{2,5,4,1,0,6,3:T(8,128)S(1)} copy(f32[3,2,4,1,2,6,1]{6,5,4,2,1,0,3:T(8,128)S(1)} %slice_subtract_fusion) | data formatting | bytes 2304 | tf_op jit(solution)/shard_map/mul | solution.py:158
  21.5 0.2 reshape.263
  21.7 0.2 multiply_reduce_fusion
  21.9 0.2 copy.43
  22.2 0.3 multiply_bitcast_fusion
  22.4 0.4 %copy.44 = f32[2,2,2,3,6,2,16]{6,2,1,5,4,3,0:T(2,128)S(1)} copy(f32[2,2,2,3,6,2,16]{4,5,2,6,1,0,3:T(2,128)S(1)} %multiply_bitcast_fusion) | data formatting | bytes 36864 | tf_op jit(solution)/shard_map/mul | solution.py:175
  23.2 2.1 %convolution_select_fusion = f32[2,4,8,2,512]{4,2,3,1,0:T(8,128)S(1)} fusion(f32[3,3,3,16,512]{4,3,2,1,0:T(8,128)} %param.18, f32[4,6,1,7,2,16]{5,3,4,1,0,2:T(8,128)S(1)} %slice.66, f32[4,6,1,8,2,16]{5,3,4,1,0,2:T(8,128)S(1)} %copy.47, pred[8,2]{0,1:T(4,128)(4,1)S(1)} %copy-done.9), kind=kOutput, calls=%fused_computation.8 | convolution fusion | flops 169971712 | bytes 1192976 | tf_op jit(solution)/shard_map/conv_general_dilated | solution.py:18
  25.3 0.2 copy.48
  26.0 0.2 maximum_bitcast_fusion
  26.2 0.5 %copy.57 = bf16[4,6,1,26,512]{4,0,3,1,2:T(4,128)(2,1)S(1)} copy(bf16[4,6,1,26,512]{4,1,3,0,2:T(8,128)(2,1)S(1)} %maximum_bitcast_fusion) | data formatting | bytes 1277952
  26.7 0.3 pad.16.clone
  27.0 0.4 %copy.51 = bf16[4,6,1,8,4,512]{5,3,4,1,0,2:T(8,128)(2,1)S(1)} copy(bf16[4,6,1,8,4,512]{5,0,4,3,1,2:T(4,128)(2,1)S(1)} %bitcast.74) | data formatting | bytes 1572864 | tf_op jit(solution)/shard_map/conv_general_dilated | solution.py:18
  27.6 2.0 %select_reduce_fusion.1 = (f32[64]{0:T(128)S(1)}, f32[2,4,8,4,64]{4,2,3,1,0:T(8,128)S(1)}) fusion(f32[64]{0:T(128)S(1)} %copy-done.4, pred[8,4]{0,1:T(4,128)(4,1)S(1)} %copy-done.8, bf16[3,3,3,64,512]{4,3,2,1,0:T(8,128)(2,1)S(1)} %copy-done, bf16[4,6,1,7,2,512]{5,3,4,1,0,2:T(8,128)(2,1)S(1)} %slice.70, bf16[4,6,1,8,4,512]{5,3,4,1,0,2:T(8,128)(2,1)S(1)} %copy.51), kind=kOutput, calls=%fused_computation.38 | convolution fusion | flops 456589248 | bytes 2966048 | tf_op jit(solution)/shard_map/conv_general_dilated | solution.py:18
  30.0 0.1 select_reduce_fusion
  30.4 0.6 %broadcast_in_dim.84 = f32[8,1,16]{2,1,0:T(1,128)} broadcast(f32[16]{0:T(128)S(1)} %pad_maximum_fusion.2), dimensions={2} | broadcast | bytes 576 | tf_op jit(solution)/shard_map/broadcast_in_dim | solution.py:206
  31.0 3.3 %all-to-all-start.1 = ((f32[8,1,16]{2,1,0:T(1,128)}), f32[8,1,16]{2,1,0:T(1,128)S(1)}, u32[]{:S(2)}, u32[]{:S(2)}) async-start(f32[8,1,16]{2,1,0:T(1,128)} %broadcast_in_dim.84), calls=%async_computation.1 | async-start | bytes 8192 | tf_op jit(solution)/shard_map/all_to_all | solution.py:209
  34.4 4.4 %all-to-all-done.1 = f32[8,1,16]{2,1,0:T(1,128)S(1)} async-done(((f32[8,1,16]{2,1,0:T(1,128)}), f32[8,1,16]{2,1,0:T(1,128)S(1)}, u32[]{:S(2)}, u32[]{:S(2)}) %all-to-all-start.1) | async-done | bytes 544 | tf_op jit(solution)/shard_map/all_to_all | solution.py:209
  39.3 0.2 copy.53
  39.5 0.7 %copy.54 = f32[4,24,128]{2,1,0:T(8,128)} copy(f32[4,24,128]{1,2,0:T(8,128)S(1)} %bitcast.78) | data formatting | bytes 98304 | tf_op jit(solution)/shard_map/reshape | solution.py:222
  (75 shorter events, 3.2 us)
Async XLA Ops:
  0.0 27.6 %copy-start = (bf16[3,3,3,64,512]{4,3,2,1,0:T(8,128)(2,1)S(1)}, bf16[3,3,3,64,512]{4,3,2,1,0:T(8,128)(2,1)}, u32[]{:S(2)}) copy-start(bf16[3,3,3,64,512]{4,3,2,1,0:T(8,128)(2,1)} %param.20) | copy-start | bytes 5308420
  0.0 12.6 %copy-start.1 = (f32[64,3072]{1,0:T(8,128)S(1)}, f32[64,3072]{1,0:T(8,128)}, u32[]{:S(2)}) copy-start(f32[64,3072]{1,0:T(8,128)} %weight_ref.1) | copy-start | bytes 2359300
  0.0 12.7 %copy-start.5 = (f32[64]{0:T(128)S(1)}, f32[64]{0:T(128)}, u32[]{:S(2)}) copy-start(f32[64]{0:T(128)} %param.16) | copy-start | bytes 772
  0.0 12.7 %copy-start.2 = (f32[3072]{0:T(1024)S(1)}, f32[3072]{0:T(1024)}, u32[]{:S(2)}) copy-start(f32[3072]{0:T(1024)} %param.14) | copy-start | bytes 36868
  4.5 15.1 %all-to-all-start = ((f32[32,1,984]{2,1,0:T(1,128)}), f32[32,1,984]{2,1,0:T(1,128)S(1)}, u32[]{:S(2)}, u32[]{:S(2)}) async-start(f32[32,1,984]{2,1,0:T(1,128)} %broadcast.253), calls=%async_computation | async-start | bytes 262144 | tf_op jit(solution)/shard_map/all_to_all | solution.py:134
  22.2 1.0 %copy-start.9 = (pred[8,2]{0,1:T(4,128)(4,1)S(1)}, pred[8,2]{0,1:T(4,128)(4,1)}, u32[]{:S(2)}) copy-start(pred[8,2]{0,1:T(4,128)(4,1)} %constant.80) | copy-start | bytes 52
  23.2 2.3 %copy-start.3 = (f32[512]{0:T(512)S(1)}, f32[512]{0:T(512)}, u32[]{:S(2)}) copy-start(f32[512]{0:T(512)} %param.19) | copy-start | bytes 6148
  26.7 0.9 %copy-start.4 = (f32[64]{0:T(128)S(1)}, f32[64]{0:T(128)}, u32[]{:S(2)}) copy-start(f32[64]{0:T(128)} %param.21) | copy-start | bytes 772
  26.7 0.9 %copy-start.8 = (pred[8,4]{0,1:T(4,128)(4,1)S(1)}, pred[8,4]{0,1:T(4,128)(4,1)}, u32[]{:S(2)}) copy-start(pred[8,4]{0,1:T(4,128)(4,1)} %constant.79) | copy-start | bytes 100
  27.6 11.7 %copy-start.6 = (f32[64]{0:T(128)S(1)}, f32[64]{0:T(128)}, u32[]{:S(2)}) copy-start(f32[64]{0:T(128)} %param.23) | copy-start | bytes 772
  27.6 11.6 %copy-start.7 = (f32[64]{0:T(128)S(1)}, f32[64]{0:T(128)}, u32[]{:S(2)}) copy-start(f32[64]{0:T(128)} %param.22) | copy-start | bytes 772
  31.0 7.8 %all-to-all-start.1 = ((f32[8,1,16]{2,1,0:T(1,128)}), f32[8,1,16]{2,1,0:T(1,128)S(1)}, u32[]{:S(2)}, u32[]{:S(2)}) async-start(f32[8,1,16]{2,1,0:T(1,128)} %broadcast_in_dim.84), calls=%async_computation.1 | async-start | bytes 8192 | tf_op jit(solution)/shard_map/all_to_all | solution.py:209

commit v6 on v5

--- a/solution.py
+++ b/solution.py
@@ -154,8 +154,12 @@
         offsets * offsets, axis=2
     )
     token_var = m2 / full_width
-    centred_proj = jnp.sum(parts[..., :out_width], axis=2) + jnp.sum(
-        offsets[..., None] * shard_columns.reshape(1, 1, n_rep, 1, 1, 1, out_width), axis=2
+    centred_proj = jnp.sum(parts[..., :out_width], axis=2) + lax.dot_general(
+        offsets,
+        shard_columns,
+        (((2,), (0,)), ((), ())),
+        precision=lax.Precision.HIGHEST,
+        preferred_element_type=jnp.float32,
     )
     velocity = lax.rsqrt(token_var + 1e-06)[..., None] * centred_proj + shift_column
     patches = (
@@ -189,7 +193,26 @@
     col_inside = (col_global >= 0) & (col_global < lat_cols * n_sec)
     clean = jnp.where(row_inside[None, :, None, None] & col_inside[None, None, :, None], clean, 0.0)
 
-    inner_features = valid_conv(clean, in_weight, "DHWIO", lax.Precision.HIGH) + in_bias
+    front = jnp.concatenate([clean[:1], clean[:1], clean], axis=0)
+    taps = jnp.concatenate(
+        [
+            front[dt : dt + frames, dy : dy + lat_rows + 2, dx : dx + lat_cols + 2]
+            for dt in range(3)
+            for dy in range(3)
+            for dx in range(3)
+        ],
+        axis=-1,
+    )
+    inner_features = (
+        lax.dot_general(
+            taps,
+            in_weight.reshape(-1, in_weight.shape[-1]),
+            (((3,), (0,)), ((), ())),
+            precision=lax.Precision.HIGH,
+            preferred_element_type=jnp.float32,
+        )
+        + in_bias
+    )
     inside = row_inside[None, 1:-1, None, None] & col_inside[None, None, 1:-1, None]
     features = jnp.where(inside, inner_features, 0.0).astype(jnp.bfloat16)
     upsampled = jnp.repeat(jnp.repeat(features, 2, axis=1), 2, axis=2)[:, 1:-1, 1:-1, :]

time: 40.6 us -> 40.8 us (level)
  waiting for transfers between devices: 9.55 us -> 7.77 us
  other arithmetic: 3.55 us -> 4.96 us
  local copies, waits for them, and re-layouts: 9.14 us -> 9.92 us
    conv_general_dilated x2 -> x1, matrix products: 4.11 us -> 2 us  [valid_conv(): lax.conv_general_dilated(front[None], kernel, (1, 1, 1), 'VALID', dimensi...]
    dot_general x0 -> x2, matrix products: none -> 1.87 us  [the longest x1 1.6 us: per_device(): lax.dot_general(taps, in_weight.reshape(-1, in_weight.shape[-1]), (((3,),...]
    all_to_all x1, waiting for transfers between devices: 5.1 us -> 3.32 us  [per_device(): lax.all_to_all(send, ALL, 0, 0, tiled=False).reshape(n_sec, n_sp, n_rep, -1)]
    reshape x1, local copies, waits for them, and re-layouts: 0.39 us -> 1.51 us  [per_device(): scaled_weight.reshape(out_width, n_rep, local_width)]
    unnamed x0 -> x18, other arithmetic: none -> 1.06 us
    mul x1, other arithmetic: 0.06 us -> 0.94 us  [per_device(): scaled_weight = proj_weight * (1.0 + mod_scale)[None, :]]
    mul x1 -> x0, local copies, waits for them, and re-layouts: 0.68 us -> none  [per_device(): offsets[..., None] * shard_columns.reshape(1, 1, n_rep, 1, 1, 1, out_width)]
    unnamed x21 -> x29, local copies, waits for them, and re-layouts: 0.55 us -> 0.99 us
  transfers between devices with their start and end apart: 2 -> 2, of which waited for: 2 -> 2; matrix products, arithmetic and copies ran while one was open for 6% -> 11% of each run, Pallas kernels for 0% -> 0%
where the time goes in v6:
time: 40.8 us; the launch traced here: 40.4 us
  starting transfers between devices  10.6 us (26%)
  local copies, waits for them, and re-layouts  9.92 us (24%)
  waiting for transfers between devices  7.77 us (19%)
  other arithmetic  4.96 us (12%)
  matrix products  4.6 us (11%)
  Pallas kernels  2.03 us (5%)
  between operations  0.47 us (1%)
    all_to_all x1, starting transfers between devices, per_device(): lax.all_to_all(send, ALL, 0, 0, tiled=False).reshape(n_sec, n_sp, n_rep, -1)  7.3 us
    all_to_all x1, waiting for transfers between devices, per_device(): stats = lax.all_to_all(stats, BLOCKS, 0, 0, tiled=False)  4.45 us
    all_to_all x1, waiting for transfers between devices, per_device(): lax.all_to_all(send, ALL, 0, 0, tiled=False).reshape(n_sec, n_sp, n_rep, -1)  3.32 us
    all_to_all x1, starting transfers between devices, per_device(): stats = lax.all_to_all(stats, BLOCKS, 0, 0, tiled=False)  3.31 us
    pallas_call x1, Pallas kernels, shard_moments(): pl.pallas_call(shard_kernel, grid_spec=pltpu.PrefetchScalarGridSpec(num_s...  2.03 us
    conv_general_dilated x1, matrix products, valid_conv(): lax.conv_general_dilated(front[None], kernel, (1, 1, 1), 'VALID', dimensi...  2 us
    dot_general x1, matrix products, per_device(): lax.dot_general(taps, in_weight.reshape(-1, in_weight.shape[-1]), (((3,),...  1.6 us
    reshape x1, local copies, waits for them, and re-layouts, per_device(): scaled_weight.reshape(out_width, n_rep, local_width)  1.51 us
  transfers between devices with their start and end apart: 2, of which 2 were waited for; matrix products, arithmetic and copies ran while one was open for 11% of the time, Pallas kernels for 0%

profile of v6, /device:TPU:0, one launch (start us, length us, event | category | flops | bytes accessed | tf_op | source)
XLA Modules:
  0.0 40.4 jit_solution(2092602713254316050)
XLA Ops:
  0.0 0.8 %constant_dynamic-slice_fusion = f32[6,2,16]{2,1,0:T(2,128)S(1)} fusion(f32[24,2,16]{2,1,0:T(2,128)} %bitcast.83, s32[]{:T(128)S(6)} %select_n.18), kind=kLoop, calls=%fused_computation.132 | loop fusion | bytes 1540 | tf_op jit(solution)/shard_map/dynamic_slice | solution.py:122
  0.9 2.0 %shard_map.118 = f32[1,2,6,66]{3,2,1,0:T(8,128)} custom-call(s32[1]{0:T(128)} %bitcast.rep_ref, f32[1,6,2,768]{3,2,1,0:T(2,128)} %bitcast.81, f32[64,3072]{1,0:T(8,128)} %weight_ref.1, f32[1,3072]{1,0:T(1,128)} %bitcast.80), custom_call_target="tpu_custom_call" | custom-call | tf_op jit(solution)/shard_map/pallas_call | solution.py:56
  3.0 0.8 %reshape.282 = f32[792]{0:T(1024)S(1)} reshape(f32[1,2,6,66]{3,2,1,0:T(8,128)} %shard_map.118) | data formatting | bytes 6336 | tf_op jit(solution)/shard_map/broadcast_in_dim | solution.py:110
  3.8 0.7 %broadcast.232 = f32[32,1,984]{2,1,0:T(1,128)} broadcast(f32[984]{0:T(1024)S(1)} %pad_maximum_fusion.2), dimensions={2} | broadcast | bytes 129888 | tf_op jit(solution)/shard_map/all_to_all | solution.py:134
  4.5 7.3 %all-to-all-start = ((f32[32,1,984]{2,1,0:T(1,128)}), f32[32,1,984]{2,1,0:T(1,128)S(1)}, u32[]{:S(2)}, u32[]{:S(2)}) async-start(f32[32,1,984]{2,1,0:T(1,128)} %broadcast.232), calls=%async_computation | async-start | bytes 262144 | tf_op jit(solution)/shard_map/all_to_all | solution.py:134
  11.9 0.7 %broadcast_add_fusion = f32[3072]{0:T(1024)S(1)} fusion(f32[3072]{0:T(1024)} %param.13), kind=kLoop, calls=%fused_computation.121 | loop fusion | flops 3072 | bytes 24576 | tf_op jit(solution)/shard_map/add | solution.py:136
  12.8 0.9 %broadcast_multiply_fusion = f32[64,3072]{1,0:T(8,128)} fusion(f32[64,3072]{1,0:T(8,128)S(1)} %copy-done.1, f32[3072]{0:T(1024)S(1)} %broadcast_add_fusion), kind=kLoop, calls=%fused_computation.25 | loop fusion | flops 196608 | bytes 1585152 | tf_op jit(solution)/shard_map/mul | solution.py:136
  13.8 1.5 %reshape.254 = f32[64,4,768]{2,1,0:T(4,128)S(1)} reshape(f32[64,3072]{1,0:T(8,128)} %broadcast_multiply_fusion) | data formatting | bytes 1572864 | tf_op jit(solution)/shard_map/reshape | solution.py:137
  15.3 0.2 reduce_sum.108
  15.5 0.7 %fusion.14 = f32[64]{0:T(128)S(1)} fusion(f32[64]{0:T(128)S(1)} %copy-done.6, f32[64,3072]{1,0:T(8,128)S(1)} %copy-done.1, f32[3072,1]{0,1:T(1,128)S(1)} %bitcast.82), kind=kOutput, calls=%fused_computation.14 | convolution fusion | flops 2359360 | bytes 799232 | tf_op jit(solution)/shard_map/dot_general | solution.py:139
  16.3 3.3 %all-to-all-done = f32[32,1,984]{2,1,0:T(1,128)S(1)} async-done(((f32[32,1,984]{2,1,0:T(1,128)}), f32[32,1,984]{2,1,0:T(1,128)S(1)}, u32[]{:S(2)}, u32[]{:S(2)}) %all-to-all-start) | async-done | bytes 125984 | tf_op jit(solution)/shard_map/all_to_all | solution.py:134
  19.6 0.3 reduce.10
  20.0 0.2 reshape.253
  20.2 0.3 slice_reduce_fusion.1
  20.7 0.3 fusion.13
  21.0 0.2 copy.114
  21.2 0.4 %copy.115 = f32[2,2,2,3,6,2,16]{6,2,1,5,4,3,0:T(2,128)S(1)} copy(f32[2,2,2,3,6,2,16]{4,5,2,6,1,0,3:T(2,128)S(1)} %bitcast.71) | data formatting | bytes 36864 | tf_op jit(solution)/shard_map/mul | solution.py:179
  21.6 0.1 copy.117
  21.8 0.2 reshape.251
  23.9 1.6 %fusion.65 = f32[2,4,14,512]{3,2,1,0:T(8,128)S(1)} fusion(f32[2,4,14,432]{2,3,1,0:T(8,128)S(1)} %slice_dynamic-update-slice_fusion, f32[432,512,1,1]{1,0,3,2:T(8,128)S(1)} %bitcast.73), kind=kOutput, calls=%fused_computation.140 | convolution fusion | flops 148635648 | bytes 1307648 | tf_op jit(solution)/shard_map/dot_general | solution.py:207
  25.5 0.2 fusion.17
  26.2 0.2 maximum_bitcast_fusion
  26.4 0.5 %copy.131 = bf16[4,6,1,26,512]{4,0,3,1,2:T(4,128)(2,1)S(1)} copy(bf16[4,6,1,26,512]{4,1,3,0,2:T(8,128)(2,1)S(1)} %maximum_bitcast_fusion) | data formatting | bytes 1277952
  26.9 0.3 pad.15.clone
  27.2 0.4 %copy.122 = bf16[4,6,1,8,4,512]{5,3,4,1,0,2:T(8,128)(2,1)S(1)} copy(bf16[4,6,1,8,4,512]{5,0,4,3,1,2:T(4,128)(2,1)S(1)} %bitcast.68) | data formatting | bytes 1572864 | tf_op jit(solution)/shard_map/conv_general_dilated | solution.py:18
  27.8 2.0 %select_reduce_fusion.1 = (f32[64]{0:T(128)S(1)}, f32[2,4,8,4,64]{4,2,3,1,0:T(8,128)S(1)}) fusion(f32[64]{0:T(128)S(1)} %copy-done.5, pred[8,4]{0,1:T(4,128)(4,1)S(1)} %copy-done.9, bf16[3,3,3,64,512]{4,3,2,1,0:T(8,128)(2,1)S(1)} %copy-done, bf16[4,6,1,7,2,512]{5,3,4,1,0,2:T(8,128)(2,1)S(1)} %slice.233, bf16[4,6,1,8,4,512]{5,3,4,1,0,2:T(8,128)(2,1)S(1)} %copy.122), kind=kOutput, calls=%fused_computation.59 | convolution fusion | flops 456589248 | bytes 2966048 | tf_op jit(solution)/shard_map/conv_general_dilated | solution.py:18
  30.1 0.1 select_reduce_fusion
  30.5 0.6 %broadcast_in_dim.79 = f32[8,1,16]{2,1,0:T(1,128)} broadcast(f32[16]{0:T(128)S(1)} %pad_maximum_fusion.3), dimensions={2} | broadcast | bytes 576 | tf_op jit(solution)/shard_map/broadcast_in_dim | solution.py:229
  31.2 3.3 %all-to-all-start.1 = ((f32[8,1,16]{2,1,0:T(1,128)}), f32[8,1,16]{2,1,0:T(1,128)S(1)}, u32[]{:S(2)}, u32[]{:S(2)}) async-start(f32[8,1,16]{2,1,0:T(1,128)} %broadcast_in_dim.79), calls=%async_computation.1 | async-start | bytes 8192 | tf_op jit(solution)/shard_map/all_to_all | solution.py:232
  34.5 4.4 %all-to-all-done.1 = f32[8,1,16]{2,1,0:T(1,128)S(1)} async-done(((f32[8,1,16]{2,1,0:T(1,128)}), f32[8,1,16]{2,1,0:T(1,128)S(1)}, u32[]{:S(2)}, u32[]{:S(2)}) %all-to-all-start.1) | async-done | bytes 544 | tf_op jit(solution)/shard_map/all_to_all | solution.py:232
  39.5 0.2 copy.124
  39.6 0.7 %copy.125 = f32[4,24,128]{2,1,0:T(8,128)} copy(f32[4,24,128]{1,2,0:T(8,128)S(1)} %bitcast.72) | data formatting | bytes 98304 | tf_op jit(solution)/shard_map/reshape | solution.py:245
  (94 shorter events, 4.3 us)
Async XLA Ops:
  0.0 27.7 %copy-start = (bf16[3,3,3,64,512]{4,3,2,1,0:T(8,128)(2,1)S(1)}, bf16[3,3,3,64,512]{4,3,2,1,0:T(8,128)(2,1)}, u32[]{:S(2)}) copy-start(bf16[3,3,3,64,512]{4,3,2,1,0:T(8,128)(2,1)} %param.20) | copy-start | bytes 5308420
  0.0 12.8 %copy-start.1 = (f32[64,3072]{1,0:T(8,128)S(1)}, f32[64,3072]{1,0:T(8,128)}, u32[]{:S(2)}) copy-start(f32[64,3072]{1,0:T(8,128)} %weight_ref.1) | copy-start | bytes 2359300
  4.5 15.0 %all-to-all-start = ((f32[32,1,984]{2,1,0:T(1,128)}), f32[32,1,984]{2,1,0:T(1,128)S(1)}, u32[]{:S(2)}, u32[]{:S(2)}) async-start(f32[32,1,984]{2,1,0:T(1,128)} %broadcast.232), calls=%async_computation | async-start | bytes 262144 | tf_op jit(solution)/shard_map/all_to_all | solution.py:134
  12.8 2.7 %copy-start.3 = (f32[3072]{0:T(1024)S(1)}, f32[3072]{0:T(1024)}, u32[]{:S(2)}) copy-start(f32[3072]{0:T(1024)} %param.14) | copy-start | bytes 36868
  12.8 2.7 %copy-start.6 = (f32[64]{0:T(128)S(1)}, f32[64]{0:T(128)}, u32[]{:S(2)}) copy-start(f32[64]{0:T(128)} %param.16) | copy-start | bytes 772
  22.5 1.4 %copy-start.2 = (f32[3,3,3,16,512]{4,3,2,1,0:T(8,128)S(1)}, f32[3,3,3,16,512]{4,3,2,1,0:T(8,128)}, u32[]{:S(2)}) copy-start(f32[3,3,3,16,512]{4,3,2,1,0:T(8,128)} %param.18) | copy-start | bytes 2654212
  23.6 2.0 %copy-start.4 = (f32[512]{0:T(512)S(1)}, f32[512]{0:T(512)}, u32[]{:S(2)}) copy-start(f32[512]{0:T(512)} %param.19) | copy-start | bytes 6148
  26.9 0.9 %copy-start.5 = (f32[64]{0:T(128)S(1)}, f32[64]{0:T(128)}, u32[]{:S(2)}) copy-start(f32[64]{0:T(128)} %param.21) | copy-start | bytes 772
  26.9 0.9 %copy-start.9 = (pred[8,4]{0,1:T(4,128)(4,1)S(1)}, pred[8,4]{0,1:T(4,128)(4,1)}, u32[]{:S(2)}) copy-start(pred[8,4]{0,1:T(4,128)(4,1)} %constant.76) | copy-start | bytes 100
  27.7 11.7 %copy-start.7 = (f32[64]{0:T(128)S(1)}, f32[64]{0:T(128)}, u32[]{:S(2)}) copy-start(f32[64]{0:T(128)} %param.23) | copy-start | bytes 772
  27.8 11.6 %copy-start.8 = (f32[64]{0:T(128)S(1)}, f32[64]{0:T(128)}, u32[]{:S(2)}) copy-start(f32[64]{0:T(128)} %param.22) | copy-start | bytes 772
  31.2 7.8 %all-to-all-start.1 = ((f32[8,1,16]{2,1,0:T(1,128)}), f32[8,1,16]{2,1,0:T(1,128)S(1)}, u32[]{:S(2)}, u32[]{:S(2)}) async-start(f32[8,1,16]{2,1,0:T(1,128)} %broadcast_in_dim.79), calls=%async_computation.1 | async-start | bytes 8192 | tf_op jit(solution)/shard_map/all_to_all | solution.py:232

commit v7 on v5

--- a/solution.py
+++ b/solution.py
@@ -154,8 +154,12 @@
         offsets * offsets, axis=2
     )
     token_var = m2 / full_width
-    centred_proj = jnp.sum(parts[..., :out_width], axis=2) + jnp.sum(
-        offsets[..., None] * shard_columns.reshape(1, 1, n_rep, 1, 1, 1, out_width), axis=2
+    centred_proj = jnp.sum(parts[..., :out_width], axis=2) + lax.dot_general(
+        offsets,
+        shard_columns,
+        (((2,), (0,)), ((), ())),
+        precision=lax.Precision.HIGHEST,
+        preferred_element_type=jnp.float32,
     )
     velocity = lax.rsqrt(token_var + 1e-06)[..., None] * centred_proj + shift_column
     patches = (

time: 40.6 us -> 38.7 us (0.953)
  waiting for transfers between devices: 9.55 us -> 7.76 us
  matrix products: 4.84 us -> 3.97 us
  local copies, waits for them, and re-layouts: 9.14 us -> 9.59 us
    all_to_all x1, waiting for transfers between devices: 5.1 us -> 3.31 us  [per_device(): lax.all_to_all(send, ALL, 0, 0, tiled=False).reshape(n_sec, n_sp, n_rep, -1)]
    conv_general_dilated x2, matrix products: 4.11 us -> 2.96 us  [valid_conv(): lax.conv_general_dilated(front[None], kernel, (1, 1, 1), 'VALID', dimensi...]
    reshape x1, local copies, waits for them, and re-layouts: 0.39 us -> 1.51 us  [per_device(): scaled_weight.reshape(out_width, n_rep, local_width)]
    mul x1, other arithmetic: 0.06 us -> 0.94 us  [per_device(): scaled_weight = proj_weight * (1.0 + mod_scale)[None, :]]
    mul x1 -> x0, local copies, waits for them, and re-layouts: 0.68 us -> none  [per_device(): offsets[..., None] * shard_columns.reshape(1, 1, n_rep, 1, 1, 1, out_width)]
  transfers between devices with their start and end apart: 2 -> 2, of which waited for: 2 -> 2; matrix products, arithmetic and copies ran while one was open for 6% -> 12% of each run, Pallas kernels for 0% -> 0%
where the time goes in v7:
time: 38.7 us; the launch traced here: 38.3 us
  starting transfers between devices  10.6 us (27%)
  local copies, waits for them, and re-layouts  9.59 us (25%)
  waiting for transfers between devices  7.76 us (20%)
  matrix products  3.97 us (10%)
  other arithmetic  3.89 us (10%)
  Pallas kernels  2.03 us (5%)
  between operations  0.43 us (1%)
    all_to_all x1, starting transfers between devices, per_device(): lax.all_to_all(send, ALL, 0, 0, tiled=False).reshape(n_sec, n_sp, n_rep, -1)  7.3 us
    all_to_all x1, waiting for transfers between devices, per_device(): stats = lax.all_to_all(stats, BLOCKS, 0, 0, tiled=False)  4.45 us
    all_to_all x1, waiting for transfers between devices, per_device(): lax.all_to_all(send, ALL, 0, 0, tiled=False).reshape(n_sec, n_sp, n_rep, -1)  3.31 us
    all_to_all x1, starting transfers between devices, per_device(): stats = lax.all_to_all(stats, BLOCKS, 0, 0, tiled=False)  3.31 us
    conv_general_dilated x2, matrix products, valid_conv(): lax.conv_general_dilated(front[None], kernel, (1, 1, 1), 'VALID', dimensi...  2.96 us
    pallas_call x1, Pallas kernels, shard_moments(): pl.pallas_call(shard_kernel, grid_spec=pltpu.PrefetchScalarGridSpec(num_s...  2.03 us
    reshape x1, local copies, waits for them, and re-layouts, per_device(): scaled_weight.reshape(out_width, n_rep, local_width)  1.51 us
    mul x1, other arithmetic, per_device(): scaled_weight = proj_weight * (1.0 + mod_scale)[None, :]  0.94 us
  transfers between devices with their start and end apart: 2, of which 2 were waited for; matrix products, arithmetic and copies ran while one was open for 12% of the time, Pallas kernels for 0%

profile of v7, /device:TPU:0, one launch (start us, length us, event | category | flops | bytes accessed | tf_op | source)
XLA Modules:
  0.0 38.3 jit_solution(11115319621304877645)
XLA Ops:
  0.0 0.8 %constant_dynamic-slice_fusion = f32[6,2,16]{2,1,0:T(2,128)S(1)} fusion(f32[24,2,16]{2,1,0:T(2,128)} %bitcast.91, s32[]{:T(128)S(6)} %select_n.18), kind=kLoop, calls=%fused_computation.65 | loop fusion | bytes 1540 | tf_op jit(solution)/shard_map/dynamic_slice | solution.py:122
  0.9 2.0 %shard_map.118 = f32[1,2,6,66]{3,2,1,0:T(8,128)} custom-call(s32[1]{0:T(128)} %bitcast.rep_ref, f32[1,6,2,768]{3,2,1,0:T(2,128)} %bitcast.89, f32[64,3072]{1,0:T(8,128)} %weight_ref.1, f32[1,3072]{1,0:T(1,128)} %bitcast.88), custom_call_target="tpu_custom_call" | custom-call | tf_op jit(solution)/shard_map/pallas_call | solution.py:56
  3.0 0.8 %reshape.292 = f32[792]{0:T(1024)S(1)} reshape(f32[1,2,6,66]{3,2,1,0:T(8,128)} %shard_map.118) | data formatting | bytes 6336 | tf_op jit(solution)/shard_map/broadcast_in_dim | solution.py:110
  3.8 0.7 %broadcast.234 = f32[32,1,984]{2,1,0:T(1,128)} broadcast(f32[984]{0:T(1024)S(1)} %pad_maximum_fusion.1), dimensions={2} | broadcast | bytes 129888 | tf_op jit(solution)/shard_map/all_to_all | solution.py:134
  4.5 7.3 %all-to-all-start = ((f32[32,1,984]{2,1,0:T(1,128)}), f32[32,1,984]{2,1,0:T(1,128)S(1)}, u32[]{:S(2)}, u32[]{:S(2)}) async-start(f32[32,1,984]{2,1,0:T(1,128)} %broadcast.234), calls=%async_computation | async-start | bytes 262144 | tf_op jit(solution)/shard_map/all_to_all | solution.py:134
  11.9 0.7 %broadcast_add_fusion = f32[3072]{0:T(1024)S(1)} fusion(f32[3072]{0:T(1024)} %param.13), kind=kLoop, calls=%fused_computation.54 | loop fusion | flops 3072 | bytes 24576 | tf_op jit(solution)/shard_map/add | solution.py:136
  12.8 0.9 %broadcast_multiply_fusion = f32[64,3072]{1,0:T(8,128)} fusion(f32[64,3072]{1,0:T(8,128)S(1)} %copy-done.1, f32[3072]{0:T(1024)S(1)} %broadcast_add_fusion), kind=kLoop, calls=%fused_computation.23 | loop fusion | flops 196608 | bytes 1585152 | tf_op jit(solution)/shard_map/mul | solution.py:136
  13.8 1.5 %reshape.251 = f32[64,4,768]{2,1,0:T(4,128)S(1)} reshape(f32[64,3072]{1,0:T(8,128)} %broadcast_multiply_fusion) | data formatting | bytes 1572864 | tf_op jit(solution)/shard_map/reshape | solution.py:137
  15.3 0.2 reduce_sum.108
  15.5 0.7 %fusion.14 = f32[64]{0:T(128)S(1)} fusion(f32[64]{0:T(128)S(1)} %copy-done.5, f32[64,3072]{1,0:T(8,128)S(1)} %copy-done.1, f32[3072,1]{0,1:T(1,128)S(1)} %bitcast.90), kind=kOutput, calls=%fused_computation.15 | convolution fusion | flops 2359360 | bytes 799232 | tf_op jit(solution)/shard_map/dot_general | solution.py:139
  16.3 3.3 %all-to-all-done = f32[32,1,984]{2,1,0:T(1,128)S(1)} async-done(((f32[32,1,984]{2,1,0:T(1,128)}), f32[32,1,984]{2,1,0:T(1,128)S(1)}, u32[]{:S(2)}, u32[]{:S(2)}) %all-to-all-start) | async-done | bytes 125984 | tf_op jit(solution)/shard_map/all_to_all | solution.py:134
  19.6 0.3 reduce.10
  20.0 0.2 reshape.250
  20.2 0.3 slice_reduce_fusion.1
  20.7 0.3 fusion.13
  21.0 0.2 copy.44
  21.2 0.4 %copy.45 = f32[2,2,2,3,6,2,16]{6,2,1,5,4,3,0:T(2,128)S(1)} copy(f32[2,2,2,3,6,2,16]{4,5,2,6,1,0,3:T(2,128)S(1)} %bitcast.78) | data formatting | bytes 36864 | tf_op jit(solution)/shard_map/mul | solution.py:179
  21.7 0.2 reshape.248
  22.2 0.2 copy-done.9
  22.4 1.0 %convolution_select_fusion = f32[2,4,8,2,512]{4,2,3,1,0:T(8,128)S(1)} fusion(f32[3,3,3,16,512]{4,3,2,1,0:T(8,128)S(1)} %copy-done.9, f32[4,6,1,7,2,16]{5,3,4,1,0,2:T(8,128)S(1)} %slice.66, f32[4,6,1,8,2,16]{5,3,4,1,0,2:T(8,128)S(1)} %copy.48, pred[8,2]{0,1:T(4,128)(4,1)S(1)} %copy-done.10), kind=kOutput, calls=%fused_computation.8 | convolution fusion | flops 169971712 | bytes 1192976 | tf_op jit(solution)/shard_map/conv_general_dilated | solution.py:18
  23.3 0.2 copy.49
  24.1 0.2 maximum_bitcast_fusion
  24.3 0.5 %copy.59 = bf16[4,6,1,26,512]{4,0,3,1,2:T(4,128)(2,1)S(1)} copy(bf16[4,6,1,26,512]{4,1,3,0,2:T(8,128)(2,1)S(1)} %maximum_bitcast_fusion) | data formatting | bytes 1277952
  24.8 0.3 pad.16.clone
  25.1 0.4 %copy.52 = bf16[4,6,1,8,4,512]{5,3,4,1,0,2:T(8,128)(2,1)S(1)} copy(bf16[4,6,1,8,4,512]{5,0,4,3,1,2:T(4,128)(2,1)S(1)} %bitcast.75) | data formatting | bytes 1572864 | tf_op jit(solution)/shard_map/conv_general_dilated | solution.py:18
  25.7 2.0 %select_reduce_fusion.1 = (f32[64]{0:T(128)S(1)}, f32[2,4,8,4,64]{4,2,3,1,0:T(8,128)S(1)}) fusion(f32[64]{0:T(128)S(1)} %copy-done.4, pred[8,4]{0,1:T(4,128)(4,1)S(1)} %copy-done.8, bf16[3,3,3,64,512]{4,3,2,1,0:T(8,128)(2,1)S(1)} %copy-done, bf16[4,6,1,7,2,512]{5,3,4,1,0,2:T(8,128)(2,1)S(1)} %slice.70, bf16[4,6,1,8,4,512]{5,3,4,1,0,2:T(8,128)(2,1)S(1)} %copy.52), kind=kOutput, calls=%fused_computation.39 | convolution fusion | flops 456589248 | bytes 2966048 | tf_op jit(solution)/shard_map/conv_general_dilated | solution.py:18
  28.1 0.1 select_reduce_fusion
  28.5 0.6 %broadcast_in_dim.83 = f32[8,1,16]{2,1,0:T(1,128)} broadcast(f32[16]{0:T(128)S(1)} %pad_maximum_fusion.2), dimensions={2} | broadcast | bytes 576 | tf_op jit(solution)/shard_map/broadcast_in_dim | solution.py:210
  29.1 3.3 %all-to-all-start.1 = ((f32[8,1,16]{2,1,0:T(1,128)}), f32[8,1,16]{2,1,0:T(1,128)S(1)}, u32[]{:S(2)}, u32[]{:S(2)}) async-start(f32[8,1,16]{2,1,0:T(1,128)} %broadcast_in_dim.83), calls=%async_computation.1 | async-start | bytes 8192 | tf_op jit(solution)/shard_map/all_to_all | solution.py:213
  32.4 4.4 %all-to-all-done.1 = f32[8,1,16]{2,1,0:T(1,128)S(1)} async-done(((f32[8,1,16]{2,1,0:T(1,128)}), f32[8,1,16]{2,1,0:T(1,128)S(1)}, u32[]{:S(2)}, u32[]{:S(2)}) %all-to-all-start.1) | async-done | bytes 544 | tf_op jit(solution)/shard_map/all_to_all | solution.py:213
  37.4 0.2 copy.54
  37.5 0.7 %copy.55 = f32[4,24,128]{2,1,0:T(8,128)} copy(f32[4,24,128]{1,2,0:T(8,128)S(1)} %bitcast.79) | data formatting | bytes 98304 | tf_op jit(solution)/shard_map/reshape | solution.py:226
  (72 shorter events, 2.8 us)
Async XLA Ops:
  0.0 25.6 %copy-start = (bf16[3,3,3,64,512]{4,3,2,1,0:T(8,128)(2,1)S(1)}, bf16[3,3,3,64,512]{4,3,2,1,0:T(8,128)(2,1)}, u32[]{:S(2)}) copy-start(bf16[3,3,3,64,512]{4,3,2,1,0:T(8,128)(2,1)} %param.20) | copy-start | bytes 5308420
  0.0 12.8 %copy-start.1 = (f32[64,3072]{1,0:T(8,128)S(1)}, f32[64,3072]{1,0:T(8,128)}, u32[]{:S(2)}) copy-start(f32[64,3072]{1,0:T(8,128)} %weight_ref.1) | copy-start | bytes 2359300
  4.5 15.0 %all-to-all-start = ((f32[32,1,984]{2,1,0:T(1,128)}), f32[32,1,984]{2,1,0:T(1,128)S(1)}, u32[]{:S(2)}, u32[]{:S(2)}) async-start(f32[32,1,984]{2,1,0:T(1,128)} %broadcast.234), calls=%async_computation | async-start | bytes 262144 | tf_op jit(solution)/shard_map/all_to_all | solution.py:134
  12.8 2.7 %copy-start.2 = (f32[3072]{0:T(1024)S(1)}, f32[3072]{0:T(1024)}, u32[]{:S(2)}) copy-start(f32[3072]{0:T(1024)} %param.14) | copy-start | bytes 36868
  12.8 2.7 %copy-start.5 = (f32[64]{0:T(128)S(1)}, f32[64]{0:T(128)}, u32[]{:S(2)}) copy-start(f32[64]{0:T(128)} %param.16) | copy-start | bytes 772
  21.2 1.2 %copy-start.9 = (f32[3,3,3,16,512]{4,3,2,1,0:T(8,128)S(1)}, f32[3,3,3,16,512]{4,3,2,1,0:T(8,128)}, u32[]{:S(2)}) copy-start(f32[3,3,3,16,512]{4,3,2,1,0:T(8,128)} %param.18) | copy-start | bytes 2654212
  21.2 1.2 %copy-start.10 = (pred[8,2]{0,1:T(4,128)(4,1)S(1)}, pred[8,2]{0,1:T(4,128)(4,1)}, u32[]{:S(2)}) copy-start(pred[8,2]{0,1:T(4,128)(4,1)} %constant.80) | copy-start | bytes 52
  22.4 1.2 %copy-start.3 = (f32[512]{0:T(512)S(1)}, f32[512]{0:T(512)}, u32[]{:S(2)}) copy-start(f32[512]{0:T(512)} %param.19) | copy-start | bytes 6148
  24.8 0.9 %copy-start.4 = (f32[64]{0:T(128)S(1)}, f32[64]{0:T(128)}, u32[]{:S(2)}) copy-start(f32[64]{0:T(128)} %param.21) | copy-start | bytes 772
  24.8 0.9 %copy-start.8 = (pred[8,4]{0,1:T(4,128)(4,1)S(1)}, pred[8,4]{0,1:T(4,128)(4,1)}, u32[]{:S(2)}) copy-start(pred[8,4]{0,1:T(4,128)(4,1)} %constant.79) | copy-start | bytes 100
  25.7 11.7 %copy-start.6 = (f32[64]{0:T(128)S(1)}, f32[64]{0:T(128)}, u32[]{:S(2)}) copy-start(f32[64]{0:T(128)} %param.23) | copy-start | bytes 772
  25.7 11.6 %copy-start.7 = (f32[64]{0:T(128)S(1)}, f32[64]{0:T(128)}, u32[]{:S(2)}) copy-start(f32[64]{0:T(128)} %param.22) | copy-start | bytes 772
  29.1 7.8 %all-to-all-start.1 = ((f32[8,1,16]{2,1,0:T(1,128)}), f32[8,1,16]{2,1,0:T(1,128)S(1)}, u32[]{:S(2)}, u32[]{:S(2)}) async-start(f32[8,1,16]{2,1,0:T(1,128)} %broadcast_in_dim.83), calls=%async_computation.1 | async-start | bytes 8192 | tf_op jit(solution)/shard_map/all_to_all | solution.py:213

commit v8 on v7

--- a/solution.py
+++ b/solution.py
@@ -13,8 +13,11 @@
 BLOCKS = ("section", "sp")
 
 
-def valid_conv(volume, kernel, kernel_spec, precision_mode):
-    front = jnp.concatenate([volume[:1], volume[:1], volume], axis=0)
+def causal_front(volume):
+    return jnp.concatenate([volume[:1], volume[:1], volume], axis=0)
+
+
+def valid_conv(front, kernel, kernel_spec, precision_mode):
     result = lax.conv_general_dilated(
         front[None],
         kernel,
@@ -27,7 +30,8 @@
     return result[0]
 
 
-def shard_kernel(rep_ref, tok_ref, weight_ref, scale_ref, out_ref):
+def shard_kernel(rep_ref, tok_ref, weight_ref, scale_ref, latent_ref, out_ref, share_ref):
+    share_ref[...] = latent_ref[...]
     weight = weight_ref[...] * (1.0 + scale_ref[...])
     for frame in range(tok_ref.shape[0]):
         for row in range(tok_ref.shape[2]):
@@ -48,10 +52,11 @@
             )
 
 
-def shard_moments(tokens, proj_weight, mod_scale, rep):
+def shard_moments(tokens, proj_weight, mod_scale, latent_lines, share, rep):
     tok_frames, patch_rows, band_cols, local_width = tokens.shape
     out_width = proj_weight.shape[0]
     whole = lambda i, r: (0, 0, 0, 0)
+    whole3 = lambda i, r: (0, 0, 0)
     lead = (tok_frames, patch_rows, band_cols)
     return pl.pallas_call(
         shard_kernel,
@@ -62,15 +67,26 @@
                 pl.BlockSpec((tok_frames, band_cols, patch_rows, local_width), whole),
                 pl.BlockSpec((out_width, local_width), lambda i, r: (0, r[0])),
                 pl.BlockSpec((1, local_width), lambda i, r: (0, r[0])),
+                pl.BlockSpec(
+                    (share,) + latent_lines.shape[1:],
+                    (lambda i, r: (r[0], 0, 0)) if share < latent_lines.shape[0] else whole3,
+                ),
             ],
-            out_specs=pl.BlockSpec(lead + (out_width + 2,), whole),
+            out_specs=[
+                pl.BlockSpec(lead + (out_width + 2,), whole),
+                pl.BlockSpec((share,) + latent_lines.shape[1:], whole3),
+            ],
         ),
-        out_shape=jax.ShapeDtypeStruct(lead + (out_width + 2,), jnp.float32),
+        out_shape=[
+            jax.ShapeDtypeStruct(lead + (out_width + 2,), jnp.float32),
+            jax.ShapeDtypeStruct((share,) + latent_lines.shape[1:], jnp.float32),
+        ],
     )(
         rep.reshape(1).astype(jnp.int32),
         tokens.transpose(0, 2, 1, 3),
         proj_weight,
         mod_scale.reshape(1, -1),
+        latent_lines,
     )
 
 
@@ -102,7 +118,14 @@
     full_width = local_width * n_rep
     out_width = proj_weight.shape[0]
 
-    partial = shard_moments(tokens, proj_weight, mod_scale, rep)
+
+    lines = frames * lat_cols
+    stored = noisy_latent.transpose(0, 2, 1, 3).reshape(lines, lat_rows, LC)
+    share = lines // n_rep if lines % n_rep == 0 else lines
+    partial, latent_part = shard_moments(
+        tokens, proj_weight, mod_scale, stored, share, rep
+    )
+    latent_part = latent_part.reshape(-1)
 
     slab = lat_rows // 2
     if patch_rows <= slab + 2:
@@ -114,15 +137,6 @@
         per_slab = jnp.stack([padded[:, p * slab : p * slab + window] for p in range(n_sp)])
     per_slab = per_slab.reshape(n_sp, -1)
     part_size = per_slab.shape[1]
-
-    lines = frames * lat_cols
-    stored = noisy_latent.transpose(0, 2, 1, 3).reshape(lines, lat_rows, LC)
-    if lines % n_rep == 0:
-        share = lines // n_rep
-        latent_part = lax.dynamic_slice_in_dim(stored, rep * share, share, 0).reshape(-1)
-    else:
-        share = lines
-        latent_part = stored.reshape(-1)
 
     send = jnp.concatenate(
         [
@@ -193,9 +207,9 @@
     col_inside = (col_global >= 0) & (col_global < lat_cols * n_sec)
     clean = jnp.where(row_inside[None, :, None, None] & col_inside[None, None, :, None], clean, 0.0)
 
-    inner_features = valid_conv(clean, in_weight, "DHWIO", lax.Precision.HIGH) + in_bias
+    inner_features = valid_conv(causal_front(clean), in_weight, "DHWIO", lax.Precision.HIGH) + in_bias
     inside = row_inside[None, 1:-1, None, None] & col_inside[None, None, 1:-1, None]
-    features = jnp.where(inside, inner_features, 0.0).astype(jnp.bfloat16)
+    features = causal_front(jnp.where(inside, inner_features, 0.0).astype(jnp.bfloat16))
     upsampled = jnp.repeat(jnp.repeat(features, 2, axis=1), 2, axis=2)[:, 1:-1, 1:-1, :]
     mixed = valid_conv(upsampled, conv_weight, "DHWOI", None) + conv_bias
 

time: 38.7 us -> 39 us (level)
    dynamic_slice x1 -> x0, local copies, waits for them, and re-layouts: 0.84 us -> none  [per_device(): lax.dynamic_slice_in_dim(stored, rep * share, share, 0).reshape(-1)]
    reshape x1, local copies, waits for them, and re-layouts: 0.09 us -> 0.78 us  [per_device(): latent_part = latent_part.reshape(-1)]
  transfers between devices with their start and end apart: 2 -> 2, of which waited for: 2 -> 2; matrix products, arithmetic and copies ran while one was open for 12% -> 11% of each run, Pallas kernels for 0% -> 0%
where the time goes in v8:
time: 39 us; the launch traced here: 38.6 us
  starting transfers between devices  10.6 us (27%)
  local copies, waits for them, and re-layouts  9.8 us (25%)
  waiting for transfers between devices  7.77 us (20%)
  matrix products  3.96 us (10%)
  other arithmetic  3.82 us (10%)
  Pallas kernels  2.18 us (6%)
  between operations  0.43 us (1%)
    all_to_all x1, starting transfers between devices, per_device(): lax.all_to_all(send, ALL, 0, 0, tiled=False).reshape(n_sec, n_sp, n_rep, -1)  7.3 us
    all_to_all x1, waiting for transfers between devices, per_device(): stats = lax.all_to_all(stats, BLOCKS, 0, 0, tiled=False)  4.45 us
    all_to_all x1, waiting for transfers between devices, per_device(): lax.all_to_all(send, ALL, 0, 0, tiled=False).reshape(n_sec, n_sp, n_rep, -1)  3.32 us
    all_to_all x1, starting transfers between devices, per_device(): stats = lax.all_to_all(stats, BLOCKS, 0, 0, tiled=False)  3.31 us
    conv_general_dilated x2, matrix products, valid_conv(): lax.conv_general_dilated(front[None], kernel, (1, 1, 1), 'VALID', dimensi...  2.96 us
    pallas_call x1, Pallas kernels, shard_moments(): pl.pallas_call(shard_kernel, grid_spec=pltpu.PrefetchScalarGridSpec(num_s...  2.18 us
    reshape x1, local copies, waits for them, and re-layouts, per_device(): scaled_weight.reshape(out_width, n_rep, local_width)  1.51 us
    mul x1, other arithmetic, per_device(): scaled_weight = proj_weight * (1.0 + mod_scale)[None, :]  0.94 us
  transfers between devices with their start and end apart: 2, of which 2 were waited for; matrix products, arithmetic and copies ran while one was open for 11% of the time, Pallas kernels for 0%

profile of v8, /device:TPU:0, one launch (start us, length us, event | category | flops | bytes accessed | tf_op | source)
XLA Modules:
  0.0 38.6 jit_solution(16736594303803536334)
XLA Ops:
  0.0 2.2 %shard_map.118 = (f32[1,2,6,66]{3,2,1,0:T(8,128)}, f32[6,2,16]{2,1,0:T(2,128)}) custom-call(s32[1]{0:T(128)} %bitcast.rep_ref, f32[1,6,2,768]{3,2,1,0:T(2,128)} %bitcast.88, f32[64,3072]{1,0:T(8,128)} %weight_ref.1, f32[1,3072]{1,0:T(1,128)} %bitcast.87, f32[24,2,16]{2,1,0:T(2,128)} %bitcast.89), custom_call_target="tpu_custom_call" | custom-call | tf_op jit(solution)/shard_map/pallas_call | solution.py:61
  2.2 0.8 %reshape.292 = f32[792]{0:T(1024)S(1)} reshape(f32[1,2,6,66]{3,2,1,0:T(8,128)} %get-tuple-element.7) | data formatting | bytes 6336 | tf_op jit(solution)/shard_map/broadcast_in_dim | solution.py:133
  3.0 0.8 %reshape.293 = f32[192]{0:T(256)S(1)} reshape(f32[6,2,16]{2,1,0:T(2,128)} %get-tuple-element.8) | data formatting | bytes 1536 | tf_op jit(solution)/shard_map/reshape | solution.py:128
  3.8 0.7 %broadcast.234 = f32[32,1,984]{2,1,0:T(1,128)} broadcast(f32[984]{0:T(1024)S(1)} %pad_maximum_fusion.2), dimensions={2} | broadcast | bytes 129888 | tf_op jit(solution)/shard_map/all_to_all | solution.py:148
  4.5 7.3 %all-to-all-start = ((f32[32,1,984]{2,1,0:T(1,128)}), f32[32,1,984]{2,1,0:T(1,128)S(1)}, u32[]{:S(2)}, u32[]{:S(2)}) async-start(f32[32,1,984]{2,1,0:T(1,128)} %broadcast.234), calls=%async_computation | async-start | bytes 262144 | tf_op jit(solution)/shard_map/all_to_all | solution.py:148
  11.8 0.7 %broadcast_add_fusion = f32[3072]{0:T(1024)S(1)} fusion(f32[3072]{0:T(1024)} %param.13), kind=kLoop, calls=%fused_computation.55 | loop fusion | flops 3072 | bytes 24576 | tf_op jit(solution)/shard_map/add | solution.py:150
  12.8 0.9 %broadcast_multiply_fusion = f32[64,3072]{1,0:T(8,128)} fusion(f32[64,3072]{1,0:T(8,128)S(1)} %copy-done.1, f32[3072]{0:T(1024)S(1)} %broadcast_add_fusion), kind=kLoop, calls=%fused_computation.23 | loop fusion | flops 196608 | bytes 1585152 | tf_op jit(solution)/shard_map/mul | solution.py:150
  13.8 1.5 %reshape.251 = f32[64,4,768]{2,1,0:T(4,128)S(1)} reshape(f32[64,3072]{1,0:T(8,128)} %broadcast_multiply_fusion) | data formatting | bytes 1572864 | tf_op jit(solution)/shard_map/reshape | solution.py:151
  15.3 0.2 reduce_sum.108
  15.5 0.7 %fusion.14 = f32[64]{0:T(128)S(1)} fusion(f32[64]{0:T(128)S(1)} %copy-done.5, f32[64,3072]{1,0:T(8,128)S(1)} %copy-done.1, f32[3072,1]{0,1:T(1,128)S(1)} %bitcast.90), kind=kOutput, calls=%fused_computation.15 | convolution fusion | flops 2359360 | bytes 799232 | tf_op jit(solution)/shard_map/dot_general | solution.py:153
  16.3 3.3 %all-to-all-done = f32[32,1,984]{2,1,0:T(1,128)S(1)} async-done(((f32[32,1,984]{2,1,0:T(1,128)}), f32[32,1,984]{2,1,0:T(1,128)S(1)}, u32[]{:S(2)}, u32[]{:S(2)}) %all-to-all-start) | async-done | bytes 125984 | tf_op jit(solution)/shard_map/all_to_all | solution.py:148
  19.6 0.3 reduce.10
  20.2 0.3 slice_reduce_fusion.1
  20.7 0.3 fusion.13
  21.0 0.2 copy.44
  21.2 0.4 %copy.45 = f32[2,2,2,3,6,2,16]{6,2,1,5,4,3,0:T(2,128)S(1)} copy(f32[2,2,2,3,6,2,16]{4,5,2,6,1,0,3:T(2,128)S(1)} %bitcast.77) | data formatting | bytes 36864 | tf_op jit(solution)/shard_map/mul | solution.py:193
  21.7 0.2 reshape.248
  22.2 0.2 copy-done.9
  22.4 1.0 %convolution_select_fusion = f32[2,4,8,2,512]{4,2,3,1,0:T(8,128)S(1)} fusion(f32[3,3,3,16,512]{4,3,2,1,0:T(8,128)S(1)} %copy-done.9, f32[4,6,1,7,2,16]{5,3,4,1,0,2:T(8,128)S(1)} %slice.65, f32[4,6,1,8,2,16]{5,3,4,1,0,2:T(8,128)S(1)} %copy.48, pred[8,2]{0,1:T(4,128)(4,1)S(1)} %copy-done.10), kind=kOutput, calls=%fused_computation.8 | convolution fusion | flops 169971712 | bytes 1192976 | tf_op jit(solution)/shard_map/conv_general_dilated | solution.py:21
  23.3 0.2 copy.49
  23.8 0.3 broadcast_in_dim.80
  24.1 0.2 reshape.252
  24.4 0.2 slice_bitcast_fusion
  24.6 0.5 %copy.59 = bf16[4,6,1,26,512]{4,0,3,1,2:T(4,128)(2,1)S(1)} copy(bf16[4,6,1,26,512]{4,1,3,0,2:T(8,128)(2,1)S(1)} %slice_bitcast_fusion) | data formatting | bytes 1277952
  25.1 0.3 pad.16.clone
  25.4 0.4 %copy.52 = bf16[4,6,1,8,4,512]{5,3,4,1,0,2:T(8,128)(2,1)S(1)} copy(bf16[4,6,1,8,4,512]{5,0,4,3,1,2:T(4,128)(2,1)S(1)} %bitcast.76) | data formatting | bytes 1572864 | tf_op jit(solution)/shard_map/conv_general_dilated | solution.py:21
  26.0 2.0 %select_reduce_fusion.1 = (f32[64]{0:T(128)S(1)}, f32[2,4,8,4,64]{4,2,3,1,0:T(8,128)S(1)}) fusion(f32[64]{0:T(128)S(1)} %copy-done.4, pred[8,4]{0,1:T(4,128)(4,1)S(1)} %copy-done.8, bf16[3,3,3,64,512]{4,3,2,1,0:T(8,128)(2,1)S(1)} %copy-done, bf16[4,6,1,7,2,512]{5,3,4,1,0,2:T(8,128)(2,1)S(1)} %slice.69, bf16[4,6,1,8,4,512]{5,3,4,1,0,2:T(8,128)(2,1)S(1)} %copy.52), kind=kOutput, calls=%fused_computation.40 | convolution fusion | flops 456589248 | bytes 2966048 | tf_op jit(solution)/shard_map/conv_general_dilated | solution.py:21
  28.8 0.6 %broadcast_in_dim.83 = f32[8,1,16]{2,1,0:T(1,128)} broadcast(f32[16]{0:T(128)S(1)} %pad_maximum_fusion.3), dimensions={2} | broadcast | bytes 576 | tf_op jit(solution)/shard_map/broadcast_in_dim | solution.py:224
  29.4 3.3 %all-to-all-start.1 = ((f32[8,1,16]{2,1,0:T(1,128)}), f32[8,1,16]{2,1,0:T(1,128)S(1)}, u32[]{:S(2)}, u32[]{:S(2)}) async-start(f32[8,1,16]{2,1,0:T(1,128)} %broadcast_in_dim.83), calls=%async_computation.1 | async-start | bytes 8192 | tf_op jit(solution)/shard_map/all_to_all | solution.py:227
  32.7 4.4 %all-to-all-done.1 = f32[8,1,16]{2,1,0:T(1,128)S(1)} async-done(((f32[8,1,16]{2,1,0:T(1,128)}), f32[8,1,16]{2,1,0:T(1,128)S(1)}, u32[]{:S(2)}, u32[]{:S(2)}) %all-to-all-start.1) | async-done | bytes 544 | tf_op jit(solution)/shard_map/all_to_all | solution.py:227
  37.7 0.2 copy.54
  37.8 0.7 %copy.55 = f32[4,24,128]{2,1,0:T(8,128)} copy(f32[4,24,128]{1,2,0:T(8,128)S(1)} %bitcast.78) | data formatting | bytes 98304 | tf_op jit(solution)/shard_map/reshape | solution.py:240
  (71 shorter events, 2.9 us)
Async XLA Ops:
  0.0 25.9 %copy-start = (bf16[3,3,3,64,512]{4,3,2,1,0:T(8,128)(2,1)S(1)}, bf16[3,3,3,64,512]{4,3,2,1,0:T(8,128)(2,1)}, u32[]{:S(2)}) copy-start(bf16[3,3,3,64,512]{4,3,2,1,0:T(8,128)(2,1)} %param.20) | copy-start | bytes 5308420
  0.0 12.8 %copy-start.1 = (f32[64,3072]{1,0:T(8,128)S(1)}, f32[64,3072]{1,0:T(8,128)}, u32[]{:S(2)}) copy-start(f32[64,3072]{1,0:T(8,128)} %weight_ref.1) | copy-start | bytes 2359300
  4.5 15.0 %all-to-all-start = ((f32[32,1,984]{2,1,0:T(1,128)}), f32[32,1,984]{2,1,0:T(1,128)S(1)}, u32[]{:S(2)}, u32[]{:S(2)}) async-start(f32[32,1,984]{2,1,0:T(1,128)} %broadcast.234), calls=%async_computation | async-start | bytes 262144 | tf_op jit(solution)/shard_map/all_to_all | solution.py:148
  12.8 2.7 %copy-start.2 = (f32[3072]{0:T(1024)S(1)}, f32[3072]{0:T(1024)}, u32[]{:S(2)}) copy-start(f32[3072]{0:T(1024)} %param.14) | copy-start | bytes 36868
  12.8 2.7 %copy-start.5 = (f32[64]{0:T(128)S(1)}, f32[64]{0:T(128)}, u32[]{:S(2)}) copy-start(f32[64]{0:T(128)} %param.16) | copy-start | bytes 772
  21.2 1.2 %copy-start.9 = (f32[3,3,3,16,512]{4,3,2,1,0:T(8,128)S(1)}, f32[3,3,3,16,512]{4,3,2,1,0:T(8,128)}, u32[]{:S(2)}) copy-start(f32[3,3,3,16,512]{4,3,2,1,0:T(8,128)} %param.18) | copy-start | bytes 2654212
  21.2 1.2 %copy-start.10 = (pred[8,2]{0,1:T(4,128)(4,1)S(1)}, pred[8,2]{0,1:T(4,128)(4,1)}, u32[]{:S(2)}) copy-start(pred[8,2]{0,1:T(4,128)(4,1)} %constant.78) | copy-start | bytes 52
  22.4 1.1 %copy-start.3 = (f32[512]{0:T(512)S(1)}, f32[512]{0:T(512)}, u32[]{:S(2)}) copy-start(f32[512]{0:T(512)} %param.19) | copy-start | bytes 6148
  25.1 0.9 %copy-start.4 = (f32[64]{0:T(128)S(1)}, f32[64]{0:T(128)}, u32[]{:S(2)}) copy-start(f32[64]{0:T(128)} %param.21) | copy-start | bytes 772
  25.1 0.9 %copy-start.8 = (pred[8,4]{0,1:T(4,128)(4,1)S(1)}, pred[8,4]{0,1:T(4,128)(4,1)}, u32[]{:S(2)}) copy-start(pred[8,4]{0,1:T(4,128)(4,1)} %constant.77) | copy-start | bytes 100
  25.9 11.7 %copy-start.6 = (f32[64]{0:T(128)S(1)}, f32[64]{0:T(128)}, u32[]{:S(2)}) copy-start(f32[64]{0:T(128)} %param.23) | copy-start | bytes 772
  26.0 11.6 %copy-start.7 = (f32[64]{0:T(128)S(1)}, f32[64]{0:T(128)}, u32[]{:S(2)}) copy-start(f32[64]{0:T(128)} %param.22) | copy-start | bytes 772
  29.4 7.8 %all-to-all-start.1 = ((f32[8,1,16]{2,1,0:T(1,128)}), f32[8,1,16]{2,1,0:T(1,128)S(1)}, u32[]{:S(2)}, u32[]{:S(2)}) async-start(f32[8,1,16]{2,1,0:T(1,128)} %broadcast_in_dim.83), calls=%async_computation.1 | async-start | bytes 8192 | tf_op jit(solution)/shard_map/all_to_all | solution.py:227

commit v9 on v8

--- a/solution.py
+++ b/solution.py
@@ -30,34 +30,45 @@
     return result[0]
 
 
-def shard_kernel(rep_ref, tok_ref, weight_ref, scale_ref, latent_ref, out_ref, share_ref):
-    share_ref[...] = latent_ref[...]
+def shard_kernel(rep_ref, tok_ref, weight_ref, scale_ref, latent_ref, out_ref):
     weight = weight_ref[...] * (1.0 + scale_ref[...])
+    width = weight.shape[0]
+    band_cols = tok_ref.shape[1]
+    record = width + 2
     for frame in range(tok_ref.shape[0]):
         for row in range(tok_ref.shape[2]):
             x = tok_ref[frame, :, row, :]
             mean = jnp.mean(x, axis=1, keepdims=True)
             centred = x - mean
-            width = weight.shape[0]
-            out_ref[frame, row, :, :width] = lax.dot_general(
+            m2 = jnp.sum(centred * centred, axis=1, keepdims=True)
+            projected = lax.dot_general(
                 centred,
                 weight,
                 (((1,), (1,)), ((), ())),
                 precision=lax.Precision.HIGHEST,
                 preferred_element_type=jnp.float32,
             )
-            out_ref[frame, row, :, width : width + 1] = mean
-            out_ref[frame, row, :, width + 1 : width + 2] = jnp.sum(
-                centred * centred, axis=1, keepdims=True
-            )
+            for col in range(band_cols):
+                base = ((frame * tok_ref.shape[2] + row) * band_cols + col) * record
+                out_ref[:, pl.ds(base, width)] = projected[col : col + 1, :]
+                out_ref[:, pl.ds(base + width, 1)] = mean[col : col + 1, :]
+                out_ref[:, pl.ds(base + width + 1, 1)] = m2[col : col + 1, :]
+    lines, lat_rows, channels = latent_ref.shape
+    offset = tok_ref.shape[0] * tok_ref.shape[2] * band_cols * record
+    share = latent_ref[...]
+    for line in range(lines):
+        for row in range(lat_rows):
+            out_ref[:, pl.ds(offset + (line * lat_rows + row) * channels, channels)] = share[
+                line, row : row + 1, :
+            ]
 
 
 def shard_moments(tokens, proj_weight, mod_scale, latent_lines, share, rep):
     tok_frames, patch_rows, band_cols, local_width = tokens.shape
     out_width = proj_weight.shape[0]
+    size = tok_frames * patch_rows * band_cols * (out_width + 2) + latent_lines[0].size * share
     whole = lambda i, r: (0, 0, 0, 0)
     whole3 = lambda i, r: (0, 0, 0)
-    lead = (tok_frames, patch_rows, band_cols)
     return pl.pallas_call(
         shard_kernel,
         grid_spec=pltpu.PrefetchScalarGridSpec(
@@ -72,22 +83,16 @@
                     (lambda i, r: (r[0], 0, 0)) if share < latent_lines.shape[0] else whole3,
                 ),
             ],
-            out_specs=[
-                pl.BlockSpec(lead + (out_width + 2,), whole),
-                pl.BlockSpec((share,) + latent_lines.shape[1:], whole3),
-            ],
+            out_specs=pl.BlockSpec((1, size), lambda i, r: (0, 0)),
         ),
-        out_shape=[
-            jax.ShapeDtypeStruct(lead + (out_width + 2,), jnp.float32),
-            jax.ShapeDtypeStruct((share,) + latent_lines.shape[1:], jnp.float32),
-        ],
+        out_shape=jax.ShapeDtypeStruct((1, size), jnp.float32),
     )(
         rep.reshape(1).astype(jnp.int32),
         tokens.transpose(0, 2, 1, 3),
         proj_weight,
         mod_scale.reshape(1, -1),
         latent_lines,
-    )
+    )[0]
 
 
 def neighbours(stack, index, axis):
@@ -122,29 +127,29 @@
     lines = frames * lat_cols
     stored = noisy_latent.transpose(0, 2, 1, 3).reshape(lines, lat_rows, LC)
     share = lines // n_rep if lines % n_rep == 0 else lines
-    partial, latent_part = shard_moments(
-        tokens, proj_weight, mod_scale, stored, share, rep
-    )
-    latent_part = latent_part.reshape(-1)
+    payload = shard_moments(tokens, proj_weight, mod_scale, stored, share, rep)
+    part_flat = tok_frames * patch_rows * band_cols * (out_width + 2)
 
     slab = lat_rows // 2
     if patch_rows <= slab + 2:
         window = patch_rows
-        per_slab = jnp.broadcast_to(partial[None], (n_sp,) + partial.shape)
+        part_size = part_flat
+        send = jnp.broadcast_to(payload, (n_dev, payload.shape[0]))
     else:
         window = slab + 2
+        partial = payload[:part_flat].reshape(tok_frames, patch_rows, band_cols, out_width + 2)
         padded = jnp.pad(partial, ((0, 0), (1, 1), (0, 0), (0, 0)))
         per_slab = jnp.stack([padded[:, p * slab : p * slab + window] for p in range(n_sp)])
-    per_slab = per_slab.reshape(n_sp, -1)
-    part_size = per_slab.shape[1]
-
-    send = jnp.concatenate(
-        [
-            jnp.broadcast_to(per_slab[None, :, None], (n_sec, n_sp, n_rep, part_size)),
-            jnp.broadcast_to(latent_part, (n_sec, n_sp, n_rep, latent_part.shape[0])),
-        ],
-        axis=-1,
-    ).reshape(n_dev, -1)
+        per_slab = per_slab.reshape(n_sp, -1)
+        part_size = per_slab.shape[1]
+        latent_part = payload[part_flat:]
+        send = jnp.concatenate(
+            [
+                jnp.broadcast_to(per_slab[None, :, None], (n_sec, n_sp, n_rep, part_size)),
+                jnp.broadcast_to(latent_part, (n_sec, n_sp, n_rep, latent_part.shape[0])),
+            ],
+            axis=-1,
+        ).reshape(n_dev, -1)
     received = lax.all_to_all(send, ALL, 0, 0, tiled=False).reshape(n_sec, n_sp, n_rep, -1)
 
     scaled_weight = proj_weight * (1.0 + mod_scale)[None, :]

time: 39 us -> 38.1 us (0.977)
  local copies, waits for them, and re-layouts: 9.8 us -> 8.93 us
    reshape x1 -> x0, local copies, waits for them, and re-layouts: 0.78 us -> none  [per_device(): latent_part = latent_part.reshape(-1)]
    all_to_all x1 -> x0, local copies, waits for them, and re-layouts: 0.72 us -> none  [per_device(): lax.all_to_all(send, ALL, 0, 0, tiled=False).reshape(n_sec, n_sp, n_rep, -1)]
    broadcast_in_dim x1, local copies, waits for them, and re-layouts: 0.77 us -> 1.4 us  [per_device(): send = jnp.broadcast_to(payload, (n_dev, payload.shape[0]))]
  transfers between devices with their start and end apart: 2 -> 2, of which waited for: 2 -> 2; matrix products, arithmetic and copies ran while one was open for 11% -> 12% of each run, Pallas kernels for 0% -> 0%
where the time goes in v9:
time: 38.1 us; the launch traced here: 37.7 us
  starting transfers between devices  10.6 us (28%)
  local copies, waits for them, and re-layouts  8.93 us (23%)
  waiting for transfers between devices  7.77 us (20%)
  matrix products  3.96 us (10%)
  other arithmetic  3.74 us (10%)
  Pallas kernels  2.28 us (6%)
  between operations  0.42 us (1%)
    all_to_all x1, starting transfers between devices, per_device(): lax.all_to_all(send, ALL, 0, 0, tiled=False).reshape(n_sec, n_sp, n_rep, -1)  7.3 us
    all_to_all x1, waiting for transfers between devices, per_device(): stats = lax.all_to_all(stats, BLOCKS, 0, 0, tiled=False)  4.45 us
    all_to_all x1, waiting for transfers between devices, per_device(): lax.all_to_all(send, ALL, 0, 0, tiled=False).reshape(n_sec, n_sp, n_rep, -1)  3.32 us
    all_to_all x1, starting transfers between devices, per_device(): stats = lax.all_to_all(stats, BLOCKS, 0, 0, tiled=False)  3.31 us
    conv_general_dilated x2, matrix products, valid_conv(): lax.conv_general_dilated(front[None], kernel, (1, 1, 1), 'VALID', dimensi...  2.96 us
    pallas_call x1, Pallas kernels, shard_moments(): pl.pallas_call(shard_kernel, grid_spec=pltpu.PrefetchScalarGridSpec(num_s...  2.28 us
    reshape x1, local copies, waits for them, and re-layouts, per_device(): scaled_weight.reshape(out_width, n_rep, local_width)  1.51 us
    broadcast_in_dim x1, local copies, waits for them, and re-layouts, per_device(): send = jnp.broadcast_to(payload, (n_dev, payload.shape[0]))  1.4 us
  transfers between devices with their start and end apart: 2, of which 2 were waited for; matrix products, arithmetic and copies ran while one was open for 12% of the time, Pallas kernels for 0%

profile of v9, /device:TPU:0, one launch (start us, length us, event | category | flops | bytes accessed | tf_op | source)
XLA Modules:
  0.0 37.7 jit_solution(16736262738253237760)
XLA Ops:
  0.0 2.3 %shard_map.118 = f32[1,984]{1,0:T(1,128)} custom-call(s32[1]{0:T(128)} %bitcast.rep_ref, f32[1,6,2,768]{3,2,1,0:T(2,128)} %bitcast.89, f32[64,3072]{1,0:T(8,128)} %weight_ref.1, f32[1,3072]{1,0:T(1,128)} %bitcast.88, f32[24,2,16]{2,1,0:T(2,128)} %bitcast.90), custom_call_target="tpu_custom_call" | custom-call | tf_op jit(solution)/shard_map/pallas_call | solution.py:72
  2.3 1.4 %broadcast_in_dim.38 = f32[32,1,984]{2,1,0:T(1,128)} broadcast(f32[984]{0:T(1024)} %bitcast.91), dimensions={2} | broadcast | bytes 129888 | tf_op jit(solution)/shard_map/broadcast_in_dim | solution.py:137
  3.7 7.3 %all-to-all-start = ((f32[32,1,984]{2,1,0:T(1,128)}), f32[32,1,984]{2,1,0:T(1,128)S(1)}, u32[]{:S(2)}, u32[]{:S(2)}) async-start(f32[32,1,984]{2,1,0:T(1,128)} %broadcast_in_dim.38), calls=%async_computation | async-start | bytes 262144 | tf_op jit(solution)/shard_map/all_to_all | solution.py:153
  11.0 0.7 %broadcast_add_fusion = f32[3072]{0:T(1024)S(1)} fusion(f32[3072]{0:T(1024)} %param.13), kind=kLoop, calls=%fused_computation.55 | loop fusion | flops 3072 | bytes 24576 | tf_op jit(solution)/shard_map/add | solution.py:155
  12.0 0.9 %broadcast_multiply_fusion = f32[64,3072]{1,0:T(8,128)} fusion(f32[64,3072]{1,0:T(8,128)S(1)} %copy-done.1, f32[3072]{0:T(1024)S(1)} %broadcast_add_fusion), kind=kLoop, calls=%fused_computation.23 | loop fusion | flops 196608 | bytes 1585152 | tf_op jit(solution)/shard_map/mul | solution.py:155
  12.9 1.5 %reshape.244 = f32[64,4,768]{2,1,0:T(4,128)S(1)} reshape(f32[64,3072]{1,0:T(8,128)} %broadcast_multiply_fusion) | data formatting | bytes 1572864 | tf_op jit(solution)/shard_map/reshape | solution.py:156
  14.4 0.2 reduce_sum.108
  14.7 0.7 %fusion.14 = f32[64]{0:T(128)S(1)} fusion(f32[64]{0:T(128)S(1)} %copy-done.5, f32[64,3072]{1,0:T(8,128)S(1)} %copy-done.1, f32[3072,1]{0,1:T(1,128)S(1)} %bitcast.92), kind=kOutput, calls=%fused_computation.15 | convolution fusion | flops 2359360 | bytes 799232 | tf_op jit(solution)/shard_map/dot_general | solution.py:158
  15.4 3.3 %all-to-all-done = f32[32,1,984]{2,1,0:T(1,128)S(1)} async-done(((f32[32,1,984]{2,1,0:T(1,128)}), f32[32,1,984]{2,1,0:T(1,128)S(1)}, u32[]{:S(2)}, u32[]{:S(2)}) %all-to-all-start) | async-done | bytes 125984 | tf_op jit(solution)/shard_map/all_to_all | solution.py:153
  18.7 0.3 reduce.10
  19.1 0.2 reshape.243
  19.3 0.3 slice_reduce_fusion.1
  19.9 0.3 fusion.13
  20.1 0.2 copy.44
  20.4 0.4 %copy.45 = f32[2,2,2,3,6,2,16]{6,2,1,5,4,3,0:T(2,128)S(1)} copy(f32[2,2,2,3,6,2,16]{4,5,2,6,1,0,3:T(2,128)S(1)} %bitcast.78) | data formatting | bytes 36864 | tf_op jit(solution)/shard_map/mul | solution.py:198
  20.8 0.2 reshape.241
  21.3 0.2 copy-done.9
  21.5 1.0 %convolution_select_fusion = f32[2,4,8,2,512]{4,2,3,1,0:T(8,128)S(1)} fusion(f32[3,3,3,16,512]{4,3,2,1,0:T(8,128)S(1)} %copy-done.9, f32[4,6,1,7,2,16]{5,3,4,1,0,2:T(8,128)S(1)} %slice.65, f32[4,6,1,8,2,16]{5,3,4,1,0,2:T(8,128)S(1)} %copy.48, pred[8,2]{0,1:T(4,128)(4,1)S(1)} %copy-done.10), kind=kOutput, calls=%fused_computation.8 | convolution fusion | flops 169971712 | bytes 1192976 | tf_op jit(solution)/shard_map/conv_general_dilated | solution.py:21
  22.5 0.2 copy.49
  22.9 0.3 broadcast_in_dim.67
  23.2 0.2 reshape.245
  23.5 0.2 slice_bitcast_fusion
  23.7 0.5 %copy.59 = bf16[4,6,1,26,512]{4,0,3,1,2:T(4,128)(2,1)S(1)} copy(bf16[4,6,1,26,512]{4,1,3,0,2:T(8,128)(2,1)S(1)} %slice_bitcast_fusion) | data formatting | bytes 1277952
  24.2 0.3 pad.16.clone
  24.5 0.4 %copy.52 = bf16[4,6,1,8,4,512]{5,3,4,1,0,2:T(8,128)(2,1)S(1)} copy(bf16[4,6,1,8,4,512]{5,0,4,3,1,2:T(4,128)(2,1)S(1)} %bitcast.77) | data formatting | bytes 1572864 | tf_op jit(solution)/shard_map/conv_general_dilated | solution.py:21
  25.1 2.0 %select_reduce_fusion.1 = (f32[64]{0:T(128)S(1)}, f32[2,4,8,4,64]{4,2,3,1,0:T(8,128)S(1)}) fusion(f32[64]{0:T(128)S(1)} %copy-done.4, pred[8,4]{0,1:T(4,128)(4,1)S(1)} %copy-done.8, bf16[3,3,3,64,512]{4,3,2,1,0:T(8,128)(2,1)S(1)} %copy-done, bf16[4,6,1,7,2,512]{5,3,4,1,0,2:T(8,128)(2,1)S(1)} %slice.69, bf16[4,6,1,8,4,512]{5,3,4,1,0,2:T(8,128)(2,1)S(1)} %copy.52), kind=kOutput, calls=%fused_computation.40 | convolution fusion | flops 456589248 | bytes 2966048 | tf_op jit(solution)/shard_map/conv_general_dilated | solution.py:21
  27.5 0.1 select_reduce_fusion
  27.9 0.6 %broadcast_in_dim.70 = f32[8,1,16]{2,1,0:T(1,128)} broadcast(f32[16]{0:T(128)S(1)} %pad_maximum_fusion.2), dimensions={2} | broadcast | bytes 576 | tf_op jit(solution)/shard_map/broadcast_in_dim | solution.py:229
  28.5 3.3 %all-to-all-start.1 = ((f32[8,1,16]{2,1,0:T(1,128)}), f32[8,1,16]{2,1,0:T(1,128)S(1)}, u32[]{:S(2)}, u32[]{:S(2)}) async-start(f32[8,1,16]{2,1,0:T(1,128)} %broadcast_in_dim.70), calls=%async_computation.1 | async-start | bytes 8192 | tf_op jit(solution)/shard_map/all_to_all | solution.py:232
  31.9 4.4 %all-to-all-done.1 = f32[8,1,16]{2,1,0:T(1,128)S(1)} async-done(((f32[8,1,16]{2,1,0:T(1,128)}), f32[8,1,16]{2,1,0:T(1,128)S(1)}, u32[]{:S(2)}, u32[]{:S(2)}) %all-to-all-start.1) | async-done | bytes 544 | tf_op jit(solution)/shard_map/all_to_all | solution.py:232
  36.8 0.2 copy.54
  37.0 0.7 %copy.55 = f32[4,24,128]{2,1,0:T(8,128)} copy(f32[4,24,128]{1,2,0:T(8,128)S(1)} %bitcast.79) | data formatting | bytes 98304 | tf_op jit(solution)/shard_map/reshape | solution.py:245
  (68 shorter events, 2.5 us)
Async XLA Ops:
  0.0 25.1 %copy-start = (bf16[3,3,3,64,512]{4,3,2,1,0:T(8,128)(2,1)S(1)}, bf16[3,3,3,64,512]{4,3,2,1,0:T(8,128)(2,1)}, u32[]{:S(2)}) copy-start(bf16[3,3,3,64,512]{4,3,2,1,0:T(8,128)(2,1)} %param.20) | copy-start | bytes 5308420
  0.0 11.9 %copy-start.1 = (f32[64,3072]{1,0:T(8,128)S(1)}, f32[64,3072]{1,0:T(8,128)}, u32[]{:S(2)}) copy-start(f32[64,3072]{1,0:T(8,128)} %weight_ref.1) | copy-start | bytes 2359300
  3.7 15.0 %all-to-all-start = ((f32[32,1,984]{2,1,0:T(1,128)}), f32[32,1,984]{2,1,0:T(1,128)S(1)}, u32[]{:S(2)}, u32[]{:S(2)}) async-start(f32[32,1,984]{2,1,0:T(1,128)} %broadcast_in_dim.38), calls=%async_computation | async-start | bytes 262144 | tf_op jit(solution)/shard_map/all_to_all | solution.py:153
  12.0 2.7 %copy-start.2 = (f32[3072]{0:T(1024)S(1)}, f32[3072]{0:T(1024)}, u32[]{:S(2)}) copy-start(f32[3072]{0:T(1024)} %param.14) | copy-start | bytes 36868
  12.0 2.7 %copy-start.5 = (f32[64]{0:T(128)S(1)}, f32[64]{0:T(128)}, u32[]{:S(2)}) copy-start(f32[64]{0:T(128)} %param.16) | copy-start | bytes 772
  20.3 1.2 %copy-start.9 = (f32[3,3,3,16,512]{4,3,2,1,0:T(8,128)S(1)}, f32[3,3,3,16,512]{4,3,2,1,0:T(8,128)}, u32[]{:S(2)}) copy-start(f32[3,3,3,16,512]{4,3,2,1,0:T(8,128)} %param.18) | copy-start | bytes 2654212
  20.3 1.2 %copy-start.10 = (pred[8,2]{0,1:T(4,128)(4,1)S(1)}, pred[8,2]{0,1:T(4,128)(4,1)}, u32[]{:S(2)}) copy-start(pred[8,2]{0,1:T(4,128)(4,1)} %constant.78) | copy-start | bytes 52
  21.5 1.1 %copy-start.3 = (f32[512]{0:T(512)S(1)}, f32[512]{0:T(512)}, u32[]{:S(2)}) copy-start(f32[512]{0:T(512)} %param.19) | copy-start | bytes 6148
  24.2 0.9 %copy-start.4 = (f32[64]{0:T(128)S(1)}, f32[64]{0:T(128)}, u32[]{:S(2)}) copy-start(f32[64]{0:T(128)} %param.21) | copy-start | bytes 772
  24.2 0.9 %copy-start.8 = (pred[8,4]{0,1:T(4,128)(4,1)S(1)}, pred[8,4]{0,1:T(4,128)(4,1)}, u32[]{:S(2)}) copy-start(pred[8,4]{0,1:T(4,128)(4,1)} %constant.77) | copy-start | bytes 100
  25.1 11.7 %copy-start.6 = (f32[64]{0:T(128)S(1)}, f32[64]{0:T(128)}, u32[]{:S(2)}) copy-start(f32[64]{0:T(128)} %param.23) | copy-start | bytes 772
  25.1 11.6 %copy-start.7 = (f32[64]{0:T(128)S(1)}, f32[64]{0:T(128)}, u32[]{:S(2)}) copy-start(f32[64]{0:T(128)} %param.22) | copy-start | bytes 772
  28.5 7.8 %all-to-all-start.1 = ((f32[8,1,16]{2,1,0:T(1,128)}), f32[8,1,16]{2,1,0:T(1,128)S(1)}, u32[]{:S(2)}, u32[]{:S(2)}) async-start(f32[8,1,16]{2,1,0:T(1,128)} %broadcast_in_dim.70), calls=%async_computation.1 | async-start | bytes 8192 | tf_op jit(solution)/shard_map/all_to_all | solution.py:232

commit v10 on v9

--- a/solution.py
+++ b/solution.py
@@ -30,7 +30,8 @@
     return result[0]
 
 
-def shard_kernel(rep_ref, tok_ref, weight_ref, scale_ref, latent_ref, out_ref):
+def shard_kernel(rep_ref, tok_ref, weight_ref, scale_ref, latent_ref, copies_ref):
+    out_ref = copies_ref.at[0]
     weight = weight_ref[...] * (1.0 + scale_ref[...])
     width = weight.shape[0]
     band_cols = tok_ref.shape[1]
@@ -61,9 +62,12 @@
             out_ref[:, pl.ds(offset + (line * lat_rows + row) * channels, channels)] = share[
                 line, row : row + 1, :
             ]
-
-
-def shard_moments(tokens, proj_weight, mod_scale, latent_lines, share, rep):
+    row_value = out_ref[...]
+    for copy in range(1, copies_ref.shape[0]):
+        copies_ref[copy] = row_value
+
+
+def shard_moments(tokens, proj_weight, mod_scale, latent_lines, share, rep, copies):
     tok_frames, patch_rows, band_cols, local_width = tokens.shape
     out_width = proj_weight.shape[0]
     size = tok_frames * patch_rows * band_cols * (out_width + 2) + latent_lines[0].size * share
@@ -83,16 +87,16 @@
                     (lambda i, r: (r[0], 0, 0)) if share < latent_lines.shape[0] else whole3,
                 ),
             ],
-            out_specs=pl.BlockSpec((1, size), lambda i, r: (0, 0)),
+            out_specs=pl.BlockSpec((copies, 1, size), whole3),
         ),
-        out_shape=jax.ShapeDtypeStruct((1, size), jnp.float32),
+        out_shape=jax.ShapeDtypeStruct((copies, 1, size), jnp.float32),
     )(
         rep.reshape(1).astype(jnp.int32),
         tokens.transpose(0, 2, 1, 3),
         proj_weight,
         mod_scale.reshape(1, -1),
         latent_lines,
-    )[0]
+    )
 
 
 def neighbours(stack, index, axis):
@@ -127,15 +131,19 @@
     lines = frames * lat_cols
     stored = noisy_latent.transpose(0, 2, 1, 3).reshape(lines, lat_rows, LC)
     share = lines // n_rep if lines % n_rep == 0 else lines
-    payload = shard_moments(tokens, proj_weight, mod_scale, stored, share, rep)
+    slab = lat_rows // 2
+    every_row = patch_rows <= slab + 2
+    payload = shard_moments(
+        tokens, proj_weight, mod_scale, stored, share, rep, n_dev if every_row else 1
+    )
     part_flat = tok_frames * patch_rows * band_cols * (out_width + 2)
 
-    slab = lat_rows // 2
-    if patch_rows <= slab + 2:
+    if every_row:
         window = patch_rows
         part_size = part_flat
-        send = jnp.broadcast_to(payload, (n_dev, payload.shape[0]))
+        send = payload
     else:
+        payload = payload[0, 0]
         window = slab + 2
         partial = payload[:part_flat].reshape(tok_frames, patch_rows, band_cols, out_width + 2)
         padded = jnp.pad(partial, ((0, 0), (1, 1), (0, 0), (0, 0)))

time: 38.1 us -> 36.7 us (0.963)
  local copies, waits for them, and re-layouts: 8.93 us -> 7.52 us
    broadcast_in_dim x1 -> x0, local copies, waits for them, and re-layouts: 1.4 us -> none  [per_device(): send = jnp.broadcast_to(payload, (n_dev, payload.shape[0]))]
where the time goes in v10:
time: 36.7 us; the launch traced here: 36.4 us
  starting transfers between devices  10.6 us (29%)
  waiting for transfers between devices  7.77 us (21%)
  local copies, waits for them, and re-layouts  7.52 us (20%)
  matrix products  3.96 us (11%)
  other arithmetic  3.74 us (10%)
  Pallas kernels  2.35 us (6%)
  between operations  0.42 us (1%)
    all_to_all x1, starting transfers between devices, per_device(): lax.all_to_all(send, ALL, 0, 0, tiled=False).reshape(n_sec, n_sp, n_rep, -1)  7.3 us
    all_to_all x1, waiting for transfers between devices, per_device(): stats = lax.all_to_all(stats, BLOCKS, 0, 0, tiled=False)  4.45 us
    all_to_all x1, waiting for transfers between devices, per_device(): lax.all_to_all(send, ALL, 0, 0, tiled=False).reshape(n_sec, n_sp, n_rep, -1)  3.32 us
    all_to_all x1, starting transfers between devices, per_device(): stats = lax.all_to_all(stats, BLOCKS, 0, 0, tiled=False)  3.31 us
    conv_general_dilated x2, matrix products, valid_conv(): lax.conv_general_dilated(front[None], kernel, (1, 1, 1), 'VALID', dimensi...  2.95 us
    pallas_call x1, Pallas kernels, shard_moments(): pl.pallas_call(shard_kernel, grid_spec=pltpu.PrefetchScalarGridSpec(num_s...  2.35 us
    reshape x1, local copies, waits for them, and re-layouts, per_device(): scaled_weight.reshape(out_width, n_rep, local_width)  1.51 us
    mul x1, other arithmetic, per_device(): scaled_weight = proj_weight * (1.0 + mod_scale)[None, :]  0.94 us
  transfers between devices with their start and end apart: 2, of which 2 were waited for; matrix products, arithmetic and copies ran while one was open for 12% of the time, Pallas kernels for 0%

profile of v10, /device:TPU:0, one launch (start us, length us, event | category | flops | bytes accessed | tf_op | source)
XLA Modules:
  0.0 36.4 jit_solution(2632353087792245703)
XLA Ops:
  0.0 2.3 %shard_map.118 = f32[32,1,984]{2,1,0:T(1,128)} custom-call(s32[1]{0:T(128)} %bitcast.rep_ref, f32[1,6,2,768]{3,2,1,0:T(2,128)} %bitcast.88, f32[64,3072]{1,0:T(8,128)} %weight_ref.1, f32[1,3072]{1,0:T(1,128)} %bitcast.87, f32[24,2,16]{2,1,0:T(2,128)} %bitcast.89), custom_call_target="tpu_custom_call" | custom-call | tf_op jit(solution)/shard_map/pallas_call | solution.py:76
  2.4 7.3 %all-to-all-start = ((f32[32,1,984]{2,1,0:T(1,128)}), f32[32,1,984]{2,1,0:T(1,128)S(1)}, u32[]{:S(2)}, u32[]{:S(2)}) async-start(f32[32,1,984]{2,1,0:T(1,128)} %shard_map.118), calls=%async_computation | async-start | bytes 262144 | tf_op jit(solution)/shard_map/all_to_all | solution.py:161
  9.7 0.7 %broadcast_add_fusion = f32[3072]{0:T(1024)S(1)} fusion(f32[3072]{0:T(1024)} %param.13), kind=kLoop, calls=%fused_computation.55 | loop fusion | flops 3072 | bytes 24576 | tf_op jit(solution)/shard_map/add | solution.py:163
  10.6 0.9 %broadcast_multiply_fusion = f32[64,3072]{1,0:T(8,128)} fusion(f32[64,3072]{1,0:T(8,128)S(1)} %copy-done.1, f32[3072]{0:T(1024)S(1)} %broadcast_add_fusion), kind=kLoop, calls=%fused_computation.23 | loop fusion | flops 196608 | bytes 1585152 | tf_op jit(solution)/shard_map/mul | solution.py:163
  11.6 1.5 %reshape.237 = f32[64,4,768]{2,1,0:T(4,128)S(1)} reshape(f32[64,3072]{1,0:T(8,128)} %broadcast_multiply_fusion) | data formatting | bytes 1572864 | tf_op jit(solution)/shard_map/reshape | solution.py:164
  13.1 0.2 reduce_sum.108
  13.3 0.7 %fusion.14 = f32[64]{0:T(128)S(1)} fusion(f32[64]{0:T(128)S(1)} %copy-done.5, f32[64,3072]{1,0:T(8,128)S(1)} %copy-done.1, f32[3072,1]{0,1:T(1,128)S(1)} %bitcast.90), kind=kOutput, calls=%fused_computation.15 | convolution fusion | flops 2359360 | bytes 799232 | tf_op jit(solution)/shard_map/dot_general | solution.py:166
  14.1 3.3 %all-to-all-done = f32[32,1,984]{2,1,0:T(1,128)S(1)} async-done(((f32[32,1,984]{2,1,0:T(1,128)}), f32[32,1,984]{2,1,0:T(1,128)S(1)}, u32[]{:S(2)}, u32[]{:S(2)}) %all-to-all-start) | async-done | bytes 125984 | tf_op jit(solution)/shard_map/all_to_all | solution.py:161
  17.4 0.3 reduce.10
  17.8 0.2 reshape.236
  18.0 0.3 slice_reduce_fusion.1
  18.5 0.3 fusion.13
  18.8 0.2 copy.43
  19.0 0.4 %copy.44 = f32[2,2,2,3,6,2,16]{6,2,1,5,4,3,0:T(2,128)S(1)} copy(f32[2,2,2,3,6,2,16]{4,5,2,6,1,0,3:T(2,128)S(1)} %bitcast.77) | data formatting | bytes 36864 | tf_op jit(solution)/shard_map/mul | solution.py:206
  19.5 0.2 reshape.234
  20.0 0.2 copy-done.9
  20.2 1.0 %convolution_select_fusion = f32[2,4,8,2,512]{4,2,3,1,0:T(8,128)S(1)} fusion(f32[3,3,3,16,512]{4,3,2,1,0:T(8,128)S(1)} %copy-done.9, f32[4,6,1,7,2,16]{5,3,4,1,0,2:T(8,128)S(1)} %slice.65, f32[4,6,1,8,2,16]{5,3,4,1,0,2:T(8,128)S(1)} %copy.47, pred[8,2]{0,1:T(4,128)(4,1)S(1)} %copy-done.10), kind=kOutput, calls=%fused_computation.8 | convolution fusion | flops 169971712 | bytes 1192976 | tf_op jit(solution)/shard_map/conv_general_dilated | solution.py:21
  21.1 0.2 copy.48
  21.5 0.1 pad_maximum_fusion.1
  21.6 0.3 broadcast_in_dim.39
  21.9 0.2 reshape.238
  22.2 0.2 slice_bitcast_fusion
  22.4 0.5 %copy.58 = bf16[4,6,1,26,512]{4,0,3,1,2:T(4,128)(2,1)S(1)} copy(bf16[4,6,1,26,512]{4,1,3,0,2:T(8,128)(2,1)S(1)} %slice_bitcast_fusion) | data formatting | bytes 1277952
  22.9 0.3 pad.16.clone
  23.2 0.4 %copy.51 = bf16[4,6,1,8,4,512]{5,3,4,1,0,2:T(8,128)(2,1)S(1)} copy(bf16[4,6,1,8,4,512]{5,0,4,3,1,2:T(4,128)(2,1)S(1)} %bitcast.76) | data formatting | bytes 1572864 | tf_op jit(solution)/shard_map/conv_general_dilated | solution.py:21
  23.8 2.0 %select_reduce_fusion.1 = (f32[64]{0:T(128)S(1)}, f32[2,4,8,4,64]{4,2,3,1,0:T(8,128)S(1)}) fusion(f32[64]{0:T(128)S(1)} %copy-done.4, pred[8,4]{0,1:T(4,128)(4,1)S(1)} %copy-done.8, bf16[3,3,3,64,512]{4,3,2,1,0:T(8,128)(2,1)S(1)} %copy-done, bf16[4,6,1,7,2,512]{5,3,4,1,0,2:T(8,128)(2,1)S(1)} %slice.69, bf16[4,6,1,8,4,512]{5,3,4,1,0,2:T(8,128)(2,1)S(1)} %copy.51), kind=kOutput, calls=%fused_computation.40 | convolution fusion | flops 456589248 | bytes 2966048 | tf_op jit(solution)/shard_map/conv_general_dilated | solution.py:21
  26.2 0.1 select_reduce_fusion
  26.6 0.6 %broadcast_in_dim.66 = f32[8,1,16]{2,1,0:T(1,128)} broadcast(f32[16]{0:T(128)S(1)} %pad_maximum_fusion.2), dimensions={2} | broadcast | bytes 576 | tf_op jit(solution)/shard_map/broadcast_in_dim | solution.py:237
  27.2 3.3 %all-to-all-start.1 = ((f32[8,1,16]{2,1,0:T(1,128)}), f32[8,1,16]{2,1,0:T(1,128)S(1)}, u32[]{:S(2)}, u32[]{:S(2)}) async-start(f32[8,1,16]{2,1,0:T(1,128)} %broadcast_in_dim.66), calls=%async_computation.1 | async-start | bytes 8192 | tf_op jit(solution)/shard_map/all_to_all | solution.py:240
  30.5 4.4 %all-to-all-done.1 = f32[8,1,16]{2,1,0:T(1,128)S(1)} async-done(((f32[8,1,16]{2,1,0:T(1,128)}), f32[8,1,16]{2,1,0:T(1,128)S(1)}, u32[]{:S(2)}, u32[]{:S(2)}) %all-to-all-start.1) | async-done | bytes 544 | tf_op jit(solution)/shard_map/all_to_all | solution.py:240
  35.5 0.2 copy.53
  35.6 0.7 %copy.54 = f32[4,24,128]{2,1,0:T(8,128)} copy(f32[4,24,128]{1,2,0:T(8,128)S(1)} %bitcast.78) | data formatting | bytes 98304 | tf_op jit(solution)/shard_map/reshape | solution.py:253
  (67 shorter events, 2.4 us)
Async XLA Ops:
  0.0 23.7 %copy-start = (bf16[3,3,3,64,512]{4,3,2,1,0:T(8,128)(2,1)S(1)}, bf16[3,3,3,64,512]{4,3,2,1,0:T(8,128)(2,1)}, u32[]{:S(2)}) copy-start(bf16[3,3,3,64,512]{4,3,2,1,0:T(8,128)(2,1)} %param.20) | copy-start | bytes 5308420
  0.0 10.6 %copy-start.1 = (f32[64,3072]{1,0:T(8,128)S(1)}, f32[64,3072]{1,0:T(8,128)}, u32[]{:S(2)}) copy-start(f32[64,3072]{1,0:T(8,128)} %weight_ref.1) | copy-start | bytes 2359300
  2.4 15.0 %all-to-all-start = ((f32[32,1,984]{2,1,0:T(1,128)}), f32[32,1,984]{2,1,0:T(1,128)S(1)}, u32[]{:S(2)}, u32[]{:S(2)}) async-start(f32[32,1,984]{2,1,0:T(1,128)} %shard_map.118), calls=%async_computation | async-start | bytes 262144 | tf_op jit(solution)/shard_map/all_to_all | solution.py:161
  10.6 2.7 %copy-start.2 = (f32[3072]{0:T(1024)S(1)}, f32[3072]{0:T(1024)}, u32[]{:S(2)}) copy-start(f32[3072]{0:T(1024)} %param.14) | copy-start | bytes 36868
  10.6 2.7 %copy-start.5 = (f32[64]{0:T(128)S(1)}, f32[64]{0:T(128)}, u32[]{:S(2)}) copy-start(f32[64]{0:T(128)} %param.16) | copy-start | bytes 772
  19.0 1.2 %copy-start.9 = (f32[3,3,3,16,512]{4,3,2,1,0:T(8,128)S(1)}, f32[3,3,3,16,512]{4,3,2,1,0:T(8,128)}, u32[]{:S(2)}) copy-start(f32[3,3,3,16,512]{4,3,2,1,0:T(8,128)} %param.18) | copy-start | bytes 2654212
  19.0 1.2 %copy-start.10 = (pred[8,2]{0,1:T(4,128)(4,1)S(1)}, pred[8,2]{0,1:T(4,128)(4,1)}, u32[]{:S(2)}) copy-start(pred[8,2]{0,1:T(4,128)(4,1)} %constant.78) | copy-start | bytes 52
  20.2 1.1 %copy-start.3 = (f32[512]{0:T(512)S(1)}, f32[512]{0:T(512)}, u32[]{:S(2)}) copy-start(f32[512]{0:T(512)} %param.19) | copy-start | bytes 6148
  22.9 0.9 %copy-start.4 = (f32[64]{0:T(128)S(1)}, f32[64]{0:T(128)}, u32[]{:S(2)}) copy-start(f32[64]{0:T(128)} %param.21) | copy-start | bytes 772
  22.9 0.9 %copy-start.8 = (pred[8,4]{0,1:T(4,128)(4,1)S(1)}, pred[8,4]{0,1:T(4,128)(4,1)}, u32[]{:S(2)}) copy-start(pred[8,4]{0,1:T(4,128)(4,1)} %constant.77) | copy-start | bytes 100
  23.8 11.7 %copy-start.6 = (f32[64]{0:T(128)S(1)}, f32[64]{0:T(128)}, u32[]{:S(2)}) copy-start(f32[64]{0:T(128)} %param.23) | copy-start | bytes 772
  23.8 11.6 %copy-start.7 = (f32[64]{0:T(128)S(1)}, f32[64]{0:T(128)}, u32[]{:S(2)}) copy-start(f32[64]{0:T(128)} %param.22) | copy-start | bytes 772
  27.2 7.8 %all-to-all-start.1 = ((f32[8,1,16]{2,1,0:T(1,128)}), f32[8,1,16]{2,1,0:T(1,128)S(1)}, u32[]{:S(2)}, u32[]{:S(2)}) async-start(f32[8,1,16]{2,1,0:T(1,128)} %broadcast_in_dim.66), calls=%async_computation.1 | async-start | bytes 8192 | tf_op jit(solution)/shard_map/all_to_all | solution.py:240

commit v11 on v10

--- a/solution.py
+++ b/solution.py
@@ -227,23 +227,26 @@
     mixed = valid_conv(upsampled, conv_weight, "DHWOI", None) + conv_bias
 
     group_size = CO // GROUPS
-    local_groups = mixed.shape[-1] // group_size
-    grouped = mixed.reshape(-1, local_groups, group_size)
-    block_count = grouped.shape[0] * group_size
-    block_mean = jnp.sum(grouped, axis=(0, 2)) / block_count
-    deviation = grouped - block_mean[None, :, None]
-    block_m2 = jnp.sum(deviation * deviation, axis=(0, 2))
+    local_chan = mixed.shape[-1]
+    local_groups = local_chan // group_size
+    flat = mixed.reshape(-1, local_chan)
+    cell_count = flat.shape[0]
+    chan_mean = jnp.sum(flat, axis=0) / cell_count
+    deviation = flat - chan_mean[None, :]
+    chan_m2 = jnp.sum(deviation * deviation, axis=0)
     n_blocks = n_sec * n_sp
     stats = jnp.broadcast_to(
-        jnp.concatenate([block_mean, block_m2])[None], (n_blocks, 2 * local_groups)
+        jnp.concatenate([chan_mean, chan_m2])[None], (n_blocks, 2 * local_chan)
     )
     stats = lax.all_to_all(stats, BLOCKS, 0, 0, tiled=False)
-    group_mean = jnp.mean(stats[:, :local_groups], axis=0)
-    mean_offsets = stats[:, :local_groups] - group_mean[None]
+    means = stats[:, :local_chan].reshape(n_blocks, local_groups, group_size)
+    m2s = stats[:, local_chan:].reshape(n_blocks, local_groups, group_size)
+    group_mean = jnp.mean(means, axis=(0, 2))
+    mean_offsets = means - group_mean[None, :, None]
     group_var = (
-        jnp.sum(stats[:, local_groups:], axis=0)
-        + block_count * jnp.sum(mean_offsets * mean_offsets, axis=0)
-    ) / (block_count * n_blocks)
+        jnp.sum(m2s, axis=(0, 2)) + cell_count * jnp.sum(mean_offsets * mean_offsets, axis=(0, 2))
+    ) / (cell_count * n_blocks * group_size)
+    grouped = mixed.reshape(-1, local_groups, group_size)
 
     normed = (
         (grouped - group_mean[None, :, None]) * lax.rsqrt(group_var + 1e-06)[None, :, None]

time: 36.7 us -> 36.8 us (level)
  no operation moved by 1% of the time
where the time goes in v11:
time: 36.8 us; the launch traced here: 36.4 us
  starting transfers between devices  10.6 us (29%)
  waiting for transfers between devices  7.77 us (21%)
  local copies, waits for them, and re-layouts  7.44 us (20%)
  matrix products  3.96 us (11%)
  other arithmetic  3.85 us (10%)
  Pallas kernels  2.35 us (6%)
  between operations  0.44 us (1%)
    all_to_all x1, starting transfers between devices, per_device(): lax.all_to_all(send, ALL, 0, 0, tiled=False).reshape(n_sec, n_sp, n_rep, -1)  7.3 us
    all_to_all x1, waiting for transfers between devices, per_device(): stats = lax.all_to_all(stats, BLOCKS, 0, 0, tiled=False)  4.45 us
    all_to_all x1, waiting for transfers between devices, per_device(): lax.all_to_all(send, ALL, 0, 0, tiled=False).reshape(n_sec, n_sp, n_rep, -1)  3.32 us
    all_to_all x1, starting transfers between devices, per_device(): stats = lax.all_to_all(stats, BLOCKS, 0, 0, tiled=False)  3.31 us
    conv_general_dilated x2, matrix products, valid_conv(): lax.conv_general_dilated(front[None], kernel, (1, 1, 1), 'VALID', dimensi...  2.95 us
    pallas_call x1, Pallas kernels, shard_moments(): pl.pallas_call(shard_kernel, grid_spec=pltpu.PrefetchScalarGridSpec(num_s...  2.35 us
    reshape x1, local copies, waits for them, and re-layouts, per_device(): scaled_weight.reshape(out_width, n_rep, local_width)  1.51 us
    mul x1, other arithmetic, per_device(): scaled_weight = proj_weight * (1.0 + mod_scale)[None, :]  0.94 us
  transfers between devices with their start and end apart: 2, of which 2 were waited for; matrix products, arithmetic and copies ran while one was open for 12% of the time, Pallas kernels for 0%

profile of v11, /device:TPU:0, one launch (start us, length us, event | category | flops | bytes accessed | tf_op | source)
XLA Modules:
  0.0 36.4 jit_solution(2788629766282536495)
XLA Ops:
  0.0 2.3 %shard_map.118 = f32[32,1,984]{2,1,0:T(1,128)} custom-call(s32[1]{0:T(128)} %bitcast.rep_ref, f32[1,6,2,768]{3,2,1,0:T(2,128)} %bitcast.88, f32[64,3072]{1,0:T(8,128)} %weight_ref.1, f32[1,3072]{1,0:T(1,128)} %bitcast.87, f32[24,2,16]{2,1,0:T(2,128)} %bitcast.89), custom_call_target="tpu_custom_call" | custom-call | tf_op jit(solution)/shard_map/pallas_call | solution.py:76
  2.4 7.3 %all-to-all-start = ((f32[32,1,984]{2,1,0:T(1,128)}), f32[32,1,984]{2,1,0:T(1,128)S(1)}, u32[]{:S(2)}, u32[]{:S(2)}) async-start(f32[32,1,984]{2,1,0:T(1,128)} %shard_map.118), calls=%async_computation | async-start | bytes 262144 | tf_op jit(solution)/shard_map/all_to_all | solution.py:161
  9.7 0.7 %broadcast_add_fusion = f32[3072]{0:T(1024)S(1)} fusion(f32[3072]{0:T(1024)} %param.13), kind=kLoop, calls=%fused_computation.55 | loop fusion | flops 3072 | bytes 24576 | tf_op jit(solution)/shard_map/add | solution.py:163
  10.6 0.9 %broadcast_multiply_fusion = f32[64,3072]{1,0:T(8,128)} fusion(f32[64,3072]{1,0:T(8,128)S(1)} %copy-done.1, f32[3072]{0:T(1024)S(1)} %broadcast_add_fusion), kind=kLoop, calls=%fused_computation.23 | loop fusion | flops 196608 | bytes 1585152 | tf_op jit(solution)/shard_map/mul | solution.py:163
  11.6 1.5 %reshape.248 = f32[64,4,768]{2,1,0:T(4,128)S(1)} reshape(f32[64,3072]{1,0:T(8,128)} %broadcast_multiply_fusion) | data formatting | bytes 1572864 | tf_op jit(solution)/shard_map/reshape | solution.py:164
  13.1 0.2 reduce_sum.115
  13.3 0.7 %fusion.14 = f32[64]{0:T(128)S(1)} fusion(f32[64]{0:T(128)S(1)} %copy-done.5, f32[64,3072]{1,0:T(8,128)S(1)} %copy-done.1, f32[3072,1]{0,1:T(1,128)S(1)} %bitcast.90), kind=kOutput, calls=%fused_computation.15 | convolution fusion | flops 2359360 | bytes 799232 | tf_op jit(solution)/shard_map/dot_general | solution.py:166
  14.1 3.3 %all-to-all-done = f32[32,1,984]{2,1,0:T(1,128)S(1)} async-done(((f32[32,1,984]{2,1,0:T(1,128)}), f32[32,1,984]{2,1,0:T(1,128)S(1)}, u32[]{:S(2)}, u32[]{:S(2)}) %all-to-all-start) | async-done | bytes 125984 | tf_op jit(solution)/shard_map/all_to_all | solution.py:161
  17.4 0.3 reduce.14
  17.8 0.2 reshape.247
  18.0 0.3 slice_reduce_fusion.1
  18.5 0.3 fusion.13
  18.8 0.2 copy.73
  19.0 0.4 %copy.74 = f32[2,2,2,3,6,2,16]{6,2,1,5,4,3,0:T(2,128)S(1)} copy(f32[2,2,2,3,6,2,16]{4,5,2,6,1,0,3:T(2,128)S(1)} %bitcast.77) | data formatting | bytes 36864 | tf_op jit(solution)/shard_map/mul | solution.py:206
  19.5 0.2 reshape.245
  20.0 0.2 copy-done.9
  20.2 1.0 %convolution_select_fusion = f32[2,4,8,2,512]{4,2,3,1,0:T(8,128)S(1)} fusion(f32[3,3,3,16,512]{4,3,2,1,0:T(8,128)S(1)} %copy-done.9, f32[4,6,1,7,2,16]{5,3,4,1,0,2:T(8,128)S(1)} %slice.64, f32[4,6,1,8,2,16]{5,3,4,1,0,2:T(8,128)S(1)} %copy.77, pred[8,2]{0,1:T(4,128)(4,1)S(1)} %copy-done.10), kind=kOutput, calls=%fused_computation.8 | convolution fusion | flops 169971712 | bytes 1192976 | tf_op jit(solution)/shard_map/conv_general_dilated | solution.py:21
  21.1 0.2 copy.78
  21.5 0.1 pad_maximum_fusion.1
  21.6 0.3 broadcast_in_dim.39
  21.9 0.2 reshape.249
  22.2 0.2 slice_bitcast_fusion
  22.4 0.5 %copy.88 = bf16[4,6,1,26,512]{4,0,3,1,2:T(4,128)(2,1)S(1)} copy(bf16[4,6,1,26,512]{4,1,3,0,2:T(8,128)(2,1)S(1)} %slice_bitcast_fusion) | data formatting | bytes 1277952
  22.9 0.3 pad.16.clone
  23.2 0.4 %copy.81 = bf16[4,6,1,8,4,512]{5,3,4,1,0,2:T(8,128)(2,1)S(1)} copy(bf16[4,6,1,8,4,512]{5,0,4,3,1,2:T(4,128)(2,1)S(1)} %bitcast.76) | data formatting | bytes 1572864 | tf_op jit(solution)/shard_map/conv_general_dilated | solution.py:21
  23.8 2.0 %select_reduce_fusion.1 = (f32[64]{0:T(128)S(1)}, f32[2,4,8,4,64]{4,2,3,1,0:T(8,128)S(1)}) fusion(f32[64]{0:T(128)S(1)} %copy-done.4, pred[8,4]{0,1:T(4,128)(4,1)S(1)} %copy-done.8, bf16[3,3,3,64,512]{4,3,2,1,0:T(8,128)(2,1)S(1)} %copy-done, bf16[4,6,1,7,2,512]{5,3,4,1,0,2:T(8,128)(2,1)S(1)} %slice.68, bf16[4,6,1,8,4,512]{5,3,4,1,0,2:T(8,128)(2,1)S(1)} %copy.81), kind=kOutput, calls=%fused_computation.40 | convolution fusion | flops 456589248 | bytes 2966048 | tf_op jit(solution)/shard_map/conv_general_dilated | solution.py:21
  26.0 0.6 %broadcast_in_dim.66 = f32[8,1,128]{2,1,0:T(1,128)} broadcast(f32[128]{0:T(128)S(1)} %pad_maximum_fusion.2), dimensions={2} | broadcast | bytes 4608 | tf_op jit(solution)/shard_map/broadcast_in_dim | solution.py:238
  26.6 3.3 %all-to-all-start.1 = ((f32[8,1,128]{2,1,0:T(1,128)}), f32[8,1,128]{2,1,0:T(1,128)S(1)}, u32[]{:S(2)}, u32[]{:S(2)}) async-start(f32[8,1,128]{2,1,0:T(1,128)} %broadcast_in_dim.66), calls=%async_computation.1 | async-start | bytes 8192 | tf_op jit(solution)/shard_map/all_to_all | solution.py:241
  30.0 4.4 %all-to-all-done.1 = f32[8,1,128]{2,1,0:T(1,128)S(1)} async-done(((f32[8,1,128]{2,1,0:T(1,128)}), f32[8,1,128]{2,1,0:T(1,128)S(1)}, u32[]{:S(2)}, u32[]{:S(2)}) %all-to-all-start.1) | async-done | bytes 4128 | tf_op jit(solution)/shard_map/all_to_all | solution.py:241
  35.2 0.1 reduce_sum.126
  35.5 0.2 copy.83
  35.7 0.7 %copy.84 = f32[4,24,128]{2,1,0:T(8,128)} copy(f32[4,24,128]{1,2,0:T(8,128)S(1)} %bitcast.78) | data formatting | bytes 98304 | tf_op jit(solution)/shard_map/reshape | solution.py:256
  (67 shorter events, 2.4 us)
Async XLA Ops:
  0.0 23.7 %copy-start = (bf16[3,3,3,64,512]{4,3,2,1,0:T(8,128)(2,1)S(1)}, bf16[3,3,3,64,512]{4,3,2,1,0:T(8,128)(2,1)}, u32[]{:S(2)}) copy-start(bf16[3,3,3,64,512]{4,3,2,1,0:T(8,128)(2,1)} %param.20) | copy-start | bytes 5308420
  0.0 10.6 %copy-start.1 = (f32[64,3072]{1,0:T(8,128)S(1)}, f32[64,3072]{1,0:T(8,128)}, u32[]{:S(2)}) copy-start(f32[64,3072]{1,0:T(8,128)} %weight_ref.1) | copy-start | bytes 2359300
  2.4 15.0 %all-to-all-start = ((f32[32,1,984]{2,1,0:T(1,128)}), f32[32,1,984]{2,1,0:T(1,128)S(1)}, u32[]{:S(2)}, u32[]{:S(2)}) async-start(f32[32,1,984]{2,1,0:T(1,128)} %shard_map.118), calls=%async_computation | async-start | bytes 262144 | tf_op jit(solution)/shard_map/all_to_all | solution.py:161
  10.6 2.7 %copy-start.2 = (f32[3072]{0:T(1024)S(1)}, f32[3072]{0:T(1024)}, u32[]{:S(2)}) copy-start(f32[3072]{0:T(1024)} %param.14) | copy-start | bytes 36868
  10.6 2.7 %copy-start.5 = (f32[64]{0:T(128)S(1)}, f32[64]{0:T(128)}, u32[]{:S(2)}) copy-start(f32[64]{0:T(128)} %param.16) | copy-start | bytes 772
  19.0 1.2 %copy-start.9 = (f32[3,3,3,16,512]{4,3,2,1,0:T(8,128)S(1)}, f32[3,3,3,16,512]{4,3,2,1,0:T(8,128)}, u32[]{:S(2)}) copy-start(f32[3,3,3,16,512]{4,3,2,1,0:T(8,128)} %param.18) | copy-start | bytes 2654212
  19.0 1.2 %copy-start.10 = (pred[8,2]{0,1:T(4,128)(4,1)S(1)}, pred[8,2]{0,1:T(4,128)(4,1)}, u32[]{:S(2)}) copy-start(pred[8,2]{0,1:T(4,128)(4,1)} %constant.79) | copy-start | bytes 52
  20.2 1.1 %copy-start.3 = (f32[512]{0:T(512)S(1)}, f32[512]{0:T(512)}, u32[]{:S(2)}) copy-start(f32[512]{0:T(512)} %param.19) | copy-start | bytes 6148
  22.9 0.9 %copy-start.4 = (f32[64]{0:T(128)S(1)}, f32[64]{0:T(128)}, u32[]{:S(2)}) copy-start(f32[64]{0:T(128)} %param.21) | copy-start | bytes 772
  22.9 0.9 %copy-start.8 = (pred[8,4]{0,1:T(4,128)(4,1)S(1)}, pred[8,4]{0,1:T(4,128)(4,1)}, u32[]{:S(2)}) copy-start(pred[8,4]{0,1:T(4,128)(4,1)} %constant.78) | copy-start | bytes 100
  23.8 11.7 %copy-start.6 = (f32[64]{0:T(128)S(1)}, f32[64]{0:T(128)}, u32[]{:S(2)}) copy-start(f32[64]{0:T(128)} %param.23) | copy-start | bytes 772
  23.8 11.7 %copy-start.7 = (f32[64]{0:T(128)S(1)}, f32[64]{0:T(128)}, u32[]{:S(2)}) copy-start(f32[64]{0:T(128)} %param.22) | copy-start | bytes 772
  26.6 7.8 %all-to-all-start.1 = ((f32[8,1,128]{2,1,0:T(1,128)}), f32[8,1,128]{2,1,0:T(1,128)S(1)}, u32[]{:S(2)}, u32[]{:S(2)}) async-start(f32[8,1,128]{2,1,0:T(1,128)} %broadcast_in_dim.66), calls=%async_computation.1 | async-start | bytes 8192 | tf_op jit(solution)/shard_map/all_to_all | solution.py:241

commit v12 on v11

--- a/solution.py
+++ b/solution.py
@@ -160,17 +160,24 @@
         ).reshape(n_dev, -1)
     received = lax.all_to_all(send, ALL, 0, 0, tiled=False).reshape(n_sec, n_sp, n_rep, -1)
 
-    scaled_weight = proj_weight * (1.0 + mod_scale)[None, :]
-    shard_columns = jnp.sum(scaled_weight.reshape(out_width, n_rep, local_width), axis=2).T
-    shift_column = (
-        jnp.dot(
-            proj_weight,
-            mod_shift,
-            precision=lax.Precision.HIGHEST,
-            preferred_element_type=jnp.float32,
-        )
-        + proj_bias
-    )
+    shard_of = jnp.arange(full_width) // local_width
+    selector = jnp.concatenate(
+        [
+            jnp.where(
+                shard_of[:, None] == jnp.arange(n_rep)[None, :], (1.0 + mod_scale)[:, None], 0.0
+            ),
+            mod_shift[:, None],
+        ],
+        axis=1,
+    )
+    folded = jnp.dot(
+        proj_weight,
+        selector,
+        precision=lax.Precision.HIGHEST,
+        preferred_element_type=jnp.float32,
+    )
+    shard_columns = folded[:, :n_rep].T
+    shift_column = folded[:, n_rep] + proj_bias
     parts = neighbours(received[..., :part_size], sec, 0).reshape(
         3, n_sp, n_rep, tok_frames, window, band_cols, out_width + 2
     )

time: 36.8 us -> 36.9 us (level)
  waiting for transfers between devices: 7.77 us -> 9.63 us
  local copies, waits for them, and re-layouts: 7.44 us -> 5.98 us
  other arithmetic: 3.85 us -> 2.79 us
  matrix products: 3.96 us -> 4.63 us
    all_to_all x1, waiting for transfers between devices: 3.32 us -> 5.18 us  [per_device(): lax.all_to_all(send, ALL, 0, 0, tiled=False).reshape(n_sec, n_sp, n_rep, -1)]
    reshape x1 -> x0, local copies, waits for them, and re-layouts: 1.51 us -> none  [per_device(): scaled_weight.reshape(out_width, n_rep, local_width)]
    mul x1 -> x0, other arithmetic: 0.94 us -> none  [per_device(): scaled_weight = proj_weight * (1.0 + mod_scale)[None, :]]
    dot_general x1, matrix products: 0.73 us -> 1.42 us  [per_device(): jnp.dot(proj_weight, selector, precision=lax.Precision.HIGHEST, preferred...]
    unnamed x23 -> x21, local copies, waits for them, and re-layouts: 0.74 us -> 0.78 us
  transfers between devices with their start and end apart: 2 -> 2, of which waited for: 2 -> 2; matrix products, arithmetic and copies ran while one was open for 12% -> 7% of each run, Pallas kernels for 0% -> 0%
where the time goes in v12:
time: 36.9 us; the launch traced here: 36.5 us
  starting transfers between devices  10.6 us (29%)
  waiting for transfers between devices  9.63 us (26%)
  local copies, waits for them, and re-layouts  5.98 us (16%)
  matrix products  4.63 us (13%)
  other arithmetic  2.79 us (8%)
  Pallas kernels  2.34 us (6%)
  between operations  0.47 us (1%)
    all_to_all x1, starting transfers between devices, per_device(): lax.all_to_all(send, ALL, 0, 0, tiled=False).reshape(n_sec, n_sp, n_rep, -1)  7.31 us
    all_to_all x1, waiting for transfers between devices, per_device(): lax.all_to_all(send, ALL, 0, 0, tiled=False).reshape(n_sec, n_sp, n_rep, -1)  5.18 us
    all_to_all x1, waiting for transfers between devices, per_device(): stats = lax.all_to_all(stats, BLOCKS, 0, 0, tiled=False)  4.45 us
    all_to_all x1, starting transfers between devices, per_device(): stats = lax.all_to_all(stats, BLOCKS, 0, 0, tiled=False)  3.31 us
    conv_general_dilated x2, matrix products, valid_conv(): lax.conv_general_dilated(front[None], kernel, (1, 1, 1), 'VALID', dimensi...  2.94 us
    pallas_call x1, Pallas kernels, shard_moments(): pl.pallas_call(shard_kernel, grid_spec=pltpu.PrefetchScalarGridSpec(num_s...  2.34 us
    dot_general x1, matrix products, per_device(): jnp.dot(proj_weight, selector, precision=lax.Precision.HIGHEST, preferred...  1.42 us
    unnamed x21, local copies, waits for them, and re-layouts  0.78 us
  transfers between devices with their start and end apart: 2, of which 2 were waited for; matrix products, arithmetic and copies ran while one was open for 7% of the time, Pallas kernels for 0%

profile of v12, /device:TPU:0, one launch (start us, length us, event | category | flops | bytes accessed | tf_op | source)
XLA Modules:
  0.0 36.5 jit_solution(11428357593559137725)
XLA Ops:
  0.0 2.3 %shard_map.118 = f32[32,1,984]{2,1,0:T(1,128)} custom-call(s32[1]{0:T(128)} %bitcast.rep_ref, f32[1,6,2,768]{3,2,1,0:T(2,128)} %bitcast.89, f32[64,3072]{1,0:T(8,128)} %weight_ref.1, f32[1,3072]{1,0:T(1,128)} %bitcast.88, f32[24,2,16]{2,1,0:T(2,128)} %bitcast.90), custom_call_target="tpu_custom_call" | custom-call | tf_op jit(solution)/shard_map/pallas_call | solution.py:76
  2.3 7.3 %all-to-all-start = ((f32[32,1,984]{2,1,0:T(1,128)}), f32[32,1,984]{2,1,0:T(1,128)S(1)}, u32[]{:S(2)}, u32[]{:S(2)}) async-start(f32[32,1,984]{2,1,0:T(1,128)} %shard_map.118), calls=%async_computation | async-start | bytes 262144 | tf_op jit(solution)/shard_map/all_to_all | solution.py:161
  9.9 0.7 %broadcast_add_fusion = f32[3072]{0:T(1024)S(1)} fusion(f32[3072]{0:T(1024)} %param.13), kind=kLoop, calls=%fused_computation.64 | loop fusion | flops 3072 | bytes 24576 | tf_op jit(solution)/shard_map/add | solution.py:167
  10.7 1.4 %convolution_bitcast_fusion = f32[64,5]{0,1:T(8,128)S(1)} fusion(f32[64,3072]{1,0:T(8,128)S(1)} %copy-done.1, f32[3072,1]{0,1:T(1,128)} %bitcast.91, f32[3072,4]{0,1:T(4,128)S(1)} %fusion.33), kind=kOutput, calls=%fused_computation.14 | convolution fusion | flops 11811840 | bytes 849152 | tf_op jit(solution)/shard_map/dot_general | solution.py:173
  12.2 5.2 %all-to-all-done = f32[32,1,984]{2,1,0:T(1,128)S(1)} async-done(((f32[32,1,984]{2,1,0:T(1,128)}), f32[32,1,984]{2,1,0:T(1,128)S(1)}, u32[]{:S(2)}, u32[]{:S(2)}) %all-to-all-start) | async-done | bytes 125984 | tf_op jit(solution)/shard_map/all_to_all | solution.py:161
  17.4 0.3 reduce.14
  17.9 0.2 reshape.257
  18.1 0.3 slice_reduce_fusion.1
  18.5 0.2 reshape.255
  18.8 0.3 fusion.13
  19.1 0.2 copy.72
  19.3 0.4 %copy.73 = f32[2,2,2,3,6,2,16]{6,2,1,5,4,3,0:T(2,128)S(1)} copy(f32[2,2,2,3,6,2,16]{4,5,2,6,1,0,3:T(2,128)S(1)} %bitcast.78) | data formatting | bytes 36864 | tf_op jit(solution)/shard_map/mul | solution.py:213
  20.0 0.2 copy-done.7
  20.2 0.9 %convolution_select_fusion = f32[2,4,8,2,512]{4,2,3,1,0:T(8,128)S(1)} fusion(f32[3,3,3,16,512]{4,3,2,1,0:T(8,128)S(1)} %copy-done.7, f32[4,6,1,7,2,16]{5,3,4,1,0,2:T(8,128)S(1)} %slice.72, f32[4,6,1,8,2,16]{5,3,4,1,0,2:T(8,128)S(1)} %copy.76, pred[8,2]{0,1:T(4,128)(4,1)S(1)} %copy-done.9), kind=kOutput, calls=%fused_computation.8 | convolution fusion | flops 169971712 | bytes 1192976 | tf_op jit(solution)/shard_map/conv_general_dilated | solution.py:21
  21.2 0.2 copy.77
  21.5 0.1 pad_maximum_fusion.1
  21.6 0.3 broadcast_in_dim.83
  21.9 0.2 reshape.258
  22.2 0.2 slice_bitcast_fusion
  22.4 0.5 %copy.86 = bf16[4,6,1,26,512]{4,0,3,1,2:T(4,128)(2,1)S(1)} copy(bf16[4,6,1,26,512]{4,1,3,0,2:T(8,128)(2,1)S(1)} %slice_bitcast_fusion) | data formatting | bytes 1277952
  22.9 0.3 pad.16.clone
  23.2 0.4 %copy.80 = bf16[4,6,1,8,4,512]{5,3,4,1,0,2:T(8,128)(2,1)S(1)} copy(bf16[4,6,1,8,4,512]{5,0,4,3,1,2:T(4,128)(2,1)S(1)} %bitcast.77) | data formatting | bytes 1572864 | tf_op jit(solution)/shard_map/conv_general_dilated | solution.py:21
  23.8 2.0 %select_reduce_fusion.1 = (f32[64]{0:T(128)S(1)}, f32[2,4,8,4,64]{4,2,3,1,0:T(8,128)S(1)}) fusion(f32[64]{0:T(128)S(1)} %copy-done.3, pred[8,4]{0,1:T(4,128)(4,1)S(1)} %copy-done.6, bf16[3,3,3,64,512]{4,3,2,1,0:T(8,128)(2,1)S(1)} %copy-done, bf16[4,6,1,7,2,512]{5,3,4,1,0,2:T(8,128)(2,1)S(1)} %slice.76, bf16[4,6,1,8,4,512]{5,3,4,1,0,2:T(8,128)(2,1)S(1)} %copy.80), kind=kOutput, calls=%fused_computation.38 | convolution fusion | flops 456589248 | bytes 2966048 | tf_op jit(solution)/shard_map/conv_general_dilated | solution.py:21
  25.8 0.1 select_reduce_fusion
  26.0 0.6 %broadcast_in_dim.86 = f32[8,1,128]{2,1,0:T(1,128)} broadcast(f32[128]{0:T(128)S(1)} %pad_maximum_fusion.2), dimensions={2} | broadcast | bytes 4608 | tf_op jit(solution)/shard_map/broadcast_in_dim | solution.py:245
  26.6 3.3 %all-to-all-start.1 = ((f32[8,1,128]{2,1,0:T(1,128)}), f32[8,1,128]{2,1,0:T(1,128)S(1)}, u32[]{:S(2)}, u32[]{:S(2)}) async-start(f32[8,1,128]{2,1,0:T(1,128)} %broadcast_in_dim.86), calls=%async_computation.1 | async-start | bytes 8192 | tf_op jit(solution)/shard_map/all_to_all | solution.py:248
  30.0 4.4 %all-to-all-done.1 = f32[8,1,128]{2,1,0:T(1,128)S(1)} async-done(((f32[8,1,128]{2,1,0:T(1,128)}), f32[8,1,128]{2,1,0:T(1,128)S(1)}, u32[]{:S(2)}, u32[]{:S(2)}) %all-to-all-start.1) | async-done | bytes 4128 | tf_op jit(solution)/shard_map/all_to_all | solution.py:248
  34.5 0.1 reduce_sum.110
  35.0 0.1 reduce_sum.116
  35.2 0.1 reduce_sum.113
  35.6 0.2 copy.82
  35.7 0.7 %copy.83 = f32[4,24,128]{2,1,0:T(8,128)} copy(f32[4,24,128]{1,2,0:T(8,128)S(1)} %bitcast.79) | data formatting | bytes 98304 | tf_op jit(solution)/shard_map/reshape | solution.py:263
  (65 shorter events, 2.1 us)
Async XLA Ops:
  0.0 23.8 %copy-start = (bf16[3,3,3,64,512]{4,3,2,1,0:T(8,128)(2,1)S(1)}, bf16[3,3,3,64,512]{4,3,2,1,0:T(8,128)(2,1)}, u32[]{:S(2)}) copy-start(bf16[3,3,3,64,512]{4,3,2,1,0:T(8,128)(2,1)} %param.20) | copy-start | bytes 5308420
  0.0 10.7 %copy-start.1 = (f32[64,3072]{1,0:T(8,128)S(1)}, f32[64,3072]{1,0:T(8,128)}, u32[]{:S(2)}) copy-start(f32[64,3072]{1,0:T(8,128)} %weight_ref.1) | copy-start | bytes 2359300
  0.0 12.2 %copy-start.8 = (f32[64]{0:T(128)S(1)}, f32[64]{0:T(128)}, u32[]{:S(2)}) copy-start(f32[64]{0:T(128)} %param.16) | copy-start | bytes 772
  2.3 15.1 %all-to-all-start = ((f32[32,1,984]{2,1,0:T(1,128)}), f32[32,1,984]{2,1,0:T(1,128)S(1)}, u32[]{:S(2)}, u32[]{:S(2)}) async-start(f32[32,1,984]{2,1,0:T(1,128)} %shard_map.118), calls=%async_computation | async-start | bytes 262144 | tf_op jit(solution)/shard_map/all_to_all | solution.py:161
  19.1 1.2 %copy-start.7 = (f32[3,3,3,16,512]{4,3,2,1,0:T(8,128)S(1)}, f32[3,3,3,16,512]{4,3,2,1,0:T(8,128)}, u32[]{:S(2)}) copy-start(f32[3,3,3,16,512]{4,3,2,1,0:T(8,128)} %param.18) | copy-start | bytes 2654212
  19.1 1.2 %copy-start.9 = (pred[8,2]{0,1:T(4,128)(4,1)S(1)}, pred[8,2]{0,1:T(4,128)(4,1)}, u32[]{:S(2)}) copy-start(pred[8,2]{0,1:T(4,128)(4,1)} %constant.89) | copy-start | bytes 52
  20.2 1.1 %copy-start.2 = (f32[512]{0:T(512)S(1)}, f32[512]{0:T(512)}, u32[]{:S(2)}) copy-start(f32[512]{0:T(512)} %param.19) | copy-start | bytes 6148
  22.9 0.9 %copy-start.3 = (f32[64]{0:T(128)S(1)}, f32[64]{0:T(128)}, u32[]{:S(2)}) copy-start(f32[64]{0:T(128)} %param.21) | copy-start | bytes 772
  22.9 0.9 %copy-start.6 = (pred[8,4]{0,1:T(4,128)(4,1)S(1)}, pred[8,4]{0,1:T(4,128)(4,1)}, u32[]{:S(2)}) copy-start(pred[8,4]{0,1:T(4,128)(4,1)} %constant.88) | copy-start | bytes 100
  23.8 11.7 %copy-start.4 = (f32[64]{0:T(128)S(1)}, f32[64]{0:T(128)}, u32[]{:S(2)}) copy-start(f32[64]{0:T(128)} %param.23) | copy-start | bytes 772
  23.8 11.7 %copy-start.5 = (f32[64]{0:T(128)S(1)}, f32[64]{0:T(128)}, u32[]{:S(2)}) copy-start(f32[64]{0:T(128)} %param.22) | copy-start | bytes 772
  26.6 7.8 %all-to-all-start.1 = ((f32[8,1,128]{2,1,0:T(1,128)}), f32[8,1,128]{2,1,0:T(1,128)S(1)}, u32[]{:S(2)}, u32[]{:S(2)}) async-start(f32[8,1,128]{2,1,0:T(1,128)} %broadcast_in_dim.86), calls=%async_computation.1 | async-start | bytes 8192 | tf_op jit(solution)/shard_map/all_to_all | solution.py:248

commit v13 on v12

--- a/solution.py
+++ b/solution.py
@@ -246,19 +246,20 @@
         jnp.concatenate([chan_mean, chan_m2])[None], (n_blocks, 2 * local_chan)
     )
     stats = lax.all_to_all(stats, BLOCKS, 0, 0, tiled=False)
-    means = stats[:, :local_chan].reshape(n_blocks, local_groups, group_size)
-    m2s = stats[:, local_chan:].reshape(n_blocks, local_groups, group_size)
-    group_mean = jnp.mean(means, axis=(0, 2))
-    mean_offsets = means - group_mean[None, :, None]
-    group_var = (
-        jnp.sum(m2s, axis=(0, 2)) + cell_count * jnp.sum(mean_offsets * mean_offsets, axis=(0, 2))
-    ) / (cell_count * n_blocks * group_size)
-    grouped = mixed.reshape(-1, local_groups, group_size)
-
-    normed = (
-        (grouped - group_mean[None, :, None]) * lax.rsqrt(group_var + 1e-06)[None, :, None]
-    ).reshape(mixed.shape)
-    activated = jax.nn.silu(normed * norm_gain + norm_bias)
+    means = stats[:, :local_chan]
+    group_mean = jnp.sum(means, axis=0).reshape(local_groups, group_size).sum(axis=1) / (
+        n_blocks * group_size
+    )
+    chan_group_mean = jnp.repeat(group_mean, group_size)
+    mean_offsets = means - chan_group_mean[None, :]
+    chan_total = jnp.sum(stats[:, local_chan:], axis=0) + cell_count * jnp.sum(
+        mean_offsets * mean_offsets, axis=0
+    )
+    group_var = chan_total.reshape(local_groups, group_size).sum(axis=1) / (
+        cell_count * n_blocks * group_size
+    )
+    chan_scale = jnp.repeat(lax.rsqrt(group_var + 1e-06), group_size) * norm_gain
+    activated = jax.nn.silu((mixed - chan_group_mean) * chan_scale + norm_bias)
     out_rows, out_cols, out_chan = (activated.shape[1], activated.shape[2], activated.shape[3])
     return activated.transpose(1, 2, 3, 0).reshape(out_rows, out_cols, out_chan * frames)
 

time: 36.9 us -> 36.7 us (level)
  no operation moved by 1% of the time
where the time goes in v13:
time: 36.7 us; the launch traced here: 36.3 us
  starting transfers between devices  10.6 us (29%)
  waiting for transfers between devices  9.63 us (26%)
  local copies, waits for them, and re-layouts  5.9 us (16%)
  matrix products  4.63 us (13%)
  other arithmetic  2.68 us (7%)
  Pallas kernels  2.34 us (6%)
  between operations  0.47 us (1%)
    all_to_all x1, starting transfers between devices, per_device(): lax.all_to_all(send, ALL, 0, 0, tiled=False).reshape(n_sec, n_sp, n_rep, -1)  7.31 us
    all_to_all x1, waiting for transfers between devices, per_device(): lax.all_to_all(send, ALL, 0, 0, tiled=False).reshape(n_sec, n_sp, n_rep, -1)  5.18 us
    all_to_all x1, waiting for transfers between devices, per_device(): stats = lax.all_to_all(stats, BLOCKS, 0, 0, tiled=False)  4.45 us
    all_to_all x1, starting transfers between devices, per_device(): stats = lax.all_to_all(stats, BLOCKS, 0, 0, tiled=False)  3.31 us
    conv_general_dilated x2, matrix products, valid_conv(): lax.conv_general_dilated(front[None], kernel, (1, 1, 1), 'VALID', dimensi...  2.94 us
    pallas_call x1, Pallas kernels, shard_moments(): pl.pallas_call(shard_kernel, grid_spec=pltpu.PrefetchScalarGridSpec(num_s...  2.34 us
    dot_general x1, matrix products, per_device(): jnp.dot(proj_weight, selector, precision=lax.Precision.HIGHEST, preferred...  1.42 us
    unnamed x21, local copies, waits for them, and re-layouts  0.78 us
  transfers between devices with their start and end apart: 2, of which 2 were waited for; matrix products, arithmetic and copies ran while one was open for 7% of the time, Pallas kernels for 0%

profile of v13, /device:TPU:0, one launch (start us, length us, event | category | flops | bytes accessed | tf_op | source)
XLA Modules:
  0.0 36.3 jit_solution(15100563252146147827)
XLA Ops:
  0.0 2.3 %shard_map.118 = f32[32,1,984]{2,1,0:T(1,128)} custom-call(s32[1]{0:T(128)} %bitcast.rep_ref, f32[1,6,2,768]{3,2,1,0:T(2,128)} %bitcast.87, f32[64,3072]{1,0:T(8,128)} %weight_ref.1, f32[1,3072]{1,0:T(1,128)} %bitcast.86, f32[24,2,16]{2,1,0:T(2,128)} %bitcast.88), custom_call_target="tpu_custom_call" | custom-call | tf_op jit(solution)/shard_map/pallas_call | solution.py:76
  2.3 7.3 %all-to-all-start = ((f32[32,1,984]{2,1,0:T(1,128)}), f32[32,1,984]{2,1,0:T(1,128)S(1)}, u32[]{:S(2)}, u32[]{:S(2)}) async-start(f32[32,1,984]{2,1,0:T(1,128)} %shard_map.118), calls=%async_computation | async-start | bytes 262144 | tf_op jit(solution)/shard_map/all_to_all | solution.py:161
  9.9 0.7 %broadcast_add_fusion = f32[3072]{0:T(1024)S(1)} fusion(f32[3072]{0:T(1024)} %param.13), kind=kLoop, calls=%fused_computation.63 | loop fusion | flops 3072 | bytes 24576 | tf_op jit(solution)/shard_map/add | solution.py:167
  10.7 1.4 %convolution_bitcast_fusion = f32[64,5]{0,1:T(8,128)S(1)} fusion(f32[64,3072]{1,0:T(8,128)S(1)} %copy-done.1, f32[3072,1]{0,1:T(1,128)} %bitcast.89, f32[3072,4]{0,1:T(4,128)S(1)} %fusion.32), kind=kOutput, calls=%fused_computation.14 | convolution fusion | flops 11811840 | bytes 849152 | tf_op jit(solution)/shard_map/dot_general | solution.py:173
  12.2 5.2 %all-to-all-done = f32[32,1,984]{2,1,0:T(1,128)S(1)} async-done(((f32[32,1,984]{2,1,0:T(1,128)}), f32[32,1,984]{2,1,0:T(1,128)S(1)}, u32[]{:S(2)}, u32[]{:S(2)}) %all-to-all-start) | async-done | bytes 125984 | tf_op jit(solution)/shard_map/all_to_all | solution.py:161
  17.4 0.3 reduce.8
  17.9 0.2 reshape.243
  18.1 0.3 slice_reduce_fusion.1
  18.5 0.2 reshape.241
  18.8 0.3 fusion.13
  19.1 0.2 copy.72
  19.3 0.4 %copy.73 = f32[2,2,2,3,6,2,16]{6,2,1,5,4,3,0:T(2,128)S(1)} copy(f32[2,2,2,3,6,2,16]{4,5,2,6,1,0,3:T(2,128)S(1)} %bitcast.76) | data formatting | bytes 36864 | tf_op jit(solution)/shard_map/mul | solution.py:213
  20.0 0.2 copy-done.6
  20.2 0.9 %convolution_select_fusion = f32[2,4,8,2,512]{4,2,3,1,0:T(8,128)S(1)} fusion(f32[3,3,3,16,512]{4,3,2,1,0:T(8,128)S(1)} %copy-done.6, f32[4,6,1,7,2,16]{5,3,4,1,0,2:T(8,128)S(1)} %slice.72, f32[4,6,1,8,2,16]{5,3,4,1,0,2:T(8,128)S(1)} %copy.76, pred[8,2]{0,1:T(4,128)(4,1)S(1)} %copy-done.9), kind=kOutput, calls=%fused_computation.8 | convolution fusion | flops 169971712 | bytes 1192976 | tf_op jit(solution)/shard_map/conv_general_dilated | solution.py:21
  21.2 0.2 copy.77
  21.4 0.1 fusion.21
  21.5 0.1 pad_maximum_fusion.1
  21.6 0.3 broadcast_in_dim.86
  21.9 0.2 reshape.244
  22.2 0.2 slice_bitcast_fusion
  22.4 0.5 %copy.86 = bf16[4,6,1,26,512]{4,0,3,1,2:T(4,128)(2,1)S(1)} copy(bf16[4,6,1,26,512]{4,1,3,0,2:T(8,128)(2,1)S(1)} %slice_bitcast_fusion) | data formatting | bytes 1277952
  22.9 0.3 pad.16.clone
  23.2 0.4 %copy.80 = bf16[4,6,1,8,4,512]{5,3,4,1,0,2:T(8,128)(2,1)S(1)} copy(bf16[4,6,1,8,4,512]{5,0,4,3,1,2:T(4,128)(2,1)S(1)} %bitcast.75) | data formatting | bytes 1572864 | tf_op jit(solution)/shard_map/conv_general_dilated | solution.py:21
  23.8 2.0 %select_reduce_fusion.1 = (f32[64]{0:T(128)S(1)}, f32[2,4,8,4,64]{4,2,3,1,0:T(8,128)S(1)}) fusion(f32[64]{0:T(128)S(1)} %copy-done.3, pred[8,4]{0,1:T(4,128)(4,1)S(1)} %copy-done.5, bf16[3,3,3,64,512]{4,3,2,1,0:T(8,128)(2,1)S(1)} %copy-done, bf16[4,6,1,7,2,512]{5,3,4,1,0,2:T(8,128)(2,1)S(1)} %slice.76, bf16[4,6,1,8,4,512]{5,3,4,1,0,2:T(8,128)(2,1)S(1)} %copy.80), kind=kOutput, calls=%fused_computation.38 | convolution fusion | flops 456589248 | bytes 2966048 | tf_op jit(solution)/shard_map/conv_general_dilated | solution.py:21
  25.8 0.1 select_reduce_fusion
  26.0 0.6 %broadcast_in_dim.89 = f32[8,1,128]{2,1,0:T(1,128)} broadcast(f32[128]{0:T(128)S(1)} %pad_maximum_fusion.2), dimensions={2} | broadcast | bytes 4608 | tf_op jit(solution)/shard_map/broadcast_in_dim | solution.py:245
  26.6 3.3 %all-to-all-start.1 = ((f32[8,1,128]{2,1,0:T(1,128)}), f32[8,1,128]{2,1,0:T(1,128)S(1)}, u32[]{:S(2)}, u32[]{:S(2)}) async-start(f32[8,1,128]{2,1,0:T(1,128)} %broadcast_in_dim.89), calls=%async_computation.1 | async-start | bytes 8192 | tf_op jit(solution)/shard_map/all_to_all | solution.py:248
  30.0 4.4 %all-to-all-done.1 = f32[8,1,128]{2,1,0:T(1,128)S(1)} async-done(((f32[8,1,128]{2,1,0:T(1,128)}), f32[8,1,128]{2,1,0:T(1,128)S(1)}, u32[]{:S(2)}, u32[]{:S(2)}) %all-to-all-start.1) | async-done | bytes 4128 | tf_op jit(solution)/shard_map/all_to_all | solution.py:248
  34.5 0.1 reduce_sum.106
  35.0 0.1 reduce_sum.109
  35.4 0.2 copy.82
  35.5 0.7 %copy.83 = f32[4,24,128]{2,1,0:T(8,128)} copy(f32[4,24,128]{1,2,0:T(8,128)S(1)} %bitcast.77) | data formatting | bytes 98304 | tf_op jit(solution)/shard_map/reshape | solution.py:264
  (65 shorter events, 1.9 us)
Async XLA Ops:
  0.0 23.8 %copy-start = (bf16[3,3,3,64,512]{4,3,2,1,0:T(8,128)(2,1)S(1)}, bf16[3,3,3,64,512]{4,3,2,1,0:T(8,128)(2,1)}, u32[]{:S(2)}) copy-start(bf16[3,3,3,64,512]{4,3,2,1,0:T(8,128)(2,1)} %param.20) | copy-start | bytes 5308420
  0.0 10.7 %copy-start.1 = (f32[64,3072]{1,0:T(8,128)S(1)}, f32[64,3072]{1,0:T(8,128)}, u32[]{:S(2)}) copy-start(f32[64,3072]{1,0:T(8,128)} %weight_ref.1) | copy-start | bytes 2359300
  0.0 12.2 %copy-start.7 = (f32[64]{0:T(128)S(1)}, f32[64]{0:T(128)}, u32[]{:S(2)}) copy-start(f32[64]{0:T(128)} %param.16) | copy-start | bytes 772
  2.3 15.1 %all-to-all-start = ((f32[32,1,984]{2,1,0:T(1,128)}), f32[32,1,984]{2,1,0:T(1,128)S(1)}, u32[]{:S(2)}, u32[]{:S(2)}) async-start(f32[32,1,984]{2,1,0:T(1,128)} %shard_map.118), calls=%async_computation | async-start | bytes 262144 | tf_op jit(solution)/shard_map/all_to_all | solution.py:161
  19.1 1.2 %copy-start.6 = (f32[3,3,3,16,512]{4,3,2,1,0:T(8,128)S(1)}, f32[3,3,3,16,512]{4,3,2,1,0:T(8,128)}, u32[]{:S(2)}) copy-start(f32[3,3,3,16,512]{4,3,2,1,0:T(8,128)} %param.18) | copy-start | bytes 2654212
  19.1 1.2 %copy-start.9 = (pred[8,2]{0,1:T(4,128)(4,1)S(1)}, pred[8,2]{0,1:T(4,128)(4,1)}, u32[]{:S(2)}) copy-start(pred[8,2]{0,1:T(4,128)(4,1)} %constant.88) | copy-start | bytes 52
  20.2 1.1 %copy-start.2 = (f32[512]{0:T(512)S(1)}, f32[512]{0:T(512)}, u32[]{:S(2)}) copy-start(f32[512]{0:T(512)} %param.19) | copy-start | bytes 6148
  22.9 0.9 %copy-start.3 = (f32[64]{0:T(128)S(1)}, f32[64]{0:T(128)}, u32[]{:S(2)}) copy-start(f32[64]{0:T(128)} %param.21) | copy-start | bytes 772
  22.9 0.9 %copy-start.5 = (pred[8,4]{0,1:T(4,128)(4,1)S(1)}, pred[8,4]{0,1:T(4,128)(4,1)}, u32[]{:S(2)}) copy-start(pred[8,4]{0,1:T(4,128)(4,1)} %constant.87) | copy-start | bytes 100
  23.8 11.5 %copy-start.8 = (f32[64]{0:T(128)S(1)}, f32[64]{0:T(128)}, u32[]{:S(2)}) copy-start(f32[64]{0:T(128)} %param.22) | copy-start | bytes 772
  23.8 11.5 %copy-start.4 = (f32[64]{0:T(128)S(1)}, f32[64]{0:T(128)}, u32[]{:S(2)}) copy-start(f32[64]{0:T(128)} %param.23) | copy-start | bytes 772
  26.6 7.8 %all-to-all-start.1 = ((f32[8,1,128]{2,1,0:T(1,128)}), f32[8,1,128]{2,1,0:T(1,128)S(1)}, u32[]{:S(2)}, u32[]{:S(2)}) async-start(f32[8,1,128]{2,1,0:T(1,128)} %broadcast_in_dim.89), calls=%async_computation.1 | async-start | bytes 8192 | tf_op jit(solution)/shard_map/all_to_all | solution.py:248

commit v14 on v10

--- a/solution.py
+++ b/solution.py
@@ -32,8 +32,18 @@
 
 def shard_kernel(rep_ref, tok_ref, weight_ref, scale_ref, latent_ref, copies_ref):
     out_ref = copies_ref.at[0]
-    weight = weight_ref[...] * (1.0 + scale_ref[...])
-    width = weight.shape[0]
+    width = weight_ref.shape[0]
+    new = lax.broadcasted_iota(jnp.int32, (width, width), 0)
+    old = lax.broadcasted_iota(jnp.int32, (width, width), 1)
+    quarter = width // 4
+    order = jnp.where(old == 4 * (new % quarter) + new // quarter, 1.0, 0.0)
+    weight = lax.dot_general(
+        order,
+        weight_ref[...] * (1.0 + scale_ref[...]),
+        (((1,), (0,)), ((), ())),
+        precision=lax.Precision.HIGHEST,
+        preferred_element_type=jnp.float32,
+    )
     band_cols = tok_ref.shape[1]
     record = width + 2
     for frame in range(tok_ref.shape[0]):
@@ -171,6 +181,9 @@
         )
         + proj_bias
     )
+    by_parity = lambda v: v.reshape(v.shape[:-1] + (LC, 4)).swapaxes(-1, -2).reshape(v.shape)
+    shard_columns = by_parity(shard_columns)
+    shift_column = by_parity(shift_column)
     parts = neighbours(received[..., :part_size], sec, 0).reshape(
         3, n_sp, n_rep, tok_frames, window, band_cols, out_width + 2
     )
@@ -190,8 +203,8 @@
     )
     velocity = lax.rsqrt(token_var + 1e-06)[..., None] * centred_proj + shift_column
     patches = (
-        velocity.reshape(3, frames, window, band_cols, LC, 2, 2)
-        .transpose(1, 2, 5, 0, 3, 6, 4)
+        velocity.reshape(3, frames, window, band_cols, 2, 2, LC)
+        .transpose(1, 2, 4, 0, 3, 5, 6)
         .reshape(frames, 2 * window, 3 * 2 * band_cols, LC)
     )
 

time: 36.7 us -> 37.2 us (1.014)
  waiting for transfers between devices: 7.77 us -> 9.09 us
  other arithmetic: 3.74 us -> 2.96 us
    all_to_all x1, waiting for transfers between devices: 3.32 us -> 4.64 us  [per_device(): lax.all_to_all(send, ALL, 0, 0, tiled=False).reshape(n_sec, n_sp, n_rep, -1)]
    reshape x1, local copies, waits for them, and re-layouts: 1.51 us -> 0.39 us  [per_device(): scaled_weight.reshape(out_width, n_rep, local_width)]
    mul x1, other arithmetic: 0.94 us -> 0.06 us  [per_device(): scaled_weight = proj_weight * (1.0 + mod_scale)[None, :]]
    sub x0 -> x1, local copies, waits for them, and re-layouts: none -> 0.4 us  [per_device(): offsets = means - mean[:, :, None]]
    reshape x0 -> x3, local copies, waits for them, and re-layouts: none -> 0.37 us  [per_device(): v.reshape(v.shape[:-1] + (LC, 4)).swapaxes(-1, -2).reshape(v.shape)]
  transfers between devices with their start and end apart: 2 -> 2, of which waited for: 2 -> 2; matrix products, arithmetic and copies ran while one was open for 12% -> 8% of each run, Pallas kernels for 0% -> 0%
where the time goes in v14:
time: 37.2 us; the launch traced here: 36.8 us
  starting transfers between devices  10.6 us (28%)
  waiting for transfers between devices  9.09 us (24%)
  local copies, waits for them, and re-layouts  7.25 us (19%)
  matrix products  3.96 us (11%)
  other arithmetic  2.96 us (8%)
  Pallas kernels  2.46 us (7%)
  between operations  0.48 us (1%)
    all_to_all x1, starting transfers between devices, per_device(): lax.all_to_all(send, ALL, 0, 0, tiled=False).reshape(n_sec, n_sp, n_rep, -1)  7.31 us
    all_to_all x1, waiting for transfers between devices, per_device(): lax.all_to_all(send, ALL, 0, 0, tiled=False).reshape(n_sec, n_sp, n_rep, -1)  4.64 us
    all_to_all x1, waiting for transfers between devices, per_device(): stats = lax.all_to_all(stats, BLOCKS, 0, 0, tiled=False)  4.45 us
    all_to_all x1, starting transfers between devices, per_device(): stats = lax.all_to_all(stats, BLOCKS, 0, 0, tiled=False)  3.31 us
    conv_general_dilated x2, matrix products, valid_conv(): lax.conv_general_dilated(front[None], kernel, (1, 1, 1), 'VALID', dimensi...  2.97 us
    pallas_call x1, Pallas kernels, shard_moments(): pl.pallas_call(shard_kernel, grid_spec=pltpu.PrefetchScalarGridSpec(num_s...  2.46 us
    unnamed x23, local copies, waits for them, and re-layouts  0.89 us
    conv_general_dilated x6, local copies, waits for them, and re-layouts, valid_conv(): lax.conv_general_dilated(front[None], kernel, (1, 1, 1), 'VALID', dimensi...  0.77 us
  transfers between devices with their start and end apart: 2, of which 2 were waited for; matrix products, arithmetic and copies ran while one was open for 8% of the time, Pallas kernels for 0%

profile of v14, /device:TPU:0, one launch (start us, length us, event | category | flops | bytes accessed | tf_op | source)
XLA Modules:
  0.0 36.8 jit_solution(9550165303158375424)
XLA Ops:
  0.0 2.5 %shard_map.118 = f32[32,1,984]{2,1,0:T(1,128)} custom-call(s32[1]{0:T(128)} %bitcast.rep_ref, f32[1,6,2,768]{3,2,1,0:T(2,128)} %bitcast.98, f32[64,3072]{1,0:T(8,128)} %weight_ref.1, f32[1,3072]{1,0:T(1,128)} %bitcast.97, f32[24,2,16]{2,1,0:T(2,128)} %bitcast.100), custom_call_target="tpu_custom_call" | custom-call | tf_op jit(solution)/shard_map/pallas_call | solution.py:86
  2.5 7.3 %all-to-all-start = ((f32[32,1,984]{2,1,0:T(1,128)}), f32[32,1,984]{2,1,0:T(1,128)S(1)}, u32[]{:S(2)}, u32[]{:S(2)}) async-start(f32[32,1,984]{2,1,0:T(1,128)} %shard_map.118), calls=%async_computation | async-start | bytes 262144 | tf_op jit(solution)/shard_map/all_to_all | solution.py:171
  9.8 0.7 %broadcast_add_fusion = f32[3072]{0:T(1024)S(1)} fusion(f32[3072]{0:T(1024)} %param.13), kind=kLoop, calls=%fused_computation.54 | loop fusion | flops 3072 | bytes 24576 | tf_op jit(solution)/shard_map/add | solution.py:173
  10.6 0.7 %fusion.14 = f32[64]{0:T(128)S(1)} fusion(f32[64]{0:T(128)S(1)} %copy-done.5, f32[64,3072]{1,0:T(8,128)S(1)} %copy-done.1, f32[3072,1]{0,1:T(1,128)S(1)} %bitcast.101), kind=kOutput, calls=%fused_computation.15 | convolution fusion | flops 2359360 | bytes 799232 | tf_op jit(solution)/shard_map/dot_general | solution.py:176
  11.6 0.4 %reshape.247 = f32[64,4,768]{2,1,0:T(4,128)S(1)} reshape(f32[64,3072]{1,0:T(8,128)S(1)} %broadcast_multiply_fusion) | data formatting | bytes 1572864 | tf_op jit(solution)/shard_map/reshape | solution.py:174
  12.0 0.2 reduce_sum.108
  12.2 0.2 copy.63
  12.9 4.6 %all-to-all-done = f32[32,1,984]{2,1,0:T(1,128)S(1)} async-done(((f32[32,1,984]{2,1,0:T(1,128)}), f32[32,1,984]{2,1,0:T(1,128)S(1)}, u32[]{:S(2)}, u32[]{:S(2)}) %all-to-all-start) | async-done | bytes 125984 | tf_op jit(solution)/shard_map/all_to_all | solution.py:171
  17.5 0.3 reduce.10
  17.9 0.2 reshape.246
  18.1 0.3 slice_reduce_fusion.3
  18.6 0.1 slice_subtract_fusion
  18.7 0.4 %copy.62 = f32[3,2,4,1,2,6,1]{5,2,4,1,0,6,3:T(4,128)S(1)} copy(f32[3,2,4,1,2,6,1]{6,5,4,2,1,0,3:T(8,128)S(1)} %slice_subtract_fusion) | data formatting | bytes 2304 | tf_op jit(solution)/shard_map/sub | solution.py:192
  19.1 0.3 fusion.13
  19.5 0.2 mul.112
  19.8 0.2 reshape.244
  20.3 0.3 copy-done.9
  20.6 1.0 %convolution_select_fusion = f32[2,4,8,2,512]{4,2,3,1,0:T(8,128)S(1)} fusion(f32[3,3,3,16,512]{4,3,2,1,0:T(8,128)S(1)} %copy-done.9, f32[4,6,1,7,2,16]{5,3,4,1,0,2:T(8,128)S(1)} %slice.65, f32[4,6,1,8,2,16]{5,3,4,1,0,2:T(8,128)S(1)} %copy.53, pred[8,2]{0,1:T(4,128)(4,1)S(1)} %copy-done.10), kind=kOutput, calls=%fused_computation.8 | convolution fusion | flops 169971712 | bytes 1192976 | tf_op jit(solution)/shard_map/conv_general_dilated | solution.py:21
  21.6 0.2 copy.54
  22.1 0.3 broadcast_in_dim.62
  22.4 0.2 reshape.251
  22.6 0.2 slice_bitcast_fusion
  22.8 0.5 %copy.65 = bf16[4,6,1,26,512]{4,0,3,1,2:T(4,128)(2,1)S(1)} copy(bf16[4,6,1,26,512]{4,1,3,0,2:T(8,128)(2,1)S(1)} %slice_bitcast_fusion) | data formatting | bytes 1277952
  23.3 0.3 pad.16.clone
  23.6 0.4 %copy.57 = bf16[4,6,1,8,4,512]{5,3,4,1,0,2:T(8,128)(2,1)S(1)} copy(bf16[4,6,1,8,4,512]{5,0,4,3,1,2:T(4,128)(2,1)S(1)} %bitcast.84) | data formatting | bytes 1572864 | tf_op jit(solution)/shard_map/conv_general_dilated | solution.py:21
  24.2 2.0 %select_reduce_fusion.1 = (f32[64]{0:T(128)S(1)}, f32[2,4,8,4,64]{4,2,3,1,0:T(8,128)S(1)}) fusion(f32[64]{0:T(128)S(1)} %copy-done.4, pred[8,4]{0,1:T(4,128)(4,1)S(1)} %copy-done.8, bf16[3,3,3,64,512]{4,3,2,1,0:T(8,128)(2,1)S(1)} %copy-done, bf16[4,6,1,7,2,512]{5,3,4,1,0,2:T(8,128)(2,1)S(1)} %slice.69, bf16[4,6,1,8,4,512]{5,3,4,1,0,2:T(8,128)(2,1)S(1)} %copy.57), kind=kOutput, calls=%fused_computation.41 | convolution fusion | flops 456589248 | bytes 2966048 | tf_op jit(solution)/shard_map/conv_general_dilated | solution.py:21
  26.6 0.1 select_reduce_fusion
  27.0 0.6 %broadcast_in_dim.65 = f32[8,1,16]{2,1,0:T(1,128)} broadcast(f32[16]{0:T(128)S(1)} %pad_maximum_fusion.2), dimensions={2} | broadcast | bytes 576 | tf_op jit(solution)/shard_map/broadcast_in_dim | solution.py:250
  27.6 3.3 %all-to-all-start.1 = ((f32[8,1,16]{2,1,0:T(1,128)}), f32[8,1,16]{2,1,0:T(1,128)S(1)}, u32[]{:S(2)}, u32[]{:S(2)}) async-start(f32[8,1,16]{2,1,0:T(1,128)} %broadcast_in_dim.65), calls=%async_computation.1 | async-start | bytes 8192 | tf_op jit(solution)/shard_map/all_to_all | solution.py:253
  31.0 4.4 %all-to-all-done.1 = f32[8,1,16]{2,1,0:T(1,128)S(1)} async-done(((f32[8,1,16]{2,1,0:T(1,128)}), f32[8,1,16]{2,1,0:T(1,128)S(1)}, u32[]{:S(2)}, u32[]{:S(2)}) %all-to-all-start.1) | async-done | bytes 544 | tf_op jit(solution)/shard_map/all_to_all | solution.py:253
  35.9 0.2 copy.59
  36.1 0.7 %copy.60 = f32[4,24,128]{2,1,0:T(8,128)} copy(f32[4,24,128]{1,2,0:T(8,128)S(1)} %bitcast.85) | data formatting | bytes 98304 | tf_op jit(solution)/shard_map/reshape | solution.py:266
  (75 shorter events, 3.1 us)
Async XLA Ops:
  0.0 24.2 %copy-start = (bf16[3,3,3,64,512]{4,3,2,1,0:T(8,128)(2,1)S(1)}, bf16[3,3,3,64,512]{4,3,2,1,0:T(8,128)(2,1)}, u32[]{:S(2)}) copy-start(bf16[3,3,3,64,512]{4,3,2,1,0:T(8,128)(2,1)} %param.20) | copy-start | bytes 5308420
  0.0 10.5 %copy-start.1 = (f32[64,3072]{1,0:T(8,128)S(1)}, f32[64,3072]{1,0:T(8,128)}, u32[]{:S(2)}) copy-start(f32[64,3072]{1,0:T(8,128)} %weight_ref.1) | copy-start | bytes 2359300
  0.0 10.6 %copy-start.2 = (f32[3072]{0:T(1024)S(1)}, f32[3072]{0:T(1024)}, u32[]{:S(2)}) copy-start(f32[3072]{0:T(1024)} %param.14) | copy-start | bytes 36868
  0.0 10.6 %copy-start.5 = (f32[64]{0:T(128)S(1)}, f32[64]{0:T(128)}, u32[]{:S(2)}) copy-start(f32[64]{0:T(128)} %param.16) | copy-start | bytes 772
  2.5 15.1 %all-to-all-start = ((f32[32,1,984]{2,1,0:T(1,128)}), f32[32,1,984]{2,1,0:T(1,128)S(1)}, u32[]{:S(2)}, u32[]{:S(2)}) async-start(f32[32,1,984]{2,1,0:T(1,128)} %shard_map.118), calls=%async_computation | async-start | bytes 262144 | tf_op jit(solution)/shard_map/all_to_all | solution.py:171
  19.4 1.2 %copy-start.9 = (f32[3,3,3,16,512]{4,3,2,1,0:T(8,128)S(1)}, f32[3,3,3,16,512]{4,3,2,1,0:T(8,128)}, u32[]{:S(2)}) copy-start(f32[3,3,3,16,512]{4,3,2,1,0:T(8,128)} %param.18) | copy-start | bytes 2654212
  19.5 1.2 %copy-start.10 = (pred[8,2]{0,1:T(4,128)(4,1)S(1)}, pred[8,2]{0,1:T(4,128)(4,1)}, u32[]{:S(2)}) copy-start(pred[8,2]{0,1:T(4,128)(4,1)} %constant.78) | copy-start | bytes 52
  20.6 1.2 %copy-start.3 = (f32[512]{0:T(512)S(1)}, f32[512]{0:T(512)}, u32[]{:S(2)}) copy-start(f32[512]{0:T(512)} %param.19) | copy-start | bytes 6148
  23.3 0.9 %copy-start.4 = (f32[64]{0:T(128)S(1)}, f32[64]{0:T(128)}, u32[]{:S(2)}) copy-start(f32[64]{0:T(128)} %param.21) | copy-start | bytes 772
  23.3 0.9 %copy-start.8 = (pred[8,4]{0,1:T(4,128)(4,1)S(1)}, pred[8,4]{0,1:T(4,128)(4,1)}, u32[]{:S(2)}) copy-start(pred[8,4]{0,1:T(4,128)(4,1)} %constant.77) | copy-start | bytes 100
  24.2 11.7 %copy-start.6 = (f32[64]{0:T(128)S(1)}, f32[64]{0:T(128)}, u32[]{:S(2)}) copy-start(f32[64]{0:T(128)} %param.23) | copy-start | bytes 772
  24.2 11.6 %copy-start.7 = (f32[64]{0:T(128)S(1)}, f32[64]{0:T(128)}, u32[]{:S(2)}) copy-start(f32[64]{0:T(128)} %param.22) | copy-start | bytes 772
  27.6 7.8 %all-to-all-start.1 = ((f32[8,1,16]{2,1,0:T(1,128)}), f32[8,1,16]{2,1,0:T(1,128)S(1)}, u32[]{:S(2)}, u32[]{:S(2)}) async-start(f32[8,1,16]{2,1,0:T(1,128)} %broadcast_in_dim.65), calls=%async_computation.1 | async-start | bytes 8192 | tf_op jit(solution)/shard_map/all_to_all | solution.py:253

commit v15 on v10

--- a/solution.py
+++ b/solution.py
@@ -171,48 +171,60 @@
         )
         + proj_bias
     )
+    def halo_band(stack, width, axis):
+        return jnp.concatenate(
+            [
+                lax.slice_in_dim(stack[0], stack.shape[axis] - width, None, axis=axis - 1),
+                stack[1],
+                lax.slice_in_dim(stack[2], 0, width, axis=axis - 1),
+            ],
+            axis=axis - 1,
+        )
+
     parts = neighbours(received[..., :part_size], sec, 0).reshape(
         3, n_sp, n_rep, tok_frames, window, band_cols, out_width + 2
     )
+    parts = halo_band(parts, 1, 5)
+    band = band_cols + 2
     means = parts[..., out_width]
-    mean = jnp.mean(means, axis=2)
-    offsets = means - mean[:, :, None]
-    m2 = jnp.sum(parts[..., out_width + 1], axis=2) + local_width * jnp.sum(
-        offsets * offsets, axis=2
+    mean = jnp.mean(means, axis=1)
+    offsets = means - mean[:, None]
+    m2 = jnp.sum(parts[..., out_width + 1], axis=1) + local_width * jnp.sum(
+        offsets * offsets, axis=1
     )
     token_var = m2 / full_width
-    centred_proj = jnp.sum(parts[..., :out_width], axis=2) + lax.dot_general(
+    centred_proj = jnp.sum(parts[..., :out_width], axis=1) + lax.dot_general(
         offsets,
         shard_columns,
-        (((2,), (0,)), ((), ())),
+        (((1,), (0,)), ((), ())),
         precision=lax.Precision.HIGHEST,
         preferred_element_type=jnp.float32,
     )
     velocity = lax.rsqrt(token_var + 1e-06)[..., None] * centred_proj + shift_column
     patches = (
-        velocity.reshape(3, frames, window, band_cols, LC, 2, 2)
-        .transpose(1, 2, 5, 0, 3, 6, 4)
-        .reshape(frames, 2 * window, 3 * 2 * band_cols, LC)
+        velocity.reshape(frames, window, band, LC, 2, 2)
+        .transpose(0, 1, 4, 2, 5, 3)
+        .reshape(frames, 2 * window, 2 * band, LC)
     )
 
     shares = neighbours(received[..., part_size:], sec, 0)
     if share == lines:
         shares = shares[:, :, 0]
     latent = shares.reshape(3, n_sp, frames, lat_cols, lat_rows, LC).transpose(0, 1, 2, 4, 3, 5)
+    latent = halo_band(latent, 2, 4)
     if window == patch_rows:
-        latent = latent.transpose(2, 1, 3, 0, 4, 5).reshape(
-            frames, n_sp * lat_rows, 3 * lat_cols, LC
+        latent = latent.transpose(1, 0, 2, 3, 4).reshape(
+            frames, n_sp * lat_rows, lat_cols + 4, LC
         )
         clean = latent - 0.5 * patches
         clean = jnp.pad(clean, ((0, 0), (2, 2), (0, 0), (0, 0)))
         clean = lax.dynamic_slice_in_dim(clean, spi * lat_rows, lat_rows + 4, 1)
     else:
-        latent = neighbours(latent.transpose(1, 2, 3, 0, 4, 5), spi, 0)
-        latent = latent.transpose(1, 0, 2, 3, 4, 5).reshape(
-            frames, 3 * lat_rows, 3 * lat_cols, LC
+        latent = neighbours(latent, spi, 0)
+        latent = latent.transpose(1, 0, 2, 3, 4).reshape(
+            frames, 3 * lat_rows, lat_cols + 4, LC
         )[:, lat_rows - 2 : 2 * lat_rows + 2]
         clean = latent - 0.5 * patches
-    clean = clean[:, :, lat_cols - 2 : 2 * lat_cols + 2]
 
     row_global = spi * lat_rows - 2 + jnp.arange(lat_rows + 4)
     col_global = sec * lat_cols - 2 + jnp.arange(lat_cols + 4)

time: 36.7 us -> 36.1 us (0.984)
  local copies, waits for them, and re-layouts: 7.52 us -> 7.02 us
    mul x2, local copies, waits for them, and re-layouts: 0.61 us -> 0.2 us  [per_device(): clean = latent - 0.5 * patches]
where the time goes in v15:
time: 36.1 us; the launch traced here: 35.8 us
  starting transfers between devices  10.6 us (29%)
  waiting for transfers between devices  7.74 us (21%)
  local copies, waits for them, and re-layouts  7.02 us (19%)
  matrix products  3.92 us (11%)
  other arithmetic  3.61 us (10%)
  Pallas kernels  2.35 us (7%)
  between operations  0.54 us (1%)
    all_to_all x1, starting transfers between devices, per_device(): lax.all_to_all(send, ALL, 0, 0, tiled=False).reshape(n_sec, n_sp, n_rep, -1)  7.3 us
    all_to_all x1, waiting for transfers between devices, per_device(): stats = lax.all_to_all(stats, BLOCKS, 0, 0, tiled=False)  4.45 us
    all_to_all x1, starting transfers between devices, per_device(): stats = lax.all_to_all(stats, BLOCKS, 0, 0, tiled=False)  3.31 us
    all_to_all x1, waiting for transfers between devices, per_device(): lax.all_to_all(send, ALL, 0, 0, tiled=False).reshape(n_sec, n_sp, n_rep, -1)  3.29 us
    conv_general_dilated x2, matrix products, valid_conv(): lax.conv_general_dilated(front[None], kernel, (1, 1, 1), 'VALID', dimensi...  2.96 us
    pallas_call x1, Pallas kernels, shard_moments(): pl.pallas_call(shard_kernel, grid_spec=pltpu.PrefetchScalarGridSpec(num_s...  2.35 us
    reshape x1, local copies, waits for them, and re-layouts, per_device(): scaled_weight.reshape(out_width, n_rep, local_width)  1.51 us
    mul x1, other arithmetic, per_device(): scaled_weight = proj_weight * (1.0 + mod_scale)[None, :]  0.94 us
  transfers between devices with their start and end apart: 2, of which 2 were waited for; matrix products, arithmetic and copies ran while one was open for 12% of the time, Pallas kernels for 0%

profile of v15, /device:TPU:0, one launch (start us, length us, event | category | flops | bytes accessed | tf_op | source)
XLA Modules:
  0.0 35.8 jit_solution(6861322477844674815)
XLA Ops:
  0.0 2.3 %shard_map.118 = f32[32,1,984]{2,1,0:T(1,128)} custom-call(s32[1]{0:T(128)} %bitcast.rep_ref, f32[1,6,2,768]{3,2,1,0:T(2,128)} %bitcast.96, f32[64,3072]{1,0:T(8,128)} %weight_ref.1, f32[1,3072]{1,0:T(1,128)} %bitcast.95, f32[24,2,16]{2,1,0:T(2,128)} %bitcast.97), custom_call_target="tpu_custom_call" | custom-call | tf_op jit(solution)/shard_map/pallas_call | solution.py:76
  2.4 7.3 %all-to-all-start = ((f32[32,1,984]{2,1,0:T(1,128)}), f32[32,1,984]{2,1,0:T(1,128)S(1)}, u32[]{:S(2)}, u32[]{:S(2)}) async-start(f32[32,1,984]{2,1,0:T(1,128)} %shard_map.118), calls=%async_computation | async-start | bytes 262144 | tf_op jit(solution)/shard_map/all_to_all | solution.py:161
  9.9 0.7 %broadcast_add_fusion = f32[3072]{0:T(1024)S(1)} fusion(f32[3072]{0:T(1024)} %param.13), kind=kLoop, calls=%fused_computation.61 | loop fusion | flops 3072 | bytes 24576 | tf_op jit(solution)/shard_map/add | solution.py:163
  10.6 0.9 %broadcast_multiply_fusion = f32[64,3072]{1,0:T(8,128)} fusion(f32[64,3072]{1,0:T(8,128)S(1)} %copy-done.1, f32[3072]{0:T(1024)S(1)} %broadcast_add_fusion), kind=kLoop, calls=%fused_computation.23 | loop fusion | flops 196608 | bytes 1585152 | tf_op jit(solution)/shard_map/mul | solution.py:163
  11.6 1.5 %reshape.240 = f32[64,4,768]{2,1,0:T(4,128)S(1)} reshape(f32[64,3072]{1,0:T(8,128)} %broadcast_multiply_fusion) | data formatting | bytes 1572864 | tf_op jit(solution)/shard_map/reshape | solution.py:164
  13.2 0.2 reduce_sum.108
  13.4 0.7 %fusion.14 = f32[64]{0:T(128)S(1)} fusion(f32[64]{0:T(128)S(1)} %copy-done.5, f32[64,3072]{1,0:T(8,128)S(1)} %copy-done.1, f32[3072,1]{0,1:T(1,128)S(1)} %bitcast.98), kind=kOutput, calls=%fused_computation.15 | convolution fusion | flops 2359360 | bytes 799232 | tf_op jit(solution)/shard_map/dot_general | solution.py:166
  14.1 3.3 %all-to-all-done = f32[32,1,984]{2,1,0:T(1,128)S(1)} async-done(((f32[32,1,984]{2,1,0:T(1,128)}), f32[32,1,984]{2,1,0:T(1,128)S(1)}, u32[]{:S(2)}, u32[]{:S(2)}) %all-to-all-start) | async-done | bytes 125984 | tf_op jit(solution)/shard_map/all_to_all | solution.py:161
  17.4 0.3 reduce.10
  18.3 0.2 slice_reduce_fusion.1
  18.6 0.2 reshape.238
  18.9 0.2 fusion.13
  19.2 0.1 copy.43
  19.6 1.0 %convolution_select_fusion = f32[2,4,8,2,512]{4,2,3,1,0:T(8,128)S(1)} fusion(f32[3,3,3,16,512]{4,3,2,1,0:T(8,128)S(1)} %copy-done.9, f32[4,6,1,7,2,16]{5,3,4,1,0,2:T(8,128)S(1)} %slice.111, f32[4,6,1,8,2,16]{5,3,4,1,0,2:T(8,128)S(1)} %copy.45, pred[8,2]{0,1:T(4,128)(4,1)S(1)} %copy-done.10), kind=kOutput, calls=%fused_computation.8 | convolution fusion | flops 169971712 | bytes 1192976 | tf_op jit(solution)/shard_map/conv_general_dilated | solution.py:21
  20.6 0.2 copy.46
  20.7 0.1 fusion.22
  20.9 0.1 pad_maximum_fusion
  21.0 0.3 broadcast_in_dim.39
  21.3 0.2 reshape.241
  21.6 0.2 slice_bitcast_fusion
  21.8 0.5 %copy.56 = bf16[4,6,1,26,512]{4,0,3,1,2:T(4,128)(2,1)S(1)} copy(bf16[4,6,1,26,512]{4,1,3,0,2:T(8,128)(2,1)S(1)} %slice_bitcast_fusion) | data formatting | bytes 1277952
  22.3 0.3 pad.16.clone
  22.6 0.4 %copy.49 = bf16[4,6,1,8,4,512]{5,3,4,1,0,2:T(8,128)(2,1)S(1)} copy(bf16[4,6,1,8,4,512]{5,0,4,3,1,2:T(4,128)(2,1)S(1)} %bitcast.84) | data formatting | bytes 1572864 | tf_op jit(solution)/shard_map/conv_general_dilated | solution.py:21
  23.2 2.0 %select_reduce_fusion.1 = (f32[64]{0:T(128)S(1)}, f32[2,4,8,4,64]{4,2,3,1,0:T(8,128)S(1)}) fusion(f32[64]{0:T(128)S(1)} %copy-done.4, pred[8,4]{0,1:T(4,128)(4,1)S(1)} %copy-done.8, bf16[3,3,3,64,512]{4,3,2,1,0:T(8,128)(2,1)S(1)} %copy-done, bf16[4,6,1,7,2,512]{5,3,4,1,0,2:T(8,128)(2,1)S(1)} %slice.115, bf16[4,6,1,8,4,512]{5,3,4,1,0,2:T(8,128)(2,1)S(1)} %copy.49), kind=kOutput, calls=%fused_computation.36 | convolution fusion | flops 456589248 | bytes 2966048 | tf_op jit(solution)/shard_map/conv_general_dilated | solution.py:21
  25.3 0.1 reduce_sum.111
  25.6 0.1 select_reduce_fusion
  25.8 0.1 reduce_sum.114
  26.0 0.6 %broadcast_in_dim.66 = f32[8,1,16]{2,1,0:T(1,128)} broadcast(f32[16]{0:T(128)S(1)} %pad_maximum_fusion.3), dimensions={2} | broadcast | bytes 576 | tf_op jit(solution)/shard_map/broadcast_in_dim | solution.py:249
  26.6 3.3 %all-to-all-start.1 = ((f32[8,1,16]{2,1,0:T(1,128)}), f32[8,1,16]{2,1,0:T(1,128)S(1)}, u32[]{:S(2)}, u32[]{:S(2)}) async-start(f32[8,1,16]{2,1,0:T(1,128)} %broadcast_in_dim.66), calls=%async_computation.1 | async-start | bytes 8192 | tf_op jit(solution)/shard_map/all_to_all | solution.py:252
  29.9 4.4 %all-to-all-done.1 = f32[8,1,16]{2,1,0:T(1,128)S(1)} async-done(((f32[8,1,16]{2,1,0:T(1,128)}), f32[8,1,16]{2,1,0:T(1,128)S(1)}, u32[]{:S(2)}, u32[]{:S(2)}) %all-to-all-start.1) | async-done | bytes 544 | tf_op jit(solution)/shard_map/all_to_all | solution.py:252
  34.9 0.2 copy.51
  35.1 0.7 %copy.52 = f32[4,24,128]{2,1,0:T(8,128)} copy(f32[4,24,128]{1,2,0:T(8,128)S(1)} %bitcast.85) | data formatting | bytes 98304 | tf_op jit(solution)/shard_map/reshape | solution.py:265
  (75 shorter events, 2.4 us)
Async XLA Ops:
  0.0 23.1 %copy-start = (bf16[3,3,3,64,512]{4,3,2,1,0:T(8,128)(2,1)S(1)}, bf16[3,3,3,64,512]{4,3,2,1,0:T(8,128)(2,1)}, u32[]{:S(2)}) copy-start(bf16[3,3,3,64,512]{4,3,2,1,0:T(8,128)(2,1)} %param.20) | copy-start | bytes 5308420
  0.0 10.6 %copy-start.1 = (f32[64,3072]{1,0:T(8,128)S(1)}, f32[64,3072]{1,0:T(8,128)}, u32[]{:S(2)}) copy-start(f32[64,3072]{1,0:T(8,128)} %weight_ref.1) | copy-start | bytes 2359300
  2.4 15.0 %all-to-all-start = ((f32[32,1,984]{2,1,0:T(1,128)}), f32[32,1,984]{2,1,0:T(1,128)S(1)}, u32[]{:S(2)}, u32[]{:S(2)}) async-start(f32[32,1,984]{2,1,0:T(1,128)} %shard_map.118), calls=%async_computation | async-start | bytes 262144 | tf_op jit(solution)/shard_map/all_to_all | solution.py:161
  10.6 2.7 %copy-start.2 = (f32[3072]{0:T(1024)S(1)}, f32[3072]{0:T(1024)}, u32[]{:S(2)}) copy-start(f32[3072]{0:T(1024)} %param.14) | copy-start | bytes 36868
  10.6 2.7 %copy-start.5 = (f32[64]{0:T(128)S(1)}, f32[64]{0:T(128)}, u32[]{:S(2)}) copy-start(f32[64]{0:T(128)} %param.16) | copy-start | bytes 772
  18.0 1.6 %copy-start.9 = (f32[3,3,3,16,512]{4,3,2,1,0:T(8,128)S(1)}, f32[3,3,3,16,512]{4,3,2,1,0:T(8,128)}, u32[]{:S(2)}) copy-start(f32[3,3,3,16,512]{4,3,2,1,0:T(8,128)} %param.18) | copy-start | bytes 2654212
  18.0 1.6 %copy-start.10 = (pred[8,2]{0,1:T(4,128)(4,1)S(1)}, pred[8,2]{0,1:T(4,128)(4,1)}, u32[]{:S(2)}) copy-start(pred[8,2]{0,1:T(4,128)(4,1)} %constant.78) | copy-start | bytes 52
  19.6 1.2 %copy-start.3 = (f32[512]{0:T(512)S(1)}, f32[512]{0:T(512)}, u32[]{:S(2)}) copy-start(f32[512]{0:T(512)} %param.19) | copy-start | bytes 6148
  22.3 0.9 %copy-start.4 = (f32[64]{0:T(128)S(1)}, f32[64]{0:T(128)}, u32[]{:S(2)}) copy-start(f32[64]{0:T(128)} %param.21) | copy-start | bytes 772
  22.3 0.9 %copy-start.8 = (pred[8,4]{0,1:T(4,128)(4,1)S(1)}, pred[8,4]{0,1:T(4,128)(4,1)}, u32[]{:S(2)}) copy-start(pred[8,4]{0,1:T(4,128)(4,1)} %constant.77) | copy-start | bytes 100
  23.2 11.7 %copy-start.6 = (f32[64]{0:T(128)S(1)}, f32[64]{0:T(128)}, u32[]{:S(2)}) copy-start(f32[64]{0:T(128)} %param.23) | copy-start | bytes 772
  23.2 11.6 %copy-start.7 = (f32[64]{0:T(128)S(1)}, f32[64]{0:T(128)}, u32[]{:S(2)}) copy-start(f32[64]{0:T(128)} %param.22) | copy-start | bytes 772
  26.6 7.8 %all-to-all-start.1 = ((f32[8,1,16]{2,1,0:T(1,128)}), f32[8,1,16]{2,1,0:T(1,128)S(1)}, u32[]{:S(2)}, u32[]{:S(2)}) async-start(f32[8,1,16]{2,1,0:T(1,128)} %broadcast_in_dim.66), calls=%async_computation.1 | async-start | bytes 8192 | tf_op jit(solution)/shard_map/all_to_all | solution.py:252

commit v16 on v15

--- a/solution.py
+++ b/solution.py
@@ -99,6 +99,12 @@
     )
 
 
+def clamped_neighbours(stack, index):
+    return jnp.stack(
+        [lax.dynamic_index_in_dim(stack, index + d, 0, keepdims=False) for d in (-1, 0, 1)]
+    )
+
+
 def neighbours(stack, index, axis):
     pad = [(0, 0)] * stack.ndim
     pad[axis] = (1, 1)
@@ -181,7 +187,7 @@
             axis=axis - 1,
         )
 
-    parts = neighbours(received[..., :part_size], sec, 0).reshape(
+    parts = clamped_neighbours(received[..., :part_size], sec).reshape(
         3, n_sp, n_rep, tok_frames, window, band_cols, out_width + 2
     )
     parts = halo_band(parts, 1, 5)
@@ -207,7 +213,7 @@
         .reshape(frames, 2 * window, 2 * band, LC)
     )
 
-    shares = neighbours(received[..., part_size:], sec, 0)
+    shares = clamped_neighbours(received[..., part_size:], sec)
     if share == lines:
         shares = shares[:, :, 0]
     latent = shares.reshape(3, n_sp, frames, lat_cols, lat_rows, LC).transpose(0, 1, 2, 4, 3, 5)

time: 36.1 us -> 36.1 us (level)
  no operation moved by 1% of the time
where the time goes in v16:
time: 36.1 us; the launch traced here: 35.8 us
  starting transfers between devices  10.6 us (29%)
  waiting for transfers between devices  7.73 us (21%)
  local copies, waits for them, and re-layouts  7 us (19%)
  matrix products  3.92 us (11%)
  other arithmetic  3.62 us (10%)
  Pallas kernels  2.35 us (7%)
  between operations  0.55 us (2%)
    all_to_all x1, starting transfers between devices, per_device(): lax.all_to_all(send, ALL, 0, 0, tiled=False).reshape(n_sec, n_sp, n_rep, -1)  7.3 us
    all_to_all x1, waiting for transfers between devices, per_device(): stats = lax.all_to_all(stats, BLOCKS, 0, 0, tiled=False)  4.45 us
    all_to_all x1, starting transfers between devices, per_device(): stats = lax.all_to_all(stats, BLOCKS, 0, 0, tiled=False)  3.31 us
    all_to_all x1, waiting for transfers between devices, per_device(): lax.all_to_all(send, ALL, 0, 0, tiled=False).reshape(n_sec, n_sp, n_rep, -1)  3.28 us
    conv_general_dilated x2, matrix products, valid_conv(): lax.conv_general_dilated(front[None], kernel, (1, 1, 1), 'VALID', dimensi...  2.96 us
    pallas_call x1, Pallas kernels, shard_moments(): pl.pallas_call(shard_kernel, grid_spec=pltpu.PrefetchScalarGridSpec(num_s...  2.35 us
    reshape x1, local copies, waits for them, and re-layouts, per_device(): scaled_weight.reshape(out_width, n_rep, local_width)  1.51 us
    mul x1, other arithmetic, per_device(): scaled_weight = proj_weight * (1.0 + mod_scale)[None, :]  0.94 us
  transfers between devices with their start and end apart: 2, of which 2 were waited for; matrix products, arithmetic and copies ran while one was open for 12% of the time, Pallas kernels for 0%

profile of v16, /device:TPU:0, one launch (start us, length us, event | category | flops | bytes accessed | tf_op | source)
XLA Modules:
  0.0 35.8 jit_solution(7822852560532086691)
XLA Ops:
  0.0 2.3 %shard_map.118 = f32[32,1,984]{2,1,0:T(1,128)} custom-call(s32[1]{0:T(128)} %bitcast.rep_ref, f32[1,6,2,768]{3,2,1,0:T(2,128)} %bitcast.96, f32[64,3072]{1,0:T(8,128)} %weight_ref.1, f32[1,3072]{1,0:T(1,128)} %bitcast.95, f32[24,2,16]{2,1,0:T(2,128)} %bitcast.97), custom_call_target="tpu_custom_call" | custom-call | tf_op jit(solution)/shard_map/pallas_call | solution.py:76
  2.4 7.3 %all-to-all-start = ((f32[32,1,984]{2,1,0:T(1,128)}), f32[32,1,984]{2,1,0:T(1,128)S(1)}, u32[]{:S(2)}, u32[]{:S(2)}) async-start(f32[32,1,984]{2,1,0:T(1,128)} %shard_map.118), calls=%async_computation | async-start | bytes 262144 | tf_op jit(solution)/shard_map/all_to_all | solution.py:167
  9.9 0.7 %broadcast_add_fusion = f32[3072]{0:T(1024)S(1)} fusion(f32[3072]{0:T(1024)} %param.13), kind=kLoop, calls=%fused_computation.58 | loop fusion | flops 3072 | bytes 24576 | tf_op jit(solution)/shard_map/add | solution.py:169
  10.6 0.9 %broadcast_multiply_fusion = f32[64,3072]{1,0:T(8,128)} fusion(f32[64,3072]{1,0:T(8,128)S(1)} %copy-done.1, f32[3072]{0:T(1024)S(1)} %broadcast_add_fusion), kind=kLoop, calls=%fused_computation.23 | loop fusion | flops 196608 | bytes 1585152 | tf_op jit(solution)/shard_map/mul | solution.py:169
  11.6 1.5 %reshape.240 = f32[64,4,768]{2,1,0:T(4,128)S(1)} reshape(f32[64,3072]{1,0:T(8,128)} %broadcast_multiply_fusion) | data formatting | bytes 1572864 | tf_op jit(solution)/shard_map/reshape | solution.py:170
  13.2 0.2 reduce_sum.108
  13.4 0.7 %fusion.14 = f32[64]{0:T(128)S(1)} fusion(f32[64]{0:T(128)S(1)} %copy-done.5, f32[64,3072]{1,0:T(8,128)S(1)} %copy-done.1, f32[3072,1]{0,1:T(1,128)S(1)} %bitcast.98), kind=kOutput, calls=%fused_computation.15 | convolution fusion | flops 2359360 | bytes 799232 | tf_op jit(solution)/shard_map/dot_general | solution.py:172
  14.1 3.3 %all-to-all-done = f32[32,1,984]{2,1,0:T(1,128)S(1)} async-done(((f32[32,1,984]{2,1,0:T(1,128)}), f32[32,1,984]{2,1,0:T(1,128)S(1)}, u32[]{:S(2)}, u32[]{:S(2)}) %all-to-all-start) | async-done | bytes 125984 | tf_op jit(solution)/shard_map/all_to_all | solution.py:167
  17.4 0.3 reduce.10
  18.3 0.2 slice_reduce_fusion.1
  18.6 0.2 reshape.238
  18.9 0.2 fusion.13
  19.2 0.1 copy.43
  19.6 1.0 %convolution_select_fusion = f32[2,4,8,2,512]{4,2,3,1,0:T(8,128)S(1)} fusion(f32[3,3,3,16,512]{4,3,2,1,0:T(8,128)S(1)} %copy-done.9, f32[4,6,1,7,2,16]{5,3,4,1,0,2:T(8,128)S(1)} %slice.102, f32[4,6,1,8,2,16]{5,3,4,1,0,2:T(8,128)S(1)} %copy.45, pred[8,2]{0,1:T(4,128)(4,1)S(1)} %copy-done.10), kind=kOutput, calls=%fused_computation.8 | convolution fusion | flops 169971712 | bytes 1192976 | tf_op jit(solution)/shard_map/conv_general_dilated | solution.py:21
  20.5 0.2 copy.46
  20.7 0.1 fusion.22
  20.9 0.1 pad_maximum_fusion
  21.0 0.3 broadcast_in_dim.39
  21.3 0.2 reshape.241
  21.6 0.2 slice_bitcast_fusion
  21.8 0.5 %copy.56 = bf16[4,6,1,26,512]{4,0,3,1,2:T(4,128)(2,1)S(1)} copy(bf16[4,6,1,26,512]{4,1,3,0,2:T(8,128)(2,1)S(1)} %slice_bitcast_fusion) | data formatting | bytes 1277952
  22.3 0.3 pad.6.clone
  22.6 0.4 %copy.49 = bf16[4,6,1,8,4,512]{5,3,4,1,0,2:T(8,128)(2,1)S(1)} copy(bf16[4,6,1,8,4,512]{5,0,4,3,1,2:T(4,128)(2,1)S(1)} %bitcast.84) | data formatting | bytes 1572864 | tf_op jit(solution)/shard_map/conv_general_dilated | solution.py:21
  23.2 2.0 %select_reduce_fusion.1 = (f32[64]{0:T(128)S(1)}, f32[2,4,8,4,64]{4,2,3,1,0:T(8,128)S(1)}) fusion(f32[64]{0:T(128)S(1)} %copy-done.4, pred[8,4]{0,1:T(4,128)(4,1)S(1)} %copy-done.8, bf16[3,3,3,64,512]{4,3,2,1,0:T(8,128)(2,1)S(1)} %copy-done, bf16[4,6,1,7,2,512]{5,3,4,1,0,2:T(8,128)(2,1)S(1)} %slice.106, bf16[4,6,1,8,4,512]{5,3,4,1,0,2:T(8,128)(2,1)S(1)} %copy.49), kind=kOutput, calls=%fused_computation.33 | convolution fusion | flops 456589248 | bytes 2966048 | tf_op jit(solution)/shard_map/conv_general_dilated | solution.py:21
  25.3 0.1 reduce_sum.111
  25.6 0.1 select_reduce_fusion
  25.8 0.1 reduce_sum.114
  26.0 0.6 %broadcast_in_dim.66 = f32[8,1,16]{2,1,0:T(1,128)} broadcast(f32[16]{0:T(128)S(1)} %pad_maximum_fusion.4), dimensions={2} | broadcast | bytes 576 | tf_op jit(solution)/shard_map/broadcast_in_dim | solution.py:255
  26.6 3.3 %all-to-all-start.1 = ((f32[8,1,16]{2,1,0:T(1,128)}), f32[8,1,16]{2,1,0:T(1,128)S(1)}, u32[]{:S(2)}, u32[]{:S(2)}) async-start(f32[8,1,16]{2,1,0:T(1,128)} %broadcast_in_dim.66), calls=%async_computation.1 | async-start | bytes 8192 | tf_op jit(solution)/shard_map/all_to_all | solution.py:258
  29.9 4.4 %all-to-all-done.1 = f32[8,1,16]{2,1,0:T(1,128)S(1)} async-done(((f32[8,1,16]{2,1,0:T(1,128)}), f32[8,1,16]{2,1,0:T(1,128)S(1)}, u32[]{:S(2)}, u32[]{:S(2)}) %all-to-all-start.1) | async-done | bytes 544 | tf_op jit(solution)/shard_map/all_to_all | solution.py:258
  34.9 0.2 copy.51
  35.0 0.7 %copy.52 = f32[4,24,128]{2,1,0:T(8,128)} copy(f32[4,24,128]{1,2,0:T(8,128)S(1)} %bitcast.85) | data formatting | bytes 98304 | tf_op jit(solution)/shard_map/reshape | solution.py:271
  (76 shorter events, 2.3 us)
Async XLA Ops:
  0.0 23.1 %copy-start = (bf16[3,3,3,64,512]{4,3,2,1,0:T(8,128)(2,1)S(1)}, bf16[3,3,3,64,512]{4,3,2,1,0:T(8,128)(2,1)}, u32[]{:S(2)}) copy-start(bf16[3,3,3,64,512]{4,3,2,1,0:T(8,128)(2,1)} %param.20) | copy-start | bytes 5308420
  0.0 10.6 %copy-start.1 = (f32[64,3072]{1,0:T(8,128)S(1)}, f32[64,3072]{1,0:T(8,128)}, u32[]{:S(2)}) copy-start(f32[64,3072]{1,0:T(8,128)} %weight_ref.1) | copy-start | bytes 2359300
  2.4 15.0 %all-to-all-start = ((f32[32,1,984]{2,1,0:T(1,128)}), f32[32,1,984]{2,1,0:T(1,128)S(1)}, u32[]{:S(2)}, u32[]{:S(2)}) async-start(f32[32,1,984]{2,1,0:T(1,128)} %shard_map.118), calls=%async_computation | async-start | bytes 262144 | tf_op jit(solution)/shard_map/all_to_all | solution.py:167
  10.6 2.7 %copy-start.2 = (f32[3072]{0:T(1024)S(1)}, f32[3072]{0:T(1024)}, u32[]{:S(2)}) copy-start(f32[3072]{0:T(1024)} %param.14) | copy-start | bytes 36868
  10.6 2.7 %copy-start.5 = (f32[64]{0:T(128)S(1)}, f32[64]{0:T(128)}, u32[]{:S(2)}) copy-start(f32[64]{0:T(128)} %param.16) | copy-start | bytes 772
  18.0 1.5 %copy-start.9 = (f32[3,3,3,16,512]{4,3,2,1,0:T(8,128)S(1)}, f32[3,3,3,16,512]{4,3,2,1,0:T(8,128)}, u32[]{:S(2)}) copy-start(f32[3,3,3,16,512]{4,3,2,1,0:T(8,128)} %param.18) | copy-start | bytes 2654212
  18.0 1.5 %copy-start.10 = (pred[8,2]{0,1:T(4,128)(4,1)S(1)}, pred[8,2]{0,1:T(4,128)(4,1)}, u32[]{:S(2)}) copy-start(pred[8,2]{0,1:T(4,128)(4,1)} %constant.96) | copy-start | bytes 52
  19.6 1.2 %copy-start.3 = (f32[512]{0:T(512)S(1)}, f32[512]{0:T(512)}, u32[]{:S(2)}) copy-start(f32[512]{0:T(512)} %param.19) | copy-start | bytes 6148
  22.3 0.9 %copy-start.4 = (f32[64]{0:T(128)S(1)}, f32[64]{0:T(128)}, u32[]{:S(2)}) copy-start(f32[64]{0:T(128)} %param.21) | copy-start | bytes 772
  22.3 0.9 %copy-start.8 = (pred[8,4]{0,1:T(4,128)(4,1)S(1)}, pred[8,4]{0,1:T(4,128)(4,1)}, u32[]{:S(2)}) copy-start(pred[8,4]{0,1:T(4,128)(4,1)} %constant.95) | copy-start | bytes 100
  23.2 11.7 %copy-start.6 = (f32[64]{0:T(128)S(1)}, f32[64]{0:T(128)}, u32[]{:S(2)}) copy-start(f32[64]{0:T(128)} %param.23) | copy-start | bytes 772
  23.2 11.6 %copy-start.7 = (f32[64]{0:T(128)S(1)}, f32[64]{0:T(128)}, u32[]{:S(2)}) copy-start(f32[64]{0:T(128)} %param.22) | copy-start | bytes 772
  26.6 7.8 %all-to-all-start.1 = ((f32[8,1,16]{2,1,0:T(1,128)}), f32[8,1,16]{2,1,0:T(1,128)S(1)}, u32[]{:S(2)}, u32[]{:S(2)}) async-start(f32[8,1,16]{2,1,0:T(1,128)} %broadcast_in_dim.66), calls=%async_computation.1 | async-start | bytes 8192 | tf_op jit(solution)/shard_map/all_to_all | solution.py:258
